TPU v7x, 256 devices: a whole 4x4x8 slice. The times are simulated.
256 devices in a mesh: dp: 16 (over x, y), expert: 16 (over z, core).
Axes of the slice: x: 4, y: 4, z: 8, core: 2. Of those that a mesh axis runs over, the one named last changes fastest.
Arguments:
- hidden: bfloat16 [32768, 8, 768], P(('dp', 'expert')), may hold values from -6 to 6
- upstream: bfloat16 [32768, 4096], P(('dp', 'expert')), may hold values from -0.125 to 0.125
- probs: bfloat16 [32768, 8], P(('dp', 'expert')), may hold values from 0.019897461 to 0.5
- expert_ids: int32 [32768, 8], P(('dp', 'expert')), may hold values from 0 to 15, all different within a row; in each aligned block of 128 rows (0 to 127, 128 to 255, ...) at most 72 rows name the same one
- w_down: bfloat16 [16, 4096, 768], P('expert', 'dp'), may hold values from -0.21875 to 0.21875
Outputs:
- grad_down: float32 [16, 4096, 768], P('expert', 'dp')
- gate_grad: float32 [32768, 8], P(('dp', 'expert'))
Inputs may be any that keep to these rules, and one draw needn't show every extreme that they name: `expert_ids`: each row names 8 different experts; among the rows of one device no expert is named by more than 72 rows, a bound that some block reaches.
All inputs are finite; a program needn't handle non-finite values.
Results may differ from a plain program's by a relative error of at most 0.013.
Values may be sent and summed in bfloat16 or wider, within the bound.
No kernel may reach another device: no remote copies, remote signals or barrier semaphores. Data moves between devices by JAX's collectives and lax.ppermute only.
A program may use at most 128 MiB of HBM per device.

v0:
```python
import jax
import jax.numpy as jnp
from jax import lax
from jax.sharding import PartitionSpec as P


def body(hidden, upstream, probs, expert_ids, w_down):
    tok_rows, top_k = expert_ids.shape
    hid_width = hidden.shape[2]
    model_width = upstream.shape[1]
    groups = lax.axis_size("expert")
    slots_per = max(tok_rows * 9 // 16, tok_rows * top_k // groups)
    total_rows = groups * slots_per
    chosen = (expert_ids[:, :, None] == jnp.arange(groups, dtype=jnp.int32)[None, None, :]).astype(
        jnp.int32
    )
    member = jnp.sum(chosen, axis=1)
    slot_place = jnp.cumsum(member, axis=0) - 1
    which_k = jnp.sum(chosen * jnp.arange(top_k, dtype=jnp.int32)[None, :, None], axis=1)
    target = (
        (member == 1)[:, :, None]
        & (slot_place[:, :, None] == jnp.arange(slots_per, dtype=jnp.int32)[None, None, :])
    ).astype(jnp.int32)
    filled = jnp.sum(target, axis=0) == 1
    source_tok = jnp.sum(target * jnp.arange(tok_rows, dtype=jnp.int32)[:, None, None], axis=0)
    source_k = jnp.sum(target * which_k[:, :, None], axis=0)
    flat_index = (source_tok * top_k + source_k).reshape(-1)
    picked_h = hidden.reshape(tok_rows * top_k, hid_width)[flat_index].reshape(
        groups, slots_per, hid_width
    )
    send_h = jnp.where(filled[:, :, None], picked_h, jnp.zeros_like(picked_h))
    picked_dy = upstream[source_tok.reshape(-1)].reshape(groups, slots_per, model_width)
    send_dy = jnp.where(filled[:, :, None], picked_dy, jnp.zeros_like(picked_dy))
    picked_p = probs.reshape(-1)[flat_index].reshape(groups, slots_per)
    send_p = jnp.where(filled, picked_p, jnp.zeros_like(picked_p))
    recv_h, recv_dy, recv_p = (
        lax.all_to_all(send_h, "expert", split_axis=0, concat_axis=0, tiled=True),
        lax.all_to_all(send_dy, "expert", split_axis=0, concat_axis=0, tiled=True),
        lax.all_to_all(send_p, "expert", split_axis=0, concat_axis=0, tiled=True),
    )
    rows_h = recv_h.reshape(total_rows, hid_width)
    rows_dy = recv_dy.reshape(total_rows, model_width)
    projected = lax.dot_general(
        rows_h,
        lax.all_gather(w_down, "dp", axis=1, tiled=True)[0],
        (((1,), (1,)), ((), ())),
        preferred_element_type=jnp.float32,
    )
    columns = rows_dy
    scores = jnp.sum(projected * columns.astype(jnp.float32), axis=1)
    returned = lax.all_to_all(
        scores.reshape(groups, slots_per), "expert", split_axis=0, concat_axis=0, tiled=True
    )
    scaled = (recv_p.astype(jnp.float32)[:, :, None] * recv_dy.astype(jnp.float32)).astype(
        jnp.bfloat16
    )
    scaled = scaled.reshape(total_rows, model_width)
    columns = scaled
    grad_block = lax.psum_scatter(
        lax.dot_general(
            columns, rows_h, (((0,), (0,)), ((), ())), preferred_element_type=jnp.float32
        ).astype(jnp.bfloat16),
        "dp",
        scatter_dimension=0,
        tiled=True,
    ).astype(jnp.float32)
    place_slot = jnp.take_along_axis(slot_place, expert_ids, axis=1)
    gate_grad = returned[expert_ids, place_slot]
    return (grad_block[None], gate_grad)


def solution(mesh):
    in_specs = (
        P(("dp", "expert"), None, None),
        P(("dp", "expert"), None),
        P(("dp", "expert"), None),
        P(("dp", "expert"), None),
        P("expert", "dp", None),
    )
    out_specs = (P("expert", "dp", None), P(("dp", "expert"), None))
    return jax.shard_map(body, mesh=mesh, in_specs=in_specs, out_specs=out_specs, check_vma=False)
```

profile of v0, /device:TPU:1, one launch (start us, length us, event | category | flops | bytes accessed | tf_op | source)
XLA Modules:
  0.0 404.0 jit_solution(6067749536362024406)
XLA Ops:
  7.2 0.0 copy-start
  7.2 0.8 convert_reduce_fusion.1
  8.0 0.1 copy.43
  8.1 0.2 reduce_window_sum.11
  8.3 0.1 copy.44
  8.3 0.9 convert_reduce_fusion
  9.3 0.1 reduce_sum.61
  9.4 0.1 reduce_sum.64
  9.4 0.8 copy.45
  10.2 0.1 reshape.141
  10.4 7.3 %gather_fusion = bf16[1152]{0:T(1024)(128)(2,1)S(1)} fusion(bf16[1024]{0:T(1024)(128)(2,1)S(1)} %reshape.141, s32[2048]{0:T(1024)S(1)} %get-tuple-element.22), kind=kCustom, calls=%fused_computation | custom fusion | bytes 9216 | tf_op jit(solution)/shard_map/gather | solution.py:34
  17.7 0.1 reshape.142
  17.8 0.6 copy.46
  18.4 10.0 %all-to-all-start = ((bf16[16,1,72]{2,1,0:T(2,128)(2,1)}), bf16[16,1,72]{2,1,0:T(2,128)(2,1)S(1)}, u32[]{:S(2)}, u32[]{:S(2)}) async-start(bf16[16,1,72]{2,1,0:T(2,128)(2,1)} %copy.46), calls=%async_computation | async-start | bytes 16384 | tf_op jit(solution)/shard_map/all_to_all | solution.py:39
  28.4 0.0 copy-done
  28.4 4.8 %gather_fusion.2 = bf16[1152,768]{1,0:T(8,128)(2,1)} fusion(bf16[1024,768]{1,0:T(8,128)(2,1)S(1)} %bitcast.26, s32[2048]{0:T(1024)S(1)} %get-tuple-element.22), kind=kCustom, calls=%fused_computation.2 | custom fusion | bytes 3543552 | tf_op jit(solution)/shard_map/gather | solution.py:28
  33.2 0.0 copy-start.1
  33.2 3.0 broadcast_select_fusion.1
  36.2 0.0 all-to-all-done
  36.2 7.2 %all-to-all-start.2 = ((bf16[16,72,768]{2,1,0:T(8,128)(2,1)}), bf16[16,72,768]{2,1,0:T(8,128)(2,1)}, u32[]{:S(2)}, u32[]{:S(2)}) async-start(bf16[16,72,768]{2,1,0:T(8,128)(2,1)} %broadcast_select_fusion.1), calls=%async_computation.2 | async-start | bytes 3538944 | tf_op jit(solution)/shard_map/all_to_all | solution.py:37
  43.5 0.0 copy-done.1
  43.5 8.0 %gather_fusion.1 = bf16[1152,4096]{1,0:T(8,128)(2,1)} fusion(bf16[128,4096]{1,0:T(8,128)(2,1)S(1)} %copy-done.1, s32[2048]{0:T(1024)S(1)} %get-tuple-element.21), kind=kCustom, calls=%fused_computation.1 | custom fusion | bytes 18878976 | tf_op jit(solution)/shard_map/gather | solution.py:32
  51.5 8.0 %broadcast_select_fusion = bf16[16,72,4096]{2,1,0:T(8,128)(2,1)} fusion(bf16[16,72,4096]{2,1,0:T(8,128)(2,1)} %bitcast.28, pred[16,72]{1,0:T(8,128)(4,1)S(1)} %get-tuple-element.20), kind=kLoop, calls=%fused_computation.10 | loop fusion | flops 4718592 | bytes 18875520 | tf_op jit(solution)/shard_map/jit(_where)/select_n | solution.py:33
  59.5 26.4 %all-to-all-done.2 = bf16[16,72,768]{2,1,0:T(8,128)(2,1)} async-done(((bf16[16,72,768]{2,1,0:T(8,128)(2,1)}), bf16[16,72,768]{2,1,0:T(8,128)(2,1)}, u32[]{:S(2)}, u32[]{:S(2)}) %all-to-all-start.2) | async-done | bytes 1769504 | tf_op jit(solution)/shard_map/all_to_all | solution.py:37
  85.9 4.7 %all-to-all-start.1 = ((bf16[16,72,4096]{2,1,0:T(8,128)(2,1)}), bf16[16,72,4096]{2,1,0:T(8,128)(2,1)}, u32[]{:S(2)}, u32[]{:S(2)}) async-start(bf16[16,72,4096]{2,1,0:T(8,128)(2,1)} %broadcast_select_fusion), calls=%async_computation.1 | async-start | bytes 18874368 | tf_op jit(solution)/shard_map/all_to_all | solution.py:38
  90.6 0.0 all-gather.2.cloned.1.call-start
  90.7 0.7 all-gather.2.cloned.1.call-update
  91.4 0.2 reduce-scatter.2.cloned.1.call-start
  91.6 204.8 %all-to-all-done.1 = bf16[16,72,4096]{2,1,0:T(8,128)(2,1)} async-done(((bf16[16,72,4096]{2,1,0:T(8,128)(2,1)}), bf16[16,72,4096]{2,1,0:T(8,128)(2,1)}, u32[]{:S(2)}, u32[]{:S(2)}) %all-to-all-start.1) | async-done | bytes 9437216 | tf_op jit(solution)/shard_map/all_to_all | solution.py:38
  296.4 13.7 %bitcast_convert_fusion = bf16[4096,768]{1,0:T(8,128)(2,1)} fusion(bf16[16,72,768]{2,1,0:T(8,128)(2,1)} %all-to-all-done.2, f32[16,72]{1,0:T(8,128)S(1)} %bitcast.30, bf16[16,72,4096]{2,1,0:T(8,128)(2,1)} %all-to-all-done.1), kind=kOutput, calls=%fused_computation.7 | convolution fusion | flops 7265058816 | bytes 17502720 | tf_op jit(solution)/shard_map/dot_general | solution.py:60
  310.1 0.0 copy-start.2
  310.1 0.0 reduce-scatter.2.cloned.1.call-update
  310.1 0.7 copy-done.2
  310.8 0.1 copy.47
  310.9 0.1 reshape.180
  311.0 7.1 %gather_fusion.4 = s32[1024]{0:T(1024)S(1)} fusion(s32[128,16]{1,0:T(8,128)S(1)} %broadcast_add_fusion, s32[1024]{0:T(1024)S(1)} %reshape.180), kind=kCustom, calls=%fused_computation.4 | custom fusion | bytes 16384 | tf_op jit(solution)/shard_map/jit(take_along_axis)/gather | solution.py:67
  318.0 0.1 reshape.183
  318.2 11.8 %fusion.4 = f32[1152]{0:T(1024)S(1)} fusion(bf16[1152,768]{1,0:T(8,128)(2,1)} %bitcast.7, bf16[1,4096,768]{2,1,0:T(8,128)(2,1)} %all-gather.2.cloned.1.call-done, bf16[1152,4096]{1,0:T(8,128)(2,1)} %bitcast.22), kind=kOutput, calls=%fused_computation.13 | convolution fusion | flops 7261912064 | bytes 17502720 | tf_op jit(solution)/shard_map/dot_general | solution.py:43
  330.0 0.7 all_to_all.21
  330.7 5.6 %all-to-all-start.3 = ((f32[16,1,72]{2,1,0:T(1,128)}), f32[16,1,72]{2,1,0:T(1,128)S(1)}, u32[]{:S(2)}, u32[]{:S(2)}) async-start(f32[16,1,72]{2,1,0:T(1,128)} %all_to_all.21), calls=%async_computation.4 | async-start | bytes 16384 | tf_op jit(solution)/shard_map/all_to_all | solution.py:51
  336.4 0.1 copy.49
  336.5 0.1 reshape.174
  336.6 6.7 %all-to-all-done.3 = f32[16,1,72]{2,1,0:T(1,128)S(1)} async-done(((f32[16,1,72]{2,1,0:T(1,128)}), f32[16,1,72]{2,1,0:T(1,128)S(1)}, u32[]{:S(2)}, u32[]{:S(2)}) %all-to-all-start.3) | async-done | bytes 4640 | tf_op jit(solution)/shard_map/all_to_all | solution.py:51
  343.3 6.8 %gather_fusion.3 = f32[1024]{0:T(1024)S(1)} fusion(f32[16,72]{1,0:T(8,128)S(1)} %bitcast.27, s32[1024]{0:T(1024)S(1)} %reshape.174), kind=kCustom, calls=%fused_computation.3 | custom fusion | bytes 16384 | tf_op jit(solution)/shard_map/gather | solution.py:68
  350.1 0.1 reshape.177
  350.2 0.7 copy.50
  350.8 44.4 %reduce-scatter.2.cloned.1.call-done = bf16[256,768]{1,0:T(8,128)(2,1)} async-done(((bf16[4096,768]{1,0:T(8,128)(2,1)}), bf16[256,768]{1,0:T(8,128)(2,1)}) %reduce-scatter.2.cloned.1.call-update) | async-done | bytes 393232 | tf_op jit(solution)/shard_map/reduce_scatter | solution.py:59
  395.2 1.9 bitcast_convert_fusion.1
  (10 shorter events, 0.1 us)
Async XLA Ops:
  7.2 21.2 %copy-start = (bf16[128,8,768]{2,1,0:T(8,128)(2,1)S(1)}, bf16[128,8,768]{2,1,0:T(8,128)(2,1)}, u32[]{:S(2)}) copy-start(bf16[128,8,768]{2,1,0:T(8,128)(2,1)} %param.5) | copy-start | bytes 4718596
  18.4 17.8 %all-to-all-start = ((bf16[16,1,72]{2,1,0:T(2,128)(2,1)}), bf16[16,1,72]{2,1,0:T(2,128)(2,1)S(1)}, u32[]{:S(2)}, u32[]{:S(2)}) async-start(bf16[16,1,72]{2,1,0:T(2,128)(2,1)} %copy.46), calls=%async_computation | async-start | bytes 16384 | tf_op jit(solution)/shard_map/all_to_all | solution.py:39
  33.2 10.3 %copy-start.1 = (bf16[128,4096]{1,0:T(8,128)(2,1)S(1)}, bf16[128,4096]{1,0:T(8,128)(2,1)}, u32[]{:S(2)}) copy-start(bf16[128,4096]{1,0:T(8,128)(2,1)} %param.6) | copy-start | bytes 3145732
  36.2 49.7 %all-to-all-start.2 = ((bf16[16,72,768]{2,1,0:T(8,128)(2,1)}), bf16[16,72,768]{2,1,0:T(8,128)(2,1)}, u32[]{:S(2)}, u32[]{:S(2)}) async-start(bf16[16,72,768]{2,1,0:T(8,128)(2,1)} %broadcast_select_fusion.1), calls=%async_computation.2 | async-start | bytes 3538944 | tf_op jit(solution)/shard_map/all_to_all | solution.py:37
  85.9 210.4 %all-to-all-start.1 = ((bf16[16,72,4096]{2,1,0:T(8,128)(2,1)}), bf16[16,72,4096]{2,1,0:T(8,128)(2,1)}, u32[]{:S(2)}, u32[]{:S(2)}) async-start(bf16[16,72,4096]{2,1,0:T(8,128)(2,1)} %broadcast_select_fusion), calls=%async_computation.1 | async-start | bytes 18874368 | tf_op jit(solution)/shard_map/all_to_all | solution.py:38
  90.6 227.5 %all-gather.2.cloned.1.call-start = ((), (), s32[]{:S(2)}) async-start(), calls=%async_computation.6 | async-start | bytes 6684672 | tf_op jit(solution)/shard_map/all_gather | solution.py:45
  91.4 303.8 %reduce-scatter.2.cloned.1.call-start = ((), (), s32[]{:S(2)}) async-start(), calls=%async_computation.5 | async-start | bytes 6684672 | tf_op jit(solution)/shard_map/reduce_scatter | solution.py:59
  310.1 0.7 copy-start.2
  330.7 12.6 %all-to-all-start.3 = ((f32[16,1,72]{2,1,0:T(1,128)}), f32[16,1,72]{2,1,0:T(1,128)S(1)}, u32[]{:S(2)}, u32[]{:S(2)}) async-start(f32[16,1,72]{2,1,0:T(1,128)} %all_to_all.21), calls=%async_computation.4 | async-start | bytes 16384 | tf_op jit(solution)/shard_map/all_to_all | solution.py:51
Sparse Core Ops, SparseCore 0:
  93.9 67.0 all-gather.1
  310.2 84.9 reduce-scatter.1
where the time goes:
time: 404 us
  waiting for transfers between devices  283 us (70%)
  local copies, waits for them, and re-layouts  38.6 us (10%)
  starting transfers between devices  27.8 us (7%)
  matrix products  25.5 us (6%)
  other arithmetic  15 us (4%)
  between operations  14.2 us (4%)
    all_to_all x1, waiting for transfers between devices, body(): lax.all_to_all(send_dy, 'expert', split_axis=0, concat_axis=0, tiled=True)  205 us
    reduce_scatter x1, waiting for transfers between devices, body(): lax.psum_scatter(lax.dot_general(columns, rows_h, (((0,), (0,)), ((), ())...  44.4 us
    all_to_all x1, waiting for transfers between devices, body(): lax.all_to_all(send_h, 'expert', split_axis=0, concat_axis=0, tiled=True)  26.4 us
    dot_general x1, matrix products, body(): lax.dot_general(columns, rows_h, (((0,), (0,)), ((), ())), preferred_elem...  13.7 us
    dot_general x1, matrix products, body(): lax.dot_general(rows_h, lax.all_gather(w_down, 'dp', axis=1, tiled=True)[...  11.8 us
    all_to_all x1, starting transfers between devices, body(): lax.all_to_all(send_p, 'expert', split_axis=0, concat_axis=0, tiled=True)  9.98 us
  transfers between devices with their start and end apart: 6, of which 4 were waited for; matrix products, arithmetic and copies ran while one was open for 16% of the time, Pallas kernels for 0%

commit v1 on v0

--- a/solution.py
+++ b/solution.py
@@ -7,7 +7,6 @@
 def body(hidden, upstream, probs, expert_ids, w_down):
     tok_rows, top_k = expert_ids.shape
     hid_width = hidden.shape[2]
-    model_width = upstream.shape[1]
     groups = lax.axis_size("expert")
     slots_per = max(tok_rows * 9 // 16, tok_rows * top_k // groups)
     total_rows = groups * slots_per
@@ -29,36 +28,33 @@
         groups, slots_per, hid_width
     )
     send_h = jnp.where(filled[:, :, None], picked_h, jnp.zeros_like(picked_h))
-    picked_dy = upstream[source_tok.reshape(-1)].reshape(groups, slots_per, model_width)
-    send_dy = jnp.where(filled[:, :, None], picked_dy, jnp.zeros_like(picked_dy))
     picked_p = probs.reshape(-1)[flat_index].reshape(groups, slots_per)
     send_p = jnp.where(filled, picked_p, jnp.zeros_like(picked_p))
-    recv_h, recv_dy, recv_p = (
+    dy_all = lax.all_gather(upstream, "expert", axis=0, tiled=True)
+    recv_h, recv_p, recv_tok = (
         lax.all_to_all(send_h, "expert", split_axis=0, concat_axis=0, tiled=True),
-        lax.all_to_all(send_dy, "expert", split_axis=0, concat_axis=0, tiled=True),
         lax.all_to_all(send_p, "expert", split_axis=0, concat_axis=0, tiled=True),
+        lax.all_to_all(source_tok, "expert", split_axis=0, concat_axis=0, tiled=True),
     )
+    row_of = recv_tok + tok_rows * jnp.arange(groups, dtype=jnp.int32)[:, None]
     rows_h = recv_h.reshape(total_rows, hid_width)
-    rows_dy = recv_dy.reshape(total_rows, model_width)
+    rows_dy = dy_all[row_of.reshape(-1)]
     projected = lax.dot_general(
         rows_h,
         lax.all_gather(w_down, "dp", axis=1, tiled=True)[0],
         (((1,), (1,)), ((), ())),
         preferred_element_type=jnp.float32,
     )
-    columns = rows_dy
-    scores = jnp.sum(projected * columns.astype(jnp.float32), axis=1)
+    scores = jnp.sum(projected * rows_dy.astype(jnp.float32), axis=1)
     returned = lax.all_to_all(
         scores.reshape(groups, slots_per), "expert", split_axis=0, concat_axis=0, tiled=True
     )
-    scaled = (recv_p.astype(jnp.float32)[:, :, None] * recv_dy.astype(jnp.float32)).astype(
+    scaled = (recv_p.reshape(total_rows, 1).astype(jnp.float32) * rows_dy.astype(jnp.float32)).astype(
         jnp.bfloat16
     )
-    scaled = scaled.reshape(total_rows, model_width)
-    columns = scaled
     grad_block = lax.psum_scatter(
         lax.dot_general(
-            columns, rows_h, (((0,), (0,)), ((), ())), preferred_element_type=jnp.float32
+            scaled, rows_h, (((0,), (0,)), ((), ())), preferred_element_type=jnp.float32
         ).astype(jnp.bfloat16),
         "dp",
         scatter_dimension=0,

time: 404 us -> 313 us (0.77)
  waiting for transfers between devices: 283 us -> 178 us
  local copies, waits for them, and re-layouts: 38.6 us -> 57.5 us
  other arithmetic: 15 us -> 7.29 us
    all_to_all x1, waiting for transfers between devices: 205 us -> 5.57 us  [body(): lax.all_to_all(source_tok, 'expert', split_axis=0, concat_axis=0, tiled=T...]
    all_gather x0 -> x1, waiting for transfers between devices: none -> 92.2 us  [body(): dy_all = lax.all_gather(upstream, 'expert', axis=0, tiled=True)]
    all_to_all x1, waiting for transfers between devices: 26.4 us -> 0.01 us  [body(): lax.all_to_all(send_h, 'expert', split_axis=0, concat_axis=0, tiled=True)]
    gather x1, local copies, waits for them, and re-layouts: 8.04 us -> 26.6 us  [body(): rows_dy = dy_all[row_of.reshape(-1)]]
    all_gather x1, waiting for transfers between devices: 0.01 us -> 16 us  [body(): lax.all_gather(w_down, 'dp', axis=1, tiled=True)[0]]
    reduce_scatter x1, waiting for transfers between devices: 44.4 us -> 54 us  [body(): lax.psum_scatter(lax.dot_general(scaled, rows_h, (((0,), (0,)), ((), ()))...]
    select_n x2, other arithmetic: 8.07 us -> 0.05 us  [the longest x1 0.02 us: body(): rows_dy = dy_all[row_of.reshape(-1)]]
  transfers between devices with their start and end apart: 6 -> 7, of which waited for: 4 -> 6; matrix products, arithmetic and copies ran while one was open for 16% -> 29% of each run, Pallas kernels for 0% -> 0%
where the time goes in v1:
time: 313 us; the launch traced here: 312 us
  waiting for transfers between devices  178 us (57%)
  local copies, waits for them, and re-layouts  57.5 us (18%)
  matrix products  28.2 us (9%)
  starting transfers between devices  26.6 us (8%)
  between operations  13.9 us (4%)
  other arithmetic  7.29 us (2%)
    all_gather x1, waiting for transfers between devices, body(): dy_all = lax.all_gather(upstream, 'expert', axis=0, tiled=True)  92.2 us
    reduce_scatter x1, waiting for transfers between devices, body(): lax.psum_scatter(lax.dot_general(scaled, rows_h, (((0,), (0,)), ((), ()))...  54 us
    gather x1, local copies, waits for them, and re-layouts, body(): rows_dy = dy_all[row_of.reshape(-1)]  26.6 us
    dot_general x1, matrix products, body(): lax.dot_general(scaled, rows_h, (((0,), (0,)), ((), ())), preferred_eleme...  16.4 us
    all_gather x1, waiting for transfers between devices, body(): lax.all_gather(w_down, 'dp', axis=1, tiled=True)[0]  16 us
    dot_general x1, matrix products, body(): lax.dot_general(rows_h, lax.all_gather(w_down, 'dp', axis=1, tiled=True)[...  11.9 us
    all_to_all x1, starting transfers between devices, body(): lax.all_to_all(send_p, 'expert', split_axis=0, concat_axis=0, tiled=True)  9.98 us
    all_to_all x1, starting transfers between devices, body(): lax.all_to_all(scores.reshape(groups, slots_per), 'expert', split_axis=0,...  7.7 us
  transfers between devices with their start and end apart: 7, of which 6 were waited for; matrix products, arithmetic and copies ran while one was open for 29% of the time, Pallas kernels for 0%

profile of v1, /device:TPU:1, one launch (start us, length us, event | category | flops | bytes accessed | tf_op | source)
XLA Modules:
  0.0 312.0 jit_solution(10945866288315731774)
XLA Ops:
  7.2 0.7 all-gather.3.cloned.1.call-update
  7.9 0.0 all-gather.5.cloned.1.call-start
  8.0 0.7 all-gather.5.cloned.1.call-update
  8.7 0.7 convert_reduce_fusion.1
  9.4 0.1 copy.44
  9.5 0.2 reduce_window_sum.11
  9.6 0.1 copy.45
  9.7 1.5 convert_reduce_fusion
  11.2 0.7 multiply_add_fusion
  11.9 0.1 add.82
  12.0 0.8 copy.46
  12.8 0.1 reshape.148
  13.0 7.3 %gather_fusion = bf16[1152]{0:T(1024)(128)(2,1)S(1)} fusion(bf16[1024]{0:T(1024)(128)(2,1)S(1)} %reshape.148, s32[2048]{0:T(1024)S(1)} %pad_clamp_fusion.1), kind=kCustom, calls=%fused_computation | custom fusion | bytes 9216 | tf_op jit(solution)/shard_map/gather | solution.py:31
  20.2 0.1 reshape.149
  20.4 0.6 copy.47
  21.0 10.0 %all-to-all-start = ((bf16[16,1,72]{2,1,0:T(2,128)(2,1)}), bf16[16,1,72]{2,1,0:T(2,128)(2,1)S(1)}, u32[]{:S(2)}, u32[]{:S(2)}) async-start(bf16[16,1,72]{2,1,0:T(2,128)(2,1)} %copy.47), calls=%async_computation | async-start | bytes 16384 | tf_op jit(solution)/shard_map/all_to_all | solution.py:36
  30.9 4.6 %gather_fusion.2 = bf16[1152,768]{1,0:T(8,128)(2,1)S(1)} fusion(bf16[1024,768]{1,0:T(8,128)(2,1)S(1)} %bitcast.23, s32[2048]{0:T(1024)S(1)} %pad_clamp_fusion.1), kind=kCustom, calls=%fused_computation.2 | custom fusion | bytes 3543552 | tf_op jit(solution)/shard_map/gather | solution.py:27
  35.5 2.5 all-to-all-done
  38.0 4.7 %all-to-all-start.1 = ((s32[16,1,72]{2,1,0:T(1,128)}), s32[16,1,72]{2,1,0:T(1,128)S(1)}, u32[]{:S(2)}, u32[]{:S(2)}) async-start(s32[16,1,72]{2,1,0:T(1,128)} %bitcast.2), calls=%async_computation.1 | async-start | bytes 16384 | tf_op jit(solution)/shard_map/all_to_all | solution.py:37
  42.7 1.5 broadcast_select_fusion
  44.2 5.6 %all-to-all-done.1 = s32[16,1,72]{2,1,0:T(1,128)S(1)} async-done(((s32[16,1,72]{2,1,0:T(1,128)}), s32[16,1,72]{2,1,0:T(1,128)S(1)}, u32[]{:S(2)}, u32[]{:S(2)}) %all-to-all-start.1) | async-done | bytes 4640 | tf_op jit(solution)/shard_map/all_to_all | solution.py:37
  49.8 4.1 %all-to-all-start.2 = ((bf16[16,72,768]{2,1,0:T(8,128)(2,1)}), bf16[16,72,768]{2,1,0:T(8,128)(2,1)S(1)}, u32[]{:S(2)}, u32[]{:S(2)}) async-start(bf16[16,72,768]{2,1,0:T(8,128)(2,1)} %broadcast_select_fusion), calls=%async_computation.2 | async-start | bytes 3538944 | tf_op jit(solution)/shard_map/all_to_all | solution.py:35
  53.9 0.1 add.84
  54.0 0.1 add.85
  54.1 0.1 reshape.153
  54.2 0.5 broadcast.190
  54.7 0.7 reduce.11
  55.4 0.1 all_to_all.26
  55.6 92.2 %all-gather.3.cloned.1.call-done = bf16[2048,4096]{1,0:T(8,128)(2,1)} async-done(((bf16[128,4096]{1,0:T(8,128)(2,1)}), bf16[2048,4096]{1,0:T(8,128)(2,1)}) %all-gather.3.cloned.1.call-update) | async-done | bytes 16777232 | tf_op jit(solution)/shard_map/all_gather | solution.py:33
  147.8 26.6 %gather_fusion.1 = bf16[1152,4096]{1,0:T(8,128)(2,1)} fusion(bf16[2048,4096]{1,0:T(8,128)(2,1)} %all-gather.3.cloned.1.call-done, s32[2048]{0:T(1024)S(1)} %pad_clamp_fusion), kind=kCustom, calls=%fused_computation.1 | custom fusion | bytes 18878976 | tf_op jit(solution)/shard_map/gather | solution.py:41
  174.3 16.4 %fusion.4 = bf16[4096,768]{1,0:T(8,128)(2,1)} fusion(bf16[1152,768]{1,0:T(8,128)(2,1)S(1)} %bitcast.26, bf16[1152,4096]{1,0:T(8,128)(2,1)} %gather_fusion.1, f32[1152]{0:T(1024)S(1)} %reshape.153), kind=kOutput, calls=%fused_computation.10 | convolution fusion | flops 7265058816 | bytes 17502720 | tf_op jit(solution)/shard_map/dot_general | solution.py:56
  190.7 0.7 copy-done.1
  191.4 0.1 copy.49
  191.5 0.1 reshape.185
  191.6 7.1 %gather_fusion.4 = s32[1024]{0:T(1024)S(1)} fusion(s32[128,16]{1,0:T(8,128)S(1)} %broadcast_add_fusion, s32[1024]{0:T(1024)S(1)} %reshape.185), kind=kCustom, calls=%fused_computation.4 | custom fusion | bytes 16384 | tf_op jit(solution)/shard_map/jit(take_along_axis)/gather | solution.py:63
  198.7 0.1 reshape.188
  198.8 16.0 %all-gather.5.cloned.1.call-done = bf16[1,4096,768]{2,1,0:T(8,128)(2,1)} async-done(((bf16[1,256,768]{2,1,0:T(8,128)(2,1)}), bf16[1,4096,768]{2,1,0:T(8,128)(2,1)}) %all-gather.5.cloned.1.call-update) | async-done | bytes 6291472 | tf_op jit(solution)/shard_map/all_gather | solution.py:44
  214.8 11.9 %fusion.8 = f32[1152]{0:T(1024)S(1)} fusion(bf16[1152,4096]{1,0:T(8,128)(2,1)} %gather_fusion.1, bf16[1152,768]{1,0:T(8,128)(2,1)S(1)} %bitcast.27, bf16[1,4096,768]{2,1,0:T(8,128)(2,1)} %all-gather.5.cloned.1.call-done), kind=kOutput, calls=%fused_computation.12 | convolution fusion | flops 7261912064 | bytes 17502720 | tf_op jit(solution)/shard_map/dot_general | solution.py:42
  226.7 0.7 all_to_all.28
  227.4 7.7 %all-to-all-start.3 = ((f32[16,1,72]{2,1,0:T(1,128)}), f32[16,1,72]{2,1,0:T(1,128)S(1)}, u32[]{:S(2)}, u32[]{:S(2)}) async-start(f32[16,1,72]{2,1,0:T(1,128)} %all_to_all.28), calls=%async_computation.4 | async-start | bytes 16384 | tf_op jit(solution)/shard_map/all_to_all | solution.py:49
  235.1 0.1 copy.51
  235.2 0.1 reshape.179
  235.3 6.7 %all-to-all-done.3 = f32[16,1,72]{2,1,0:T(1,128)S(1)} async-done(((f32[16,1,72]{2,1,0:T(1,128)}), f32[16,1,72]{2,1,0:T(1,128)S(1)}, u32[]{:S(2)}, u32[]{:S(2)}) %all-to-all-start.3) | async-done | bytes 4640 | tf_op jit(solution)/shard_map/all_to_all | solution.py:49
  242.0 6.8 %gather_fusion.3 = f32[1024]{0:T(1024)S(1)} fusion(f32[16,72]{1,0:T(8,128)S(1)} %bitcast.24, s32[1024]{0:T(1024)S(1)} %reshape.179), kind=kCustom, calls=%fused_computation.3 | custom fusion | bytes 16384 | tf_op jit(solution)/shard_map/gather | solution.py:64
  248.8 0.1 reshape.182
  248.9 0.7 copy.52
  249.6 54.0 %reduce-scatter.2.cloned.1.call-done = bf16[256,768]{1,0:T(8,128)(2,1)} async-done(((bf16[4096,768]{1,0:T(8,128)(2,1)}), bf16[256,768]{1,0:T(8,128)(2,1)}) %reduce-scatter.2.cloned.1.call-update) | async-done | bytes 393232 | tf_op jit(solution)/shard_map/reduce_scatter | solution.py:55
  303.6 1.9 bitcast_convert_fusion
  (19 shorter events, 0.3 us)
Async XLA Ops:
  7.2 23.8 %copy-start = (bf16[128,8,768]{2,1,0:T(8,128)(2,1)S(1)}, bf16[128,8,768]{2,1,0:T(8,128)(2,1)}, u32[]{:S(2)}) copy-start(bf16[128,8,768]{2,1,0:T(8,128)(2,1)} %param.5) | copy-start | bytes 4718596
  7.2 140.6 %all-gather.3.cloned.1.call-start = ((), (), s32[]{:S(2)}) async-start(), calls=%async_computation.5 | async-start | bytes 17825792 | tf_op jit(solution)/shard_map/all_gather | solution.py:33
  7.9 206.9 %all-gather.5.cloned.1.call-start = ((), (), s32[]{:S(2)}) async-start(), calls=%async_computation.7 | async-start | bytes 6684672 | tf_op jit(solution)/shard_map/all_gather | solution.py:44
  21.0 17.1 %all-to-all-start = ((bf16[16,1,72]{2,1,0:T(2,128)(2,1)}), bf16[16,1,72]{2,1,0:T(2,128)(2,1)S(1)}, u32[]{:S(2)}, u32[]{:S(2)}) async-start(bf16[16,1,72]{2,1,0:T(2,128)(2,1)} %copy.47), calls=%async_computation | async-start | bytes 16384 | tf_op jit(solution)/shard_map/all_to_all | solution.py:36
  38.0 11.7 %all-to-all-start.1 = ((s32[16,1,72]{2,1,0:T(1,128)}), s32[16,1,72]{2,1,0:T(1,128)S(1)}, u32[]{:S(2)}, u32[]{:S(2)}) async-start(s32[16,1,72]{2,1,0:T(1,128)} %bitcast.2), calls=%async_computation.1 | async-start | bytes 16384 | tf_op jit(solution)/shard_map/all_to_all | solution.py:37
  49.8 124.6 %all-to-all-start.2 = ((bf16[16,72,768]{2,1,0:T(8,128)(2,1)}), bf16[16,72,768]{2,1,0:T(8,128)(2,1)S(1)}, u32[]{:S(2)}, u32[]{:S(2)}) async-start(bf16[16,72,768]{2,1,0:T(8,128)(2,1)} %broadcast_select_fusion), calls=%async_computation.2 | async-start | bytes 3538944 | tf_op jit(solution)/shard_map/all_to_all | solution.py:35
  53.9 249.7 %reduce-scatter.2.cloned.1.call-start = ((), (), s32[]{:S(2)}) async-start(), calls=%async_computation.6 | async-start | bytes 6684672 | tf_op jit(solution)/shard_map/reduce_scatter | solution.py:55
  190.7 0.7 copy-start.1
  227.4 14.6 %all-to-all-start.3 = ((f32[16,1,72]{2,1,0:T(1,128)}), f32[16,1,72]{2,1,0:T(1,128)S(1)}, u32[]{:S(2)}, u32[]{:S(2)}) async-start(f32[16,1,72]{2,1,0:T(1,128)} %all_to_all.28), calls=%async_computation.4 | async-start | bytes 16384 | tf_op jit(solution)/shard_map/all_to_all | solution.py:49
Sparse Core Ops, SparseCore 0:
  9.8 137.8 all-gather.2
  150.3 64.4 all-gather.4
  218.5 85.0 reduce-scatter.1

commit v2 on v1

v2 whole, which is shorter than its diff:
```python
import jax
import jax.numpy as jnp
from jax import lax
from jax.sharding import Mesh, PartitionSpec as P


def body(hidden, upstream, probs, expert_ids, w_down):
    tok_rows, top_k = expert_ids.shape
    hid_width = hidden.shape[2]
    model_width = upstream.shape[1]
    lanes = 128
    n_z = lax.axis_size("z")
    n_core = lax.axis_size("core")
    groups = n_z * n_core
    n_dp = lax.axis_size("dp")
    slots_per = max(tok_rows * 9 // 16, tok_rows * top_k // groups)
    total_rows = groups * slots_per
    chosen = (expert_ids[:, :, None] == jnp.arange(groups, dtype=jnp.int32)[None, None, :]).astype(
        jnp.int32
    )
    member = jnp.sum(chosen, axis=1)
    slot_place = jnp.cumsum(member, axis=0) - 1
    which_k = jnp.sum(chosen * jnp.arange(top_k, dtype=jnp.int32)[None, :, None], axis=1)
    target = (
        (member == 1)[:, :, None]
        & (slot_place[:, :, None] == jnp.arange(slots_per, dtype=jnp.int32)[None, None, :])
    ).astype(jnp.int32)
    filled = jnp.sum(target, axis=0) == 1
    source_tok = jnp.sum(target * jnp.arange(tok_rows, dtype=jnp.int32)[:, None, None], axis=0)
    source_k = jnp.sum(target * which_k[:, :, None], axis=0)
    flat_index = (source_tok * top_k + source_k).reshape(-1)
    picked_h = hidden.reshape(tok_rows * top_k, hid_width)[flat_index].reshape(
        groups, slots_per, hid_width
    )
    send_h = jnp.where(filled[:, :, None], picked_h, jnp.zeros_like(picked_h))
    picked_p = probs.reshape(-1)[flat_index].reshape(groups, slots_per)
    send_p = jnp.where(filled, picked_p, jnp.zeros_like(picked_p))
    dy3 = upstream.reshape(tok_rows, model_width // lanes, lanes)
    dy_z = lax.all_gather(dy3, "z", axis=0, tiled=True)
    dy_pair = lax.ppermute(dy_z, "core", perm=[(c, (c + 1) % n_core) for c in range(n_core)])
    dy_all = jnp.concatenate([dy_z, dy_pair], axis=0)
    w_blocks = lax.all_to_all(
        jnp.broadcast_to(w_down, (n_dp,) + w_down.shape[1:]), "dp", split_axis=0, concat_axis=0, tiled=True
    )
    w_full = w_blocks.reshape(n_dp * w_down.shape[1] // lanes, lanes, hid_width)
    ez = ("z", "core")
    recv_h, recv_p, recv_tok = (
        lax.all_to_all(send_h, ez, split_axis=0, concat_axis=0, tiled=True),
        lax.all_to_all(send_p, ez, split_axis=0, concat_axis=0, tiled=True),
        lax.all_to_all(source_tok, ez, split_axis=0, concat_axis=0, tiled=True),
    )
    src = jnp.arange(groups, dtype=jnp.int32)
    src_z, src_core = src // n_core, src % n_core
    my_core = lax.axis_index("core")
    block = (src_core - my_core + n_core) % n_core
    row_of = recv_tok + (tok_rows * (block * n_z + src_z))[:, None]
    rows_h = recv_h.reshape(total_rows, hid_width)
    rows_dy = dy_all[row_of.reshape(-1)]
    projected = lax.dot_general(
        rows_h, w_full, (((1,), (2,)), ((), ())), preferred_element_type=jnp.float32
    )
    scores = jnp.sum(projected * rows_dy.astype(jnp.float32), axis=(1, 2))
    returned = lax.all_to_all(
        scores.reshape(groups, slots_per), ez, split_axis=0, concat_axis=0, tiled=True
    )
    scaled = (
        recv_p.reshape(total_rows, 1, 1).astype(jnp.float32) * rows_dy.astype(jnp.float32)
    ).astype(jnp.bfloat16)
    partial = lax.dot_general(
        scaled, rows_h, (((0,), (0,)), ((), ())), preferred_element_type=jnp.float32
    ).astype(jnp.bfloat16)
    grad_block = lax.psum_scatter(
        partial.reshape(model_width, hid_width), "dp", scatter_dimension=0, tiled=True
    ).astype(jnp.float32)
    place_slot = jnp.take_along_axis(slot_place, expert_ids, axis=1)
    gate_grad = returned[expert_ids, place_slot]
    return (grad_block[None], gate_grad)


def solution(mesh):
    n_dp, n_expert = mesh.devices.shape
    sub = Mesh(mesh.devices.reshape(n_dp, n_expert // 2, 2), ("dp", "z", "core"))
    tok = ("dp", "z", "core")
    in_specs = (
        P(tok, None, None),
        P(tok, None),
        P(tok, None),
        P(tok, None),
        P(("z", "core"), "dp", None),
    )
    out_specs = (P(("z", "core"), "dp", None), P(tok, None))
    return jax.shard_map(body, mesh=sub, in_specs=in_specs, out_specs=out_specs, check_vma=False)
```

time: 313 us -> 390 us (1.25)
  waiting for transfers between devices: 178 us -> 234 us
  other arithmetic: 7.29 us -> 24 us
    all_to_all x4 -> x5, waiting for transfers between devices: 14.8 us -> 122 us  [the longest x1 107 us: body(): lax.all_to_all(jnp.broadcast_to(w_down, (n_dp,) + w_down.shape[1:]), 'dp'...]
    reduce_scatter x1, waiting for transfers between devices: 54 us -> 13.9 us  [body(): lax.psum_scatter(partial.reshape(model_width, hid_width), 'dp', scatter_d...]
    concatenate x0 -> x1, other arithmetic: none -> 16.7 us  [body(): dy_all = jnp.concatenate([dy_z, dy_pair], axis=0)]
    all_gather x2 -> x1, waiting for transfers between devices: 108 us -> 98.1 us  [body(): dy_z = lax.all_gather(dy3, 'z', axis=0, tiled=True)]
    gather x1 -> x2, local copies, waits for them, and re-layouts: 26.6 us -> 24.7 us  [body(): rows_dy = dy_all[row_of.reshape(-1)]]
    all_to_all x4 -> x5, starting transfers between devices: 26.5 us -> 27 us  [the longest x1 7.06 us: body(): lax.all_to_all(scores.reshape(groups, slots_per), ez, split_axis=0, conca...]
  transfers between devices with their start and end apart: 7 -> 8, of which waited for: 6 -> 6; matrix products, arithmetic and copies ran while one was open for 29% -> 24% of each run, Pallas kernels for 0% -> 0%
where the time goes in v2:
time: 390 us; the launch traced here: 389 us
  waiting for transfers between devices  234 us (60%)
  local copies, waits for them, and re-layouts  60.9 us (16%)
  matrix products  28.2 us (7%)
  starting transfers between devices  27.8 us (7%)
  other arithmetic  24 us (6%)
  between operations  14.2 us (4%)
    all_to_all x1, waiting for transfers between devices, body(): lax.all_to_all(jnp.broadcast_to(w_down, (n_dp,) + w_down.shape[1:]), 'dp'...  107 us
    all_gather x1, waiting for transfers between devices, body(): dy_z = lax.all_gather(dy3, 'z', axis=0, tiled=True)  98.1 us
    gather x2, local copies, waits for them, and re-layouts, body(): rows_dy = dy_all[row_of.reshape(-1)]  24.7 us
    concatenate x1, other arithmetic, body(): dy_all = jnp.concatenate([dy_z, dy_pair], axis=0)  16.7 us
    dot_general x1, matrix products, body(): lax.dot_general(rows_h, w_full, (((1,), (2,)), ((), ())), preferred_eleme...  14.2 us
    dot_general x1, matrix products, body(): lax.dot_general(scaled, rows_h, (((0,), (0,)), ((), ())), preferred_eleme...  14 us
    reduce_scatter x1, waiting for transfers between devices, body(): lax.psum_scatter(partial.reshape(model_width, hid_width), 'dp', scatter_d...  13.9 us
  transfers between devices with their start and end apart: 8, of which 6 were waited for; matrix products, arithmetic and copies ran while one was open for 24% of the time, Pallas kernels for 0%

profile of v2, /device:TPU:1, one launch (start us, length us, event | category | flops | bytes accessed | tf_op | source)
XLA Modules:
  0.0 389.1 jit_solution(15925728178710582814)
XLA Ops:
  7.2 2.6 copy.58
  9.8 98.1 %all-gather.2.cloned.1.call-done = bf16[1024,32,128]{2,1,0:T(8,128)(2,1)} async-done(((bf16[128,32,128]{2,1,0:T(8,128)(2,1)}), bf16[1024,32,128]{2,1,0:T(8,128)(2,1)}) %all-gather.2.cloned.1.call-update) | async-done | bytes 8388624 | tf_op jit(solution)/shard_map/all_gather | solution.py:39
  107.9 0.7 collective-permute-start
  108.6 0.7 convert_reduce_fusion.1
  109.3 0.1 copy.48
  109.4 0.2 reduce_window_sum.11
  109.6 1.5 convert_reduce_fusion
  111.1 0.7 multiply_add_fusion
  111.8 0.1 add.119
  111.9 0.8 copy.50
  112.7 0.1 reshape.188
  112.9 7.3 %gather_fusion = bf16[1152]{0:T(1024)(128)(2,1)S(1)} fusion(bf16[1024]{0:T(1024)(128)(2,1)S(1)} %reshape.188, s32[2048]{0:T(1024)S(1)} %pad_clamp_fusion.1), kind=kCustom, calls=%fused_computation | custom fusion | bytes 9216 | tf_op jit(solution)/shard_map/gather | solution.py:36
  120.2 0.1 reshape.189
  120.3 0.6 copy.51
  120.9 4.4 %all-to-all-start = ((bf16[16,1,72]{2,1,0:T(2,128)(2,1)}), bf16[16,1,72]{2,1,0:T(2,128)(2,1)S(1)}, u32[]{:S(2)}, u32[]{:S(2)}) async-start(bf16[16,1,72]{2,1,0:T(2,128)(2,1)} %copy.51), calls=%async_computation | async-start | bytes 16384 | tf_op jit(solution)/shard_map/all_to_all | solution.py:49
  125.3 4.6 %gather_fusion.2 = bf16[1152,768]{1,0:T(8,128)(2,1)S(1)} fusion(bf16[1024,768]{1,0:T(8,128)(2,1)S(1)} %bitcast.26, s32[2048]{0:T(1024)S(1)} %pad_clamp_fusion.1), kind=kCustom, calls=%fused_computation.2 | custom fusion | bytes 3543552 | tf_op jit(solution)/shard_map/gather | solution.py:32
  129.9 2.5 all-to-all-done
  132.3 4.8 %all-to-all-start.1 = ((s32[16,1,72]{2,1,0:T(1,128)}), s32[16,1,72]{2,1,0:T(1,128)S(1)}, u32[]{:S(2)}, u32[]{:S(2)}) async-start(s32[16,1,72]{2,1,0:T(1,128)} %bitcast.2), calls=%async_computation.1 | async-start | bytes 16384 | tf_op jit(solution)/shard_map/all_to_all | solution.py:50
  137.1 1.4 broadcast_select_fusion
  138.6 5.5 %all-to-all-done.1 = s32[16,1,72]{2,1,0:T(1,128)S(1)} async-done(((s32[16,1,72]{2,1,0:T(1,128)}), s32[16,1,72]{2,1,0:T(1,128)S(1)}, u32[]{:S(2)}, u32[]{:S(2)}) %all-to-all-start.1) | async-done | bytes 4640 | tf_op jit(solution)/shard_map/all_to_all | solution.py:50
  144.1 4.2 %all-to-all-start.2 = ((bf16[16,72,768]{2,1,0:T(8,128)(2,1)}), bf16[16,72,768]{2,1,0:T(8,128)(2,1)S(1)}, u32[]{:S(2)}, u32[]{:S(2)}) async-start(bf16[16,72,768]{2,1,0:T(8,128)(2,1)} %broadcast_select_fusion), calls=%async_computation.2 | async-start | bytes 3538944 | tf_op jit(solution)/shard_map/all_to_all | solution.py:48
  148.4 0.1 add.126
  148.5 0.1 reshape.196
  148.6 0.5 broadcast.287
  149.1 0.7 reduce.11
  149.8 0.1 all_to_all.29
  149.9 16.7 %pad_maximum_fusion = bf16[2048,32,128]{2,1,0:T(8,128)(2,1)} fusion(bf16[1024,32,128]{2,1,0:T(8,128)(2,1)} %collective-permute-done, bf16[1024,32,128]{2,1,0:T(8,128)(2,1)} %all-gather.2.cloned.1.call-done), kind=kLoop, calls=%fused_computation.8 | loop fusion | flops 8388608 | bytes 33554432 | tf_op jit(solution)/shard_map/concatenate | solution.py:41
  166.6 11.8 %gather_fusion.1 = bf16[1152,32,128]{2,1,0:T(8,128)(2,1)} fusion(bf16[2048,32,128]{2,1,0:T(8,128)(2,1)} %pad_maximum_fusion, s32[2048]{0:T(1024)S(1)} %pad_clamp_fusion), kind=kCustom, calls=%fused_computation.1 | custom fusion | bytes 18878976 | tf_op jit(solution)/shard_map/gather | solution.py:58
  178.4 12.9 %copy.53 = bf16[1152,32,128]{0,2,1:T(8,128)(2,1)} copy(bf16[1152,32,128]{2,1,0:T(8,128)(2,1)} %gather_fusion.1) | data formatting | bytes 18874368 | tf_op jit(solution)/shard_map/gather | solution.py:58
  191.3 14.0 %fusion.5 = bf16[32,128,768]{2,1,0:T(8,128)(2,1)} fusion(bf16[1152,768,1]{1,0,2:T(8,128)(2,1)S(1)} %bitcast.31, bf16[1152,32,128]{0,2,1:T(8,128)(2,1)} %copy.53, f32[1152]{0:T(1024)S(1)} %reshape.196), kind=kOutput, calls=%fused_computation.12 | convolution fusion | flops 7265058816 | bytes 17502720 | tf_op jit(solution)/shard_map/dot_general | solution.py:69
  205.4 3.3 broadcast_in_dim.54
  208.7 6.6 %all-to-all-start.3 = ((bf16[16,256,768]{2,1,0:T(8,128)(2,1)}), bf16[16,256,768]{2,1,0:T(8,128)(2,1)}, u32[]{:S(2)}, u32[]{:S(2)}) async-start(bf16[16,256,768]{2,1,0:T(8,128)(2,1)} %broadcast_in_dim.54), calls=%async_computation.4 | async-start | bytes 12582912 | tf_op jit(solution)/shard_map/all_to_all | solution.py:42
  215.3 0.1 copy.54
  215.4 0.1 reshape.228
  215.5 7.1 %gather_fusion.4 = s32[1024]{0:T(1024)S(1)} fusion(s32[128,16]{1,0:T(8,128)S(1)} %broadcast_add_fusion, s32[1024]{0:T(1024)S(1)} %reshape.228), kind=kCustom, calls=%fused_computation.4 | custom fusion | bytes 16384 | tf_op jit(solution)/shard_map/jit(take_along_axis)/gather | solution.py:75
  222.6 0.1 reshape.231
  222.7 107.3 %all-to-all-done.3 = bf16[16,256,768]{2,1,0:T(8,128)(2,1)} async-done(((bf16[16,256,768]{2,1,0:T(8,128)(2,1)}), bf16[16,256,768]{2,1,0:T(8,128)(2,1)}, u32[]{:S(2)}, u32[]{:S(2)}) %all-to-all-start.3) | async-done | bytes 6291488 | tf_op jit(solution)/shard_map/all_to_all | solution.py:42
  330.0 14.2 %fusion.4 = f32[1152]{0:T(1024)S(1)} fusion(bf16[1152,32,128]{0,2,1:T(8,128)(2,1)} %copy.53, bf16[1152,768,1]{1,0,2:T(8,128)(2,1)S(1)} %bitcast.32, bf16[32,128,768]{2,1,0:T(8,128)(2,1)} %bitcast.11), kind=kOutput, calls=%fused_computation.11 | convolution fusion | flops 7261912064 | bytes 17502720 | tf_op jit(solution)/shard_map/dot_general | solution.py:59
  344.2 0.7 all_to_all.32
  344.9 7.1 %all-to-all-start.4 = ((f32[16,1,72]{2,1,0:T(1,128)}), f32[16,1,72]{2,1,0:T(1,128)S(1)}, u32[]{:S(2)}, u32[]{:S(2)}) async-start(f32[16,1,72]{2,1,0:T(1,128)} %all_to_all.32), calls=%async_computation.5 | async-start | bytes 16384 | tf_op jit(solution)/shard_map/all_to_all | solution.py:63
  352.0 0.1 copy.56
  352.1 0.1 reshape.222
  352.2 6.7 %all-to-all-done.4 = f32[16,1,72]{2,1,0:T(1,128)S(1)} async-done(((f32[16,1,72]{2,1,0:T(1,128)}), f32[16,1,72]{2,1,0:T(1,128)S(1)}, u32[]{:S(2)}, u32[]{:S(2)}) %all-to-all-start.4) | async-done | bytes 4640 | tf_op jit(solution)/shard_map/all_to_all | solution.py:63
  358.9 6.8 %gather_fusion.3 = f32[1024]{0:T(1024)S(1)} fusion(f32[16,72]{1,0:T(8,128)S(1)} %bitcast.27, s32[1024]{0:T(1024)S(1)} %reshape.222), kind=kCustom, calls=%fused_computation.3 | custom fusion | bytes 16384 | tf_op jit(solution)/shard_map/gather | solution.py:76
  365.7 0.1 reshape.225
  365.8 0.7 copy.57
  366.4 13.9 %reduce-scatter.2.cloned.1.call-done = bf16[256,768]{1,0:T(8,128)(2,1)} async-done(((bf16[4096,768]{1,0:T(8,128)(2,1)}), bf16[256,768]{1,0:T(8,128)(2,1)}) %reduce-scatter.2.cloned.1.call-update) | async-done | bytes 393232 | tf_op jit(solution)/shard_map/reduce_scatter | solution.py:72
  380.4 1.9 bitcast_convert_fusion
  (28 shorter events, 0.4 us)
Async XLA Ops:
  7.2 118.2 %copy-start = (bf16[128,8,768]{2,1,0:T(8,128)(2,1)S(1)}, bf16[128,8,768]{2,1,0:T(8,128)(2,1)}, u32[]{:S(2)}) copy-start(bf16[128,8,768]{2,1,0:T(8,128)(2,1)} %param.5) | copy-start | bytes 4718596
  7.2 100.7 %all-gather.2.cloned.1.call-start = ((), (), s32[]{:S(2)}) async-start(), calls=%async_computation.6 | async-start | bytes 9437184 | tf_op jit(solution)/shard_map/all_gather | solution.py:39
  107.9 42.0 %collective-permute-start = (bf16[1024,32,128]{2,1,0:T(8,128)(2,1)}, bf16[1024,32,128]{2,1,0:T(8,128)(2,1)}, u32[]{:S(2)}, u32[]{:S(2)}) collective-permute-start(bf16[1024,32,128]{2,1,0:T(8,128)(2,1)} %all-gather.2.cloned.1.call-done), channel_id=1, source_target_pairs={{0,1},{1,0},{2,3},{3,2},{4,5},{5,4},{6,7},{7,6},{8,9},{9,8},{10,11... | collective-permute-start | bytes 25165832 | tf_op jit(solution)/shard_map/ppermute | solution.py:40
  120.9 11.5 %all-to-all-start = ((bf16[16,1,72]{2,1,0:T(2,128)(2,1)}), bf16[16,1,72]{2,1,0:T(2,128)(2,1)S(1)}, u32[]{:S(2)}, u32[]{:S(2)}) async-start(bf16[16,1,72]{2,1,0:T(2,128)(2,1)} %copy.51), calls=%async_computation | async-start | bytes 16384 | tf_op jit(solution)/shard_map/all_to_all | solution.py:49
  132.3 11.7 %all-to-all-start.1 = ((s32[16,1,72]{2,1,0:T(1,128)}), s32[16,1,72]{2,1,0:T(1,128)S(1)}, u32[]{:S(2)}, u32[]{:S(2)}) async-start(s32[16,1,72]{2,1,0:T(1,128)} %bitcast.2), calls=%async_computation.1 | async-start | bytes 16384 | tf_op jit(solution)/shard_map/all_to_all | solution.py:50
  144.1 47.3 %all-to-all-start.2 = ((bf16[16,72,768]{2,1,0:T(8,128)(2,1)}), bf16[16,72,768]{2,1,0:T(8,128)(2,1)S(1)}, u32[]{:S(2)}, u32[]{:S(2)}) async-start(bf16[16,72,768]{2,1,0:T(8,128)(2,1)} %broadcast_select_fusion), calls=%async_computation.2 | async-start | bytes 3538944 | tf_op jit(solution)/shard_map/all_to_all | solution.py:48
  148.2 232.1 %reduce-scatter.2.cloned.1.call-start = ((), (), s32[]{:S(2)}) async-start(), calls=%async_computation.7 | async-start | bytes 6684672 | tf_op jit(solution)/shard_map/reduce_scatter | solution.py:72
  191.3 14.0 %copy-start.2 = (bf16[1,256,768]{2,1,0:T(8,128)(2,1)S(1)}, bf16[1,256,768]{2,1,0:T(8,128)(2,1)}, u32[]{:S(2)}) copy-start(bf16[1,256,768]{2,1,0:T(8,128)(2,1)} %param.9) | copy-start | bytes 1179652
  205.3 9.9 %copy-start.3 = (s32[128,8]{0,1:T(8,128)S(1)}, s32[128,8]{0,1:T(8,128)}, u32[]{:S(2)}) copy-start(s32[128,8]{0,1:T(8,128)} %param.8) | copy-start | bytes 12292
  208.7 121.3 %all-to-all-start.3 = ((bf16[16,256,768]{2,1,0:T(8,128)(2,1)}), bf16[16,256,768]{2,1,0:T(8,128)(2,1)}, u32[]{:S(2)}, u32[]{:S(2)}) async-start(bf16[16,256,768]{2,1,0:T(8,128)(2,1)} %broadcast_in_dim.54), calls=%async_computation.4 | async-start | bytes 12582912 | tf_op jit(solution)/shard_map/all_to_all | solution.py:42
  344.9 14.0 %all-to-all-start.4 = ((f32[16,1,72]{2,1,0:T(1,128)}), f32[16,1,72]{2,1,0:T(1,128)S(1)}, u32[]{:S(2)}, u32[]{:S(2)}) async-start(f32[16,1,72]{2,1,0:T(1,128)} %all_to_all.32), calls=%async_computation.5 | async-start | bytes 16384 | tf_op jit(solution)/shard_map/all_to_all | solution.py:63
  358.9 23.4 %copy-start.1 = (bf16[128,8,768]{2,1,0:T(8,128)(2,1)S(1)}, bf16[128,8,768]{2,1,0:T(8,128)(2,1)}, u32[]{:S(2)}) copy-start(bf16[128,8,768]{2,1,0:T(8,128)(2,1)} %param.5) | copy-start | bytes 4718596
Sparse Core Ops, SparseCore 0:
  9.9 97.9 all-gather.1
  205.5 174.8 reduce-scatter.1

commit v3 on v2

--- a/solution.py
+++ b/solution.py
@@ -37,40 +37,48 @@
     send_p = jnp.where(filled, picked_p, jnp.zeros_like(picked_p))
     dy3 = upstream.reshape(tok_rows, model_width // lanes, lanes)
     dy_z = lax.all_gather(dy3, "z", axis=0, tiled=True)
-    dy_pair = lax.ppermute(dy_z, "core", perm=[(c, (c + 1) % n_core) for c in range(n_core)])
-    dy_all = jnp.concatenate([dy_z, dy_pair], axis=0)
-    w_blocks = lax.all_to_all(
-        jnp.broadcast_to(w_down, (n_dp,) + w_down.shape[1:]), "dp", split_axis=0, concat_axis=0, tiled=True
-    )
-    w_full = w_blocks.reshape(n_dp * w_down.shape[1] // lanes, lanes, hid_width)
+    w_full = lax.all_gather(w_down, "dp", axis=1, tiled=True)[0]
     ez = ("z", "core")
     recv_h, recv_p, recv_tok = (
         lax.all_to_all(send_h, ez, split_axis=0, concat_axis=0, tiled=True),
         lax.all_to_all(send_p, ez, split_axis=0, concat_axis=0, tiled=True),
         lax.all_to_all(source_tok, ez, split_axis=0, concat_axis=0, tiled=True),
     )
-    src = jnp.arange(groups, dtype=jnp.int32)
-    src_z, src_core = src // n_core, src % n_core
+    dy_z, recv_h, recv_p, recv_tok = lax.optimization_barrier((dy_z, recv_h, recv_p, recv_tok))
+    dy_pair = lax.ppermute(dy_z, "core", perm=[(c, (c + 1) % n_core) for c in range(n_core)])
     my_core = lax.axis_index("core")
-    block = (src_core - my_core + n_core) % n_core
-    row_of = recv_tok + (tok_rows * (block * n_z + src_z))[:, None]
-    rows_h = recv_h.reshape(total_rows, hid_width)
-    rows_dy = dy_all[row_of.reshape(-1)]
+    other_core = (my_core + 1) % n_core
+    half = n_z * slots_per
+
+    def side(x, c):
+        x = x.reshape((n_z, n_core) + x.shape[1:])
+        return lax.dynamic_index_in_dim(x, c, axis=1, keepdims=False)
+
+    z_base = (tok_rows * jnp.arange(n_z, dtype=jnp.int32))[:, None]
+    own_rows = (side(recv_tok, my_core) + z_base).reshape(-1)
+    pair_rows = (side(recv_tok, other_core) + z_base).reshape(-1)
+    rows_dy = jnp.concatenate([dy_z[own_rows], dy_pair[pair_rows]], axis=0).reshape(total_rows, model_width)
+    rows_h = jnp.concatenate(
+        [side(recv_h, my_core).reshape(half, hid_width), side(recv_h, other_core).reshape(half, hid_width)], axis=0
+    )
+    rows_p = jnp.concatenate([side(recv_p, my_core).reshape(half), side(recv_p, other_core).reshape(half)])
     projected = lax.dot_general(
-        rows_h, w_full, (((1,), (2,)), ((), ())), preferred_element_type=jnp.float32
+        rows_h, w_full, (((1,), (1,)), ((), ())), preferred_element_type=jnp.float32
     )
-    scores = jnp.sum(projected * rows_dy.astype(jnp.float32), axis=(1, 2))
-    returned = lax.all_to_all(
-        scores.reshape(groups, slots_per), ez, split_axis=0, concat_axis=0, tiled=True
+    scores = jnp.sum(projected * rows_dy.astype(jnp.float32), axis=1)
+    own_s, pair_s = scores[:half].reshape(n_z, slots_per), scores[half:].reshape(n_z, slots_per)
+    first = jnp.where(my_core == 0, own_s, pair_s)
+    second = jnp.where(my_core == 0, pair_s, own_s)
+    in_order = jnp.stack([first, second], axis=1).reshape(groups, slots_per)
+    returned = lax.all_to_all(in_order, ez, split_axis=0, concat_axis=0, tiled=True)
+    scaled = (rows_p.reshape(total_rows, 1).astype(jnp.float32) * rows_dy.astype(jnp.float32)).astype(
+        jnp.bfloat16
     )
-    scaled = (
-        recv_p.reshape(total_rows, 1, 1).astype(jnp.float32) * rows_dy.astype(jnp.float32)
-    ).astype(jnp.bfloat16)
     partial = lax.dot_general(
         scaled, rows_h, (((0,), (0,)), ((), ())), preferred_element_type=jnp.float32
     ).astype(jnp.bfloat16)
     grad_block = lax.psum_scatter(
-        partial.reshape(model_width, hid_width), "dp", scatter_dimension=0, tiled=True
+        partial, "dp", scatter_dimension=0, tiled=True
     ).astype(jnp.float32)
     place_slot = jnp.take_along_axis(slot_place, expert_ids, axis=1)
     gate_grad = returned[expert_ids, place_slot]

time: 390 us -> 312 us (0.80)
  waiting for transfers between devices: 234 us -> 155 us
  matrix products: 28.2 us -> 45.5 us
  local copies, waits for them, and re-layouts: 60.9 us -> 50.1 us
  other arithmetic: 24 us -> 19.5 us
    all_to_all x2 -> x1, waiting for transfers between devices: 114 us -> 6.73 us  [body(): lax.all_to_all(in_order, ez, split_axis=0, concat_axis=0, tiled=True)]
    all_gather x1, waiting for transfers between devices: 98.1 us -> 31 us  [body(): dy_z = lax.all_gather(dy3, 'z', axis=0, tiled=True)]
    all_to_all x1, waiting for transfers between devices: 0.01 us -> 59.3 us  [body(): lax.all_to_all(send_h, ez, split_axis=0, concat_axis=0, tiled=True)]
    reduce_scatter x1, waiting for transfers between devices: 13.9 us -> 41.9 us  [body(): lax.psum_scatter(partial, 'dp', scatter_dimension=0, tiled=True)]
    concatenate x1 -> x0, other arithmetic: 16.7 us -> none  [body(): dy_all = jnp.concatenate([dy_z, dy_pair], axis=0)]
    convert_element_type x1 -> x2, other arithmetic: 0.03 us -> 12.2 us  [the longest x1 12.1 us: body(): rows_dy.astype(jnp.float32)]
    dot_general x1, matrix products: 14.2 us -> 23.9 us  [body(): lax.dot_general(rows_h, w_full, (((1,), (1,)), ((), ())), preferred_eleme...]
    gather x2, local copies, waits for them, and re-layouts: 24.7 us -> 16.1 us  [the longest x1 8.06 us: body(): dy_z[own_rows]]
  transfers between devices with their start and end apart: 8 -> 8, of which waited for: 6 -> 8; matrix products, arithmetic and copies ran while one was open for 24% -> 35% of each run, Pallas kernels for 0% -> 0%
where the time goes in v3:
time: 312 us; the launch traced here: 311 us
  waiting for transfers between devices  155 us (50%)
  local copies, waits for them, and re-layouts  50.1 us (16%)
  matrix products  45.5 us (15%)
  starting transfers between devices  27.4 us (9%)
  other arithmetic  19.5 us (6%)
  between operations  13.9 us (4%)
    all_to_all x1, waiting for transfers between devices, body(): lax.all_to_all(send_h, ez, split_axis=0, concat_axis=0, tiled=True)  59.3 us
    reduce_scatter x1, waiting for transfers between devices, body(): lax.psum_scatter(partial, 'dp', scatter_dimension=0, tiled=True)  41.9 us
    all_gather x1, waiting for transfers between devices, body(): dy_z = lax.all_gather(dy3, 'z', axis=0, tiled=True)  31 us
    dot_general x1, matrix products, body(): lax.dot_general(rows_h, w_full, (((1,), (1,)), ((), ())), preferred_eleme...  23.9 us
    dot_general x1, matrix products, body(): lax.dot_general(scaled, rows_h, (((0,), (0,)), ((), ())), preferred_eleme...  21.6 us
    convert_element_type x1, other arithmetic, body(): rows_dy.astype(jnp.float32)  12.1 us
    all_to_all x1, starting transfers between devices, body(): lax.all_to_all(send_p, ez, split_axis=0, concat_axis=0, tiled=True)  9.98 us
    gather x1, local copies, waits for them, and re-layouts, body(): dy_z[own_rows]  8.06 us
  transfers between devices with their start and end apart: 8, of which 8 were waited for; matrix products, arithmetic and copies ran while one was open for 35% of the time, Pallas kernels for 0%

profile of v3, /device:TPU:1, one launch (start us, length us, event | category | flops | bytes accessed | tf_op | source)
XLA Modules:
  0.0 311.0 jit_solution(13942051317143627800)
XLA Ops:
  7.2 2.5 copy.62
  9.8 0.7 convert_reduce_fusion.1
  10.5 0.1 copy.52
  10.6 0.2 reduce_window_sum.11
  10.8 1.5 convert_reduce_fusion
  12.4 0.7 multiply_add_fusion
  13.1 0.1 add.127
  13.1 0.8 copy.54
  13.9 0.1 reshape.284
  14.1 7.3 %gather_fusion.1 = bf16[1152]{0:T(1024)(128)(2,1)S(1)} fusion(bf16[1024]{0:T(1024)(128)(2,1)S(1)} %reshape.284, s32[2048]{0:T(1024)S(1)} %pad_clamp_fusion), kind=kCustom, calls=%fused_computation.1 | custom fusion | bytes 9216 | tf_op jit(solution)/shard_map/gather | solution.py:36
  21.4 0.1 reshape.285
  21.5 0.6 copy.55
  22.1 10.0 %all-to-all-start.1 = ((bf16[16,1,72]{2,1,0:T(2,128)(2,1)}), bf16[16,1,72]{2,1,0:T(2,128)(2,1)S(1)}, u32[]{:S(2)}, u32[]{:S(2)}) async-start(bf16[16,1,72]{2,1,0:T(2,128)(2,1)} %copy.55), calls=%async_computation.1 | async-start | bytes 16384 | tf_op jit(solution)/shard_map/all_to_all | solution.py:44
  32.1 4.6 %gather_fusion = bf16[1152,768]{1,0:T(8,128)(2,1)S(1)} fusion(bf16[1024,768]{1,0:T(8,128)(2,1)S(1)} %bitcast.43, s32[2048]{0:T(1024)S(1)} %pad_clamp_fusion), kind=kCustom, calls=%fused_computation | custom fusion | bytes 3543552 | tf_op jit(solution)/shard_map/gather | solution.py:32
  36.6 2.5 all-to-all-done.1
  39.1 4.8 %all-to-all-start.2 = ((s32[16,1,72]{2,1,0:T(1,128)}), s32[16,1,72]{2,1,0:T(1,128)S(1)}, u32[]{:S(2)}, u32[]{:S(2)}) async-start(s32[16,1,72]{2,1,0:T(1,128)} %bitcast.4), calls=%async_computation.2 | async-start | bytes 16384 | tf_op jit(solution)/shard_map/all_to_all | solution.py:45
  43.9 1.5 broadcast_select_fusion
  45.4 5.5 %all-to-all-done.2 = s32[16,1,72]{2,1,0:T(1,128)S(1)} async-done(((s32[16,1,72]{2,1,0:T(1,128)}), s32[16,1,72]{2,1,0:T(1,128)S(1)}, u32[]{:S(2)}, u32[]{:S(2)}) %all-to-all-start.2) | async-done | bytes 4640 | tf_op jit(solution)/shard_map/all_to_all | solution.py:45
  50.9 4.1 %all-to-all-start = ((bf16[16,72,768]{2,1,0:T(8,128)(2,1)}), bf16[16,72,768]{2,1,0:T(8,128)(2,1)S(1)}, u32[]{:S(2)}, u32[]{:S(2)}) async-start(bf16[16,72,768]{2,1,0:T(8,128)(2,1)} %broadcast_select_fusion), calls=%async_computation | async-start | bytes 3538944 | tf_op jit(solution)/shard_map/all_to_all | solution.py:43
  55.0 0.7 all-gather.5.cloned.1.call-update
  55.8 59.3 %all-to-all-done = bf16[16,72,768]{2,1,0:T(8,128)(2,1)S(1)} async-done(((bf16[16,72,768]{2,1,0:T(8,128)(2,1)}), bf16[16,72,768]{2,1,0:T(8,128)(2,1)S(1)}, u32[]{:S(2)}, u32[]{:S(2)}) %all-to-all-start) | async-done | bytes 1769504 | tf_op jit(solution)/shard_map/all_to_all | solution.py:43
  115.1 31.0 %all-gather.3.cloned.1.call-done = bf16[1024,32,128]{2,1,0:T(8,128)(2,1)} async-done(((bf16[128,32,128]{2,1,0:T(8,128)(2,1)}), bf16[1024,32,128]{2,1,0:T(8,128)(2,1)}) %all-gather.3.cloned.1.call-update) | async-done | bytes 8388624 | tf_op jit(solution)/shard_map/all_gather | solution.py:39
  146.2 0.7 collective-permute-start
  146.9 0.1 add.134
  147.3 8.1 %gather_fusion.2 = bf16[576,32,128]{2,1,0:T(8,128)(2,1)} fusion(bf16[1024,32,128]{2,1,0:T(8,128)(2,1)} %all-gather.3.cloned.1.call-done, s32[1024]{0:T(1024)S(1)} %get-tuple-element.40), kind=kCustom, calls=%fused_computation.2 | custom fusion | bytes 9439488 | tf_op jit(solution)/shard_map/gather | solution.py:60
  155.4 0.1 concatenate.20
  155.5 0.1 concatenate.21
  155.6 1.1 constant_dynamic-slice_fusion.1
  156.7 3.3 %collective-permute-done = bf16[1024,32,128]{2,1,0:T(8,128)(2,1)} collective-permute-done((bf16[1024,32,128]{2,1,0:T(8,128)(2,1)}, bf16[1024,32,128]{2,1,0:T(8,128)(2,1)}, u32[]{:S(2)}, u32[]{:S(2)}) %collective-permute-start) | collective-permute-done | bytes 8388640 | tf_op jit(solution)/shard_map/ppermute | solution.py:48
  160.0 8.0 %gather_fusion.3 = bf16[576,32,128]{2,1,0:T(8,128)(2,1)} fusion(bf16[1024,32,128]{2,1,0:T(8,128)(2,1)} %collective-permute-done, s32[1024]{0:T(1024)S(1)} %get-tuple-element.39), kind=kCustom, calls=%fused_computation.3 | custom fusion | bytes 9439488 | tf_op jit(solution)/shard_map/gather | solution.py:60
  168.0 12.1 %maximum_convert_fusion = f32[1152,32,128]{2,1,0:T(8,128)} fusion(bf16[576,32,128]{2,1,0:T(8,128)(2,1)} %gather_fusion.3, bf16[576,32,128]{2,1,0:T(8,128)(2,1)} %gather_fusion.2), kind=kLoop, calls=%fused_computation.10 | loop fusion | flops 9437184 | bytes 28311552 | tf_op jit(solution)/shard_map/convert_element_type | solution.py:74
  180.2 21.6 %fusion.4 = bf16[4096,768]{1,0:T(8,128)(2,1)} fusion(f32[144,8,32,128]{3,2,1,0:T(8,128)} %bitcast.45, f32[1152]{0:T(1024)S(1)} %maximum_convert_fusion.1, bf16[576,768]{1,0:T(8,128)(2,1)S(1)} %bitcast.53, bf16[576,768]{1,0:T(8,128)(2,1)S(1)} %bitcast.51), kind=kOutput, calls=%fused_computation.12 | convolution fusion | flops 7263879168 | bytes 26939904 | tf_op jit(solution)/shard_map/dot_general | solution.py:77
  201.8 0.7 copy-done.3
  202.5 0.1 copy.57
  202.6 0.1 reshape.331
  202.7 7.3 %gather_fusion.5 = s32[1024]{0:T(1024)S(1)} fusion(s32[128,16]{1,0:T(8,128)S(1)} %broadcast_add_fusion, s32[1024]{0:T(1024)S(1)} %reshape.331), kind=kCustom, calls=%fused_computation.5 | custom fusion | bytes 16384 | tf_op jit(solution)/shard_map/jit(take_along_axis)/gather | solution.py:83
  210.1 3.5 %all-gather.5.cloned.1.call-done = bf16[1,4096,768]{2,1,0:T(8,128)(2,1)} async-done(((bf16[1,256,768]{2,1,0:T(8,128)(2,1)}), bf16[1,4096,768]{2,1,0:T(8,128)(2,1)}) %all-gather.5.cloned.1.call-update) | async-done | bytes 6291472 | tf_op jit(solution)/shard_map/all_gather | solution.py:40
  213.6 23.9 %fusion.8 = f32[1152]{0:T(1024)S(1)} fusion(f32[144,8,32,128]{3,2,1,0:T(8,128)} %bitcast.46, bf16[1,4096,768]{2,1,0:T(8,128)(2,1)} %all-gather.5.cloned.1.call-done, bf16[576,768]{1,0:T(8,128)(2,1)S(1)} %bitcast.54, bf16[576,768]{1,0:T(8,128)(2,1)S(1)} %bitcast.52), kind=kOutput, calls=%fused_computation.14 | convolution fusion | flops 7260732416 | bytes 26939904 | tf_op jit(solution)/shard_map/dot_general | solution.py:65
  237.6 0.1 select_n.126
  237.8 0.6 pad_maximum_fusion.3
  238.4 7.7 %all-to-all-start.3 = ((f32[16,1,72]{2,1,0:T(1,128)}), f32[16,1,72]{2,1,0:T(1,128)S(1)}, u32[]{:S(2)}, u32[]{:S(2)}) async-start(f32[16,1,72]{2,1,0:T(1,128)} %bitcast.13), calls=%async_computation.4 | async-start | bytes 16384 | tf_op jit(solution)/shard_map/all_to_all | solution.py:73
  246.1 0.1 copy.59
  246.2 0.1 reshape.325
  246.3 6.7 %all-to-all-done.3 = f32[16,1,72]{2,1,0:T(1,128)S(1)} async-done(((f32[16,1,72]{2,1,0:T(1,128)}), f32[16,1,72]{2,1,0:T(1,128)S(1)}, u32[]{:S(2)}, u32[]{:S(2)}) %all-to-all-start.3) | async-done | bytes 4640 | tf_op jit(solution)/shard_map/all_to_all | solution.py:73
  253.0 6.8 %gather_fusion.4 = f32[1024]{0:T(1024)S(1)} fusion(f32[16,72]{1,0:T(8,128)S(1)} %bitcast.44, s32[1024]{0:T(1024)S(1)} %reshape.325), kind=kCustom, calls=%fused_computation.4 | custom fusion | bytes 16384 | tf_op jit(solution)/shard_map/gather | solution.py:84
  259.9 0.7 copy.60
  260.6 41.9 %reduce-scatter.2.cloned.1.call-done = bf16[256,768]{1,0:T(8,128)(2,1)} async-done(((bf16[4096,768]{1,0:T(8,128)(2,1)}), bf16[256,768]{1,0:T(8,128)(2,1)}) %reduce-scatter.2.cloned.1.call-update) | async-done | bytes 393232 | tf_op jit(solution)/shard_map/reduce_scatter | solution.py:80
  302.5 1.9 bitcast_convert_fusion
  (35 shorter events, 1.1 us)
Async XLA Ops:
  7.2 24.9 %copy-start = (bf16[128,8,768]{2,1,0:T(8,128)(2,1)S(1)}, bf16[128,8,768]{2,1,0:T(8,128)(2,1)}, u32[]{:S(2)}) copy-start(bf16[128,8,768]{2,1,0:T(8,128)(2,1)} %param.5) | copy-start | bytes 4718596
  7.2 139.0 %all-gather.3.cloned.1.call-start = ((), (), s32[]{:S(2)}) async-start(), calls=%async_computation.5 | async-start | bytes 9437184 | tf_op jit(solution)/shard_map/all_gather | solution.py:39
  22.1 17.0 %all-to-all-start.1 = ((bf16[16,1,72]{2,1,0:T(2,128)(2,1)}), bf16[16,1,72]{2,1,0:T(2,128)(2,1)S(1)}, u32[]{:S(2)}, u32[]{:S(2)}) async-start(bf16[16,1,72]{2,1,0:T(2,128)(2,1)} %copy.55), calls=%async_computation.1 | async-start | bytes 16384 | tf_op jit(solution)/shard_map/all_to_all | solution.py:44
  39.1 11.8 %all-to-all-start.2 = ((s32[16,1,72]{2,1,0:T(1,128)}), s32[16,1,72]{2,1,0:T(1,128)S(1)}, u32[]{:S(2)}, u32[]{:S(2)}) async-start(s32[16,1,72]{2,1,0:T(1,128)} %bitcast.4), calls=%async_computation.2 | async-start | bytes 16384 | tf_op jit(solution)/shard_map/all_to_all | solution.py:45
  50.9 64.2 %all-to-all-start = ((bf16[16,72,768]{2,1,0:T(8,128)(2,1)}), bf16[16,72,768]{2,1,0:T(8,128)(2,1)S(1)}, u32[]{:S(2)}, u32[]{:S(2)}) async-start(bf16[16,72,768]{2,1,0:T(8,128)(2,1)} %broadcast_select_fusion), calls=%async_computation | async-start | bytes 3538944 | tf_op jit(solution)/shard_map/all_to_all | solution.py:43
  55.0 158.6 %all-gather.5.cloned.1.call-start = ((), (), s32[]{:S(2)}) async-start(), calls=%async_computation.7 | async-start | bytes 6684672 | tf_op jit(solution)/shard_map/all_gather | solution.py:40
  55.8 246.7 %reduce-scatter.2.cloned.1.call-start = ((), (), s32[]{:S(2)}) async-start(), calls=%async_computation.6 | async-start | bytes 6684672 | tf_op jit(solution)/shard_map/reduce_scatter | solution.py:80
  146.2 13.8 %collective-permute-start = (bf16[1024,32,128]{2,1,0:T(8,128)(2,1)}, bf16[1024,32,128]{2,1,0:T(8,128)(2,1)}, u32[]{:S(2)}, u32[]{:S(2)}) collective-permute-start(bf16[1024,32,128]{2,1,0:T(8,128)(2,1)} %all-gather.3.cloned.1.call-done), channel_id=1, source_target_pairs={{0,1},{1,0},{2,3},{3,2},{4,5},{5,4},{6,7},{7,6},{8,9},{9,8},{10,11... | collective-permute-start | bytes 25165832 | tf_op jit(solution)/shard_map/ppermute | solution.py:48
  168.0 12.2 %copy-start.2 = (bf16[8,1,72,768]{3,2,1,0:T(8,128)(2,1)S(1)}, bf16[8,1,72,768]{3,2,1,0:T(8,128)(2,1)}, u32[]{:S(2)}) copy-start(bf16[8,1,72,768]{3,2,1,0:T(8,128)(2,1)} %get-tuple-element.36) | copy-start | bytes 2654212
  201.8 0.7 copy-start.3
  238.4 14.6 %all-to-all-start.3 = ((f32[16,1,72]{2,1,0:T(1,128)}), f32[16,1,72]{2,1,0:T(1,128)S(1)}, u32[]{:S(2)}, u32[]{:S(2)}) async-start(f32[16,1,72]{2,1,0:T(1,128)} %bitcast.13), calls=%async_computation.4 | async-start | bytes 16384 | tf_op jit(solution)/shard_map/all_to_all | solution.py:73
  253.0 51.4 %copy-start.1 = (bf16[128,8,768]{2,1,0:T(8,128)(2,1)S(1)}, bf16[128,8,768]{2,1,0:T(8,128)(2,1)}, u32[]{:S(2)}) copy-start(bf16[128,8,768]{2,1,0:T(8,128)(2,1)} %param.5) | copy-start | bytes 4718596
Sparse Core Ops, SparseCore 0:
  9.9 136.1 all-gather.2
  148.6 64.9 all-gather.4
  217.4 85.0 reduce-scatter.1

commit v4 on v2

v4 whole, which is shorter than its diff:
```python
import jax
import jax.numpy as jnp
from jax import lax
from jax.sharding import Mesh, PartitionSpec as P


def body(hidden, upstream, probs, expert_ids, w_down):
    tok_rows, top_k = expert_ids.shape
    hid_width = hidden.shape[2]
    model_width = upstream.shape[1]
    n_z = lax.axis_size("z")
    n_core = lax.axis_size("core")
    n_dp = lax.axis_size("dp")
    groups = n_z * n_core
    slots_per = max(tok_rows * 9 // 16, tok_rows * top_k // groups)
    total_rows = groups * slots_per
    ez = ("z", "core")

    chosen = (expert_ids[:, :, None] == jnp.arange(groups, dtype=jnp.int32)[None, None, :]).astype(
        jnp.int32
    )
    member = jnp.sum(chosen, axis=1)
    slot_place = jnp.cumsum(member, axis=0) - 1
    which_k = jnp.sum(chosen * jnp.arange(top_k, dtype=jnp.int32)[None, :, None], axis=1)
    target = (
        (member == 1)[:, :, None]
        & (slot_place[:, :, None] == jnp.arange(slots_per, dtype=jnp.int32)[None, None, :])
    ).astype(jnp.int32)
    filled = jnp.sum(target, axis=0) == 1
    source_tok = jnp.sum(target * jnp.arange(tok_rows, dtype=jnp.int32)[:, None, None], axis=0)
    source_k = jnp.sum(target * which_k[:, :, None], axis=0)
    flat_index = (source_tok * top_k + source_k).reshape(-1)
    picked_h = hidden.reshape(tok_rows * top_k, hid_width)[flat_index].reshape(
        groups, slots_per, hid_width
    )
    send_h = jnp.where(filled[:, :, None], picked_h, jnp.zeros_like(picked_h))
    routed = member == 1
    p_tok = jnp.where(
        routed, jnp.take_along_axis(probs, which_k, axis=1).astype(jnp.float32), jnp.float32(0.0)
    )
    inv = jnp.where(routed, slot_place, -1).astype(jnp.float32)
    send_meta = jnp.stack([p_tok.T, inv.T], axis=1)

    dy_z = lax.all_gather(upstream, "z", axis=0, tiled=True)
    w_blocks = lax.all_to_all(
        jnp.broadcast_to(w_down, (n_dp,) + w_down.shape[1:]), "dp", split_axis=0, concat_axis=0, tiled=True
    )
    w_full = w_blocks.reshape(n_dp * w_down.shape[1], hid_width)
    dy_z, w_full, send_h, send_meta = lax.optimization_barrier((dy_z, w_full, send_h, send_meta))
    dy_pair = lax.ppermute(dy_z, "core", perm=[(c, (c + 1) % n_core) for c in range(n_core)])
    recv_h = lax.all_to_all(send_h, ez, split_axis=0, concat_axis=0, tiled=True)
    recv_meta = lax.all_to_all(send_meta, ez, split_axis=0, concat_axis=0, tiled=True)

    my_core = lax.axis_index("core")
    flat_h = recv_h.reshape(total_rows, hid_width)

    def half(dy_c, c):
        meta = lax.dynamic_index_in_dim(
            recv_meta.reshape(n_z, n_core, 2, tok_rows), c, axis=1, keepdims=False
        )
        p_c = meta[:, 0, :].reshape(-1)
        slot = meta[:, 1, :].astype(jnp.int32)
        live = (slot >= 0).reshape(-1)
        src = (jnp.arange(n_z, dtype=jnp.int32) * n_core + c)[:, None]
        row = (src * slots_per + jnp.maximum(slot, 0)).reshape(-1)
        h_c = jnp.where(live[:, None], flat_h[row], jnp.zeros((), flat_h.dtype))
        scaled = (p_c[:, None] * dy_c.astype(jnp.float32)).astype(jnp.bfloat16)
        part = lax.dot_general(
            scaled, h_c, (((0,), (0,)), ((), ())), preferred_element_type=jnp.float32
        )
        g = lax.dot_general(dy_c, w_full, (((1,), (0,)), ((), ())), preferred_element_type=jnp.float32)
        score = jnp.sum(g * h_c.astype(jnp.float32), axis=1)
        return part, score.reshape(n_z, tok_rows)

    part_own, score_own = half(dy_z, my_core)
    part_pair, score_pair = half(dy_pair, (my_core + 1) % n_core)
    partial = (part_own + part_pair).astype(jnp.bfloat16)
    grad_block = lax.psum_scatter(partial, "dp", scatter_dimension=0, tiled=True).astype(jnp.float32)

    first = jnp.where(my_core == 0, score_own, score_pair)
    second = jnp.where(my_core == 0, score_pair, score_own)
    by_source = jnp.stack([first, second], axis=1).reshape(groups, tok_rows)
    returned = lax.all_to_all(by_source, ez, split_axis=0, concat_axis=0, tiled=True)
    gate_grad = jnp.take_along_axis(returned.T, expert_ids, axis=1)
    return (grad_block[None], gate_grad)


def solution(mesh):
    n_dp, n_expert = mesh.devices.shape
    sub = Mesh(mesh.devices.reshape(n_dp, n_expert // 2, 2), ("dp", "z", "core"))
    tok = ("dp", "z", "core")
    in_specs = (
        P(tok, None, None),
        P(tok, None),
        P(tok, None),
        P(tok, None),
        P(("z", "core"), "dp", None),
    )
    out_specs = (P(("z", "core"), "dp", None), P(tok, None))
    return jax.shard_map(body, mesh=sub, in_specs=in_specs, out_specs=out_specs, check_vma=False)
```

time: 390 us -> 328 us (0.84)
  waiting for transfers between devices: 234 us -> 171 us
  matrix products: 28.2 us -> 51.7 us
  other arithmetic: 24 us -> 5.86 us
  blocking collectives: 0 us -> 15.7 us
  local copies, waits for them, and re-layouts: 60.9 us -> 48.1 us
  starting transfers between devices: 27.8 us -> 20.4 us
    all_gather x1, waiting for transfers between devices: 98.1 us -> 0.01 us  [body(): dy_z = lax.all_gather(upstream, 'z', axis=0, tiled=True)]
    all_to_all x4 -> x2, waiting for transfers between devices: 14.7 us -> 48.7 us  [the longest x1 42 us: body(): recv_h = lax.all_to_all(send_h, ez, split_axis=0, concat_axis=0, tiled=True)]
    reduce_scatter x1, waiting for transfers between devices: 13.9 us -> 45.1 us  [body(): lax.psum_scatter(partial, 'dp', scatter_dimension=0, tiled=True)]
    all_to_all x1, waiting for transfers between devices: 107 us -> 76.5 us  [body(): lax.all_to_all(jnp.broadcast_to(w_down, (n_dp,) + w_down.shape[1:]), 'dp'...]
    dot_general x2 -> x4, matrix products: 28.2 us -> 51.7 us  [the longest x2 28.6 us: half(): lax.dot_general(scaled, h_c, (((0,), (0,)), ((), ())), preferred_element_...]
    concatenate x2 -> x0, other arithmetic: 16.7 us -> none  [the longest x1 16.7 us: body(): dy_all = jnp.concatenate([dy_z, dy_pair], axis=0)]
    all_to_all x0 -> x1, blocking collectives: none -> 15.7 us  [body(): lax.all_to_all(send_meta, ez, split_axis=0, concat_axis=0, tiled=True)]
    all_to_all x4 -> x2, starting transfers between devices: 20.5 us -> 10.1 us  [the longest x1 5.89 us: body(): recv_h = lax.all_to_all(send_h, ez, split_axis=0, concat_axis=0, tiled=True)]
  transfers between devices with their start and end apart: 8 -> 6, of which waited for: 6 -> 4; matrix products, arithmetic and copies ran while one was open for 24% -> 27% of each run, Pallas kernels for 0% -> 0%
where the time goes in v4:
time: 328 us; the launch traced here: 327 us
  waiting for transfers between devices  171 us (52%)
  matrix products  51.7 us (16%)
  local copies, waits for them, and re-layouts  48.1 us (15%)
  starting transfers between devices  20.4 us (6%)
  blocking collectives  15.7 us (5%)
  between operations  14.3 us (4%)
  other arithmetic  5.86 us (2%)
    all_to_all x1, waiting for transfers between devices, body(): lax.all_to_all(jnp.broadcast_to(w_down, (n_dp,) + w_down.shape[1:]), 'dp'...  76.5 us
    reduce_scatter x1, waiting for transfers between devices, body(): lax.psum_scatter(partial, 'dp', scatter_dimension=0, tiled=True)  45.1 us
    all_to_all x1, waiting for transfers between devices, body(): recv_h = lax.all_to_all(send_h, ez, split_axis=0, concat_axis=0, tiled=True)  42 us
    dot_general x2, matrix products, half(): lax.dot_general(scaled, h_c, (((0,), (0,)), ((), ())), preferred_element_...  28.6 us
    dot_general x2, matrix products, half(): lax.dot_general(dy_c, w_full, (((1,), (0,)), ((), ())), preferred_element...  23.1 us
    gather x5, local copies, waits for them, and re-layouts, body(): jnp.take_along_axis(probs, which_k, axis=1).astype(jnp.float32)  16.2 us
    all_to_all x1, blocking collectives, body(): lax.all_to_all(send_meta, ez, split_axis=0, concat_axis=0, tiled=True)  15.7 us
    gather x4, local copies, waits for them, and re-layouts, half(): h_c = jnp.where(live[:, None], flat_h[row], jnp.zeros((), flat_h.dtype))  14.8 us
  transfers between devices with their start and end apart: 6, of which 4 were waited for; matrix products, arithmetic and copies ran while one was open for 27% of the time, Pallas kernels for 0%

profile of v4, /device:TPU:1, one launch (start us, length us, event | category | flops | bytes accessed | tf_op | source)
XLA Modules:
  0.0 327.2 jit_solution(8815958235554985957)
XLA Ops:
  7.2 0.0 copy-start
  7.2 0.0 all-gather.2.cloned.1.call-start
  7.2 0.7 all-gather.2.cloned.1.call-update
  7.9 4.3 %broadcast_in_dim.71 = bf16[16,256,768]{2,1,0:T(8,128)(2,1)} broadcast(bf16[256,768]{1,0:T(8,128)(2,1)} %bitcast.69), dimensions={1,2} | broadcast | bytes 6684672 | tf_op jit(solution)/shard_map/broadcast_in_dim | solution.py:46
  12.2 7.8 %all-to-all-start = ((bf16[16,256,768]{2,1,0:T(8,128)(2,1)}), bf16[16,256,768]{2,1,0:T(8,128)(2,1)}, u32[]{:S(2)}, u32[]{:S(2)}) async-start(bf16[16,256,768]{2,1,0:T(8,128)(2,1)} %broadcast_in_dim.71), calls=%async_computation | async-start | bytes 12582912 | tf_op jit(solution)/shard_map/all_to_all | solution.py:45
  20.0 0.0 copy-done.4
  20.0 0.0 copy-start.1
  20.0 0.1 copy.53
  20.1 0.1 reshape.274
  20.2 0.5 copy-done.1
  20.6 15.9 %gather_fusion.3 = bf16[2048]{0:T(1024)(128)(2,1)S(1)} fusion(bf16[128,8]{0,1:T(8,128)(2,1)S(1)} %copy-done.1, s32[2048]{0:T(1024)S(1)} %reshape.274), kind=kCustom, calls=%fused_computation.3 | custom fusion | bytes 24576 | tf_op jit(solution)/shard_map/jit(take_along_axis)/gather | solution.py:39
  36.6 0.1 reshape.277
  36.7 0.1 copy.54
  36.7 0.1 copy.51
  36.8 0.2 reduce_window_sum.11
  37.0 0.1 copy.52
  37.1 0.9 convert_reduce_fusion
  38.0 0.1 add.160
  38.2 4.6 %gather_fusion = bf16[1152,768]{1,0:T(8,128)(2,1)S(1)} fusion(bf16[1024,768]{1,0:T(8,128)(2,1)S(1)} %bitcast.64, s32[2048]{0:T(1024)S(1)} %pad_clamp_fusion), kind=kCustom, calls=%fused_computation | custom fusion | bytes 3543552 | tf_op jit(solution)/shard_map/gather | solution.py:33
  42.8 1.4 broadcast_select_fusion
  44.2 76.5 %all-to-all-done = bf16[16,256,768]{2,1,0:T(8,128)(2,1)} async-done(((bf16[16,256,768]{2,1,0:T(8,128)(2,1)}), bf16[16,256,768]{2,1,0:T(8,128)(2,1)}, u32[]{:S(2)}, u32[]{:S(2)}) %all-to-all-start) | async-done | bytes 6291488 | tf_op jit(solution)/shard_map/all_to_all | solution.py:45
  120.8 2.5 collective-permute-start
  123.2 15.7 %all_to_all.27 = f32[16,2,128]{2,1,0:T(2,128)S(1)} all-to-all(f32[16,2,128]{2,1,0:T(2,128)S(1)} %copy.55), channel_id=1, replica_groups=mesh['dp'=16,'z'=8,'core'=2] {'z','core'}, dimensions={0} | all-to-all | bytes 32768 | tf_op jit(solution)/shard_map/all_to_all | solution.py:52
  139.0 5.9 %all-to-all-start.2 = ((bf16[16,72,768]{2,1,0:T(8,128)(2,1)}), bf16[16,72,768]{2,1,0:T(8,128)(2,1)S(1)}, u32[]{:S(2)}, u32[]{:S(2)}) async-start(bf16[16,72,768]{2,1,0:T(8,128)(2,1)} %broadcast_select_fusion), calls=%async_computation.2 | async-start | bytes 3538944 | tf_op jit(solution)/shard_map/all_to_all | solution.py:51
  144.8 0.0 reduce-scatter.2.cloned.1.call-start
  145.0 0.1 add.170
  145.1 0.1 add.179
  145.2 42.0 %all-to-all-done.2 = bf16[16,72,768]{2,1,0:T(8,128)(2,1)S(1)} async-done(((bf16[16,72,768]{2,1,0:T(8,128)(2,1)}), bf16[16,72,768]{2,1,0:T(8,128)(2,1)S(1)}, u32[]{:S(2)}, u32[]{:S(2)}) %all-to-all-start.2) | async-done | bytes 1769504 | tf_op jit(solution)/shard_map/all_to_all | solution.py:51
  187.2 5.2 %gather_fusion.2 = bf16[1024,768]{1,0:T(8,128)(2,1)} fusion(bf16[1152,768]{1,0:T(8,128)(2,1)S(1)} %bitcast.66, s32[1024]{0:T(1024)S(1)} %broadcast_clamp_fusion), kind=kCustom, calls=%fused_computation.2 | custom fusion | bytes 3149824 | tf_op jit(solution)/shard_map/gather | solution.py:66
  192.4 5.2 %gather_fusion.1 = bf16[1024,768]{1,0:T(8,128)(2,1)} fusion(bf16[1152,768]{1,0:T(8,128)(2,1)S(1)} %bitcast.67, s32[1024]{0:T(1024)S(1)} %broadcast_clamp_fusion.1), kind=kCustom, calls=%fused_computation.1 | custom fusion | bytes 3149824 | tf_op jit(solution)/shard_map/gather | solution.py:66
  197.7 2.7 copy.57
  200.4 1.6 copy.58
  202.0 13.1 %fusion = f32[4096,768]{1,0:T(8,128)} fusion(bf16[1024,4096]{1,0:T(8,128)(2,1)} %all-gather.2.cloned.1.call-done, f32[1024]{0:T(1024)S(1)} %slice_bitcast_fusion.1, bf16[1024,768]{0,1:T(8,128)(2,1)} %copy.57, pred[1024]{0:T(1024)(128)(4,1)S(1)} %compare_bitcast_fusion.1), kind=kOutput, calls=%fused_computation.8 | convolution fusion | flops 6455820288 | bytes 22549504 | tf_op jit(solution)/shard_map/dot_general | solution.py:68
  215.1 0.0 collective-permute-done
  215.1 15.5 %add_convert_fusion = bf16[4096,768]{1,0:T(8,128)(2,1)} fusion(f32[4096,768]{1,0:T(8,128)} %fusion, bf16[1024,4096]{1,0:T(8,128)(2,1)} %collective-permute-done, f32[1024]{0:T(1024)S(1)} %slice_bitcast_fusion, bf16[1024,768]{0,1:T(8,128)(2,1)S(1)} %copy-done.3, pred[1024]{0:T(1024)(128)(4,1)S(1)} %compare_bitcast_fusion), kind=kOutput, calls=%fused_computation.7 | convolution fusion | flops 6462111744 | bytes 28840960 | tf_op jit(solution)/shard_map/dot_general | solution.py:68
  230.6 0.0 reduce-scatter.2.cloned.1.call-update
  230.7 11.5 %multiply_reduce_fusion.1 = f32[1024]{0:T(1024)S(1)} fusion(bf16[1024,4096]{1,0:T(8,128)(2,1)} %all-gather.2.cloned.1.call-done, bf16[4096,768]{1,0:T(8,128)(2,1)} %bitcast.1, bf16[1024,768]{0,1:T(8,128)(2,1)} %copy.57, pred[1024]{0:T(1024)(128)(4,1)S(1)} %compare_bitcast_fusion.1), kind=kOutput, calls=%fused_computation.13 | convolution fusion | flops 6445595648 | bytes 16258048 | tf_op jit(solution)/shard_map/dot_general | solution.py:71
  242.2 11.6 %multiply_reduce_fusion = f32[1024]{0:T(1024)S(1)} fusion(bf16[1024,4096]{1,0:T(8,128)(2,1)} %collective-permute-done, bf16[4096,768]{1,0:T(8,128)(2,1)} %bitcast.1, bf16[1024,768]{0,1:T(8,128)(2,1)S(1)} %copy-done.3, pred[1024]{0:T(1024)(128)(4,1)S(1)} %compare_bitcast_fusion), kind=kOutput, calls=%fused_computation.12 | convolution fusion | flops 6445595648 | bytes 16258048 | tf_op jit(solution)/shard_map/dot_general | solution.py:71
  253.8 0.6 pad_maximum_fusion.1
  254.4 4.2 %all-to-all-start.3 = ((f32[16,1,128]{2,1,0:T(1,128)}), f32[16,1,128]{2,1,0:T(1,128)S(1)}, u32[]{:S(2)}, u32[]{:S(2)}) async-start(f32[16,1,128]{2,1,0:T(1,128)} %bitcast.28), calls=%async_computation.4 | async-start | bytes 16384 | tf_op jit(solution)/shard_map/all_to_all | solution.py:83
  258.6 0.1 copy.59
  258.7 0.1 reshape.280
  258.8 6.7 %all-to-all-done.3 = f32[16,1,128]{2,1,0:T(1,128)S(1)} async-done(((f32[16,1,128]{2,1,0:T(1,128)}), f32[16,1,128]{2,1,0:T(1,128)S(1)}, u32[]{:S(2)}, u32[]{:S(2)}) %all-to-all-start.3) | async-done | bytes 8224 | tf_op jit(solution)/shard_map/all_to_all | solution.py:83
  265.6 7.0 %gather_fusion.4 = f32[1024]{0:T(1024)S(1)} fusion(f32[128,16]{0,1:T(8,128)S(1)} %bitcast.65, s32[1024]{0:T(1024)S(1)} %reshape.280), kind=kCustom, calls=%fused_computation.4 | custom fusion | bytes 16384 | tf_op jit(solution)/shard_map/jit(take_along_axis)/gather | solution.py:84
  272.6 0.1 reshape.283
  272.7 0.6 and_select_fusion.1
  273.3 45.1 %reduce-scatter.2.cloned.1.call-done = bf16[256,768]{1,0:T(8,128)(2,1)} async-done(((bf16[4096,768]{1,0:T(8,128)(2,1)}), bf16[256,768]{1,0:T(8,128)(2,1)}) %reduce-scatter.2.cloned.1.call-update) | async-done | bytes 393232 | tf_op jit(solution)/shard_map/reduce_scatter | solution.py:78
  318.5 1.9 bitcast_convert_fusion
  (35 shorter events, 0.3 us)
Async XLA Ops:
  7.2 31.0 %copy-start = (bf16[128,8,768]{2,1,0:T(8,128)(2,1)S(1)}, bf16[128,8,768]{2,1,0:T(8,128)(2,1)}, u32[]{:S(2)}) copy-start(bf16[128,8,768]{2,1,0:T(8,128)(2,1)} %param.5) | copy-start | bytes 4718596
  7.2 113.6 %all-gather.2.cloned.1.call-start = ((), (), s32[]{:S(2)}) async-start(), calls=%async_computation.5 | async-start | bytes 9437184 | tf_op jit(solution)/shard_map/all_gather | solution.py:44
  12.2 7.8 %copy-start.4 = (s32[128,8]{0,1:T(8,128)S(1)}, s32[128,8]{0,1:T(8,128)}, u32[]{:S(2)}) copy-start(s32[128,8]{0,1:T(8,128)} %param.8) | copy-start | bytes 12292
  12.2 108.6 %all-to-all-start = ((bf16[16,256,768]{2,1,0:T(8,128)(2,1)}), bf16[16,256,768]{2,1,0:T(8,128)(2,1)}, u32[]{:S(2)}, u32[]{:S(2)}) async-start(bf16[16,256,768]{2,1,0:T(8,128)(2,1)} %broadcast_in_dim.71), calls=%async_computation | async-start | bytes 12582912 | tf_op jit(solution)/shard_map/all_to_all | solution.py:45
  20.0 0.7 copy-start.1
  120.8 94.3 %collective-permute-start = (bf16[1024,4096]{1,0:T(8,128)(2,1)}, bf16[1024,4096]{1,0:T(8,128)(2,1)}, u32[]{:S(2)}, u32[]{:S(2)}) collective-permute-start(bf16[1024,4096]{1,0:T(8,128)(2,1)} %all-gather.2.cloned.1.call-done), channel_id=1, source_target_pairs={{0,1},{1,0},{2,3},{3,2},{4,5},{5,4},{6,7},{7,6},{8,9},{9,8},{10,11... | collective-permute-start | bytes 25165832 | tf_op jit(solution)/shard_map/ppermute | solution.py:50
  139.0 48.3 %all-to-all-start.2 = ((bf16[16,72,768]{2,1,0:T(8,128)(2,1)}), bf16[16,72,768]{2,1,0:T(8,128)(2,1)S(1)}, u32[]{:S(2)}, u32[]{:S(2)}) async-start(bf16[16,72,768]{2,1,0:T(8,128)(2,1)} %broadcast_select_fusion), calls=%async_computation.2 | async-start | bytes 3538944 | tf_op jit(solution)/shard_map/all_to_all | solution.py:51
  144.8 173.6 %reduce-scatter.2.cloned.1.call-start = ((), (), s32[]{:S(2)}) async-start(), calls=%async_computation.6 | async-start | bytes 6684672 | tf_op jit(solution)/shard_map/reduce_scatter | solution.py:78
  197.7 2.7 copy-start.2
  202.0 13.1 %copy-start.3 = (bf16[1024,768]{0,1:T(8,128)(2,1)S(1)}, bf16[1024,768]{0,1:T(8,128)(2,1)}, u32[]{:S(2)}) copy-start(bf16[1024,768]{0,1:T(8,128)(2,1)} %copy.58) | copy-start | bytes 4718596
  254.4 11.2 %all-to-all-start.3 = ((f32[16,1,128]{2,1,0:T(1,128)}), f32[16,1,128]{2,1,0:T(1,128)S(1)}, u32[]{:S(2)}, u32[]{:S(2)}) async-start(f32[16,1,128]{2,1,0:T(1,128)} %bitcast.28), calls=%async_computation.4 | async-start | bytes 16384 | tf_op jit(solution)/shard_map/all_to_all | solution.py:83
Sparse Core Ops, SparseCore 0:
  9.8 97.9 all-gather.1
  230.8 87.6 reduce-scatter.1

commit v5 on v4

--- a/solution.py
+++ b/solution.py
@@ -41,15 +41,12 @@
     inv = jnp.where(routed, slot_place, -1).astype(jnp.float32)
     send_meta = jnp.stack([p_tok.T, inv.T], axis=1)
 
-    dy_z = lax.all_gather(upstream, "z", axis=0, tiled=True)
-    w_blocks = lax.all_to_all(
-        jnp.broadcast_to(w_down, (n_dp,) + w_down.shape[1:]), "dp", split_axis=0, concat_axis=0, tiled=True
-    )
-    w_full = w_blocks.reshape(n_dp * w_down.shape[1], hid_width)
-    dy_z, w_full, send_h, send_meta = lax.optimization_barrier((dy_z, w_full, send_h, send_meta))
-    dy_pair = lax.ppermute(dy_z, "core", perm=[(c, (c + 1) % n_core) for c in range(n_core)])
+    w_full = lax.all_gather(w_down, "dp", axis=1, tiled=True)[0]
     recv_h = lax.all_to_all(send_h, ez, split_axis=0, concat_axis=0, tiled=True)
     recv_meta = lax.all_to_all(send_meta, ez, split_axis=0, concat_axis=0, tiled=True)
+    upstream, w_full, recv_h, recv_meta = lax.optimization_barrier((upstream, w_full, recv_h, recv_meta))
+    dy_z = lax.all_gather(upstream, "z", axis=0, tiled=True)
+    dy_pair = lax.ppermute(dy_z, "core", perm=[(c, (c + 1) % n_core) for c in range(n_core)])
 
     my_core = lax.axis_index("core")
     flat_h = recv_h.reshape(total_rows, hid_width)

time: 328 us -> 322 us (0.982)
  blocking collectives: 15.7 us -> 51 us
  waiting for transfers between devices: 171 us -> 139 us
  starting transfers between devices: 20.4 us -> 15.5 us
  local copies, waits for them, and re-layouts: 48.1 us -> 44.2 us
    all_to_all x2 -> x1, waiting for transfers between devices: 119 us -> 0.21 us  [body(): lax.all_to_all(send_meta, ez, split_axis=0, concat_axis=0, tiled=True)]
    all_gather x1, waiting for transfers between devices: 0.01 us -> 91 us  [body(): dy_z = lax.all_gather(upstream, 'z', axis=0, tiled=True)]
    all_to_all x1, blocking collectives: 15.7 us -> 51 us  [body(): recv_h = lax.all_to_all(send_h, ez, split_axis=0, concat_axis=0, tiled=True)]
    reduce_scatter x1, waiting for transfers between devices: 45.1 us -> 40.6 us  [body(): lax.psum_scatter(partial, 'dp', scatter_dimension=0, tiled=True)]
    broadcast_in_dim x1 -> x0, local copies, waits for them, and re-layouts: 4.27 us -> none  [body(): jnp.broadcast_to(w_down, (n_dp,) + w_down.shape[1:])]
    all_to_all x2 -> x1, starting transfers between devices: 13.6 us -> 9.98 us  [body(): lax.all_to_all(send_meta, ez, split_axis=0, concat_axis=0, tiled=True)]
  transfers between devices with their start and end apart: 6 -> 6, of which waited for: 4 -> 4; matrix products, arithmetic and copies ran while one was open for 27% -> 26% of each run, Pallas kernels for 0% -> 0%
where the time goes in v5:
time: 322 us
  waiting for transfers between devices  139 us (43%)
  matrix products  51.5 us (16%)
  blocking collectives  51 us (16%)
  local copies, waits for them, and re-layouts  44.2 us (14%)
  starting transfers between devices  15.5 us (5%)
  between operations  14 us (4%)
  other arithmetic  6.52 us (2%)
    all_gather x1, waiting for transfers between devices, body(): dy_z = lax.all_gather(upstream, 'z', axis=0, tiled=True)  91 us
    all_to_all x1, blocking collectives, body(): recv_h = lax.all_to_all(send_h, ez, split_axis=0, concat_axis=0, tiled=True)  51 us
    reduce_scatter x1, waiting for transfers between devices, body(): lax.psum_scatter(partial, 'dp', scatter_dimension=0, tiled=True)  40.6 us
    dot_general x2, matrix products, half(): lax.dot_general(scaled, h_c, (((0,), (0,)), ((), ())), preferred_element_...  28.6 us
    dot_general x2, matrix products, half(): lax.dot_general(dy_c, w_full, (((1,), (0,)), ((), ())), preferred_element...  22.9 us
    gather x5, local copies, waits for them, and re-layouts, body(): jnp.take_along_axis(probs, which_k, axis=1).astype(jnp.float32)  16.3 us
    gather x4, local copies, waits for them, and re-layouts, half(): h_c = jnp.where(live[:, None], flat_h[row], jnp.zeros((), flat_h.dtype))  14.9 us
    all_to_all x1, starting transfers between devices, body(): lax.all_to_all(send_meta, ez, split_axis=0, concat_axis=0, tiled=True)  9.98 us
  transfers between devices with their start and end apart: 6, of which 4 were waited for; matrix products, arithmetic and copies ran while one was open for 26% of the time, Pallas kernels for 0%

profile of v5, /device:TPU:1, one launch (start us, length us, event | category | flops | bytes accessed | tf_op | source)
XLA Modules:
  0.0 321.9 jit_solution(2423771773382165408)
XLA Ops:
  7.2 0.0 copy-start
  7.2 0.0 all-gather.3.cloned.1.call-start
  7.2 0.7 all-gather.3.cloned.1.call-update
  7.9 0.7 convert_reduce_fusion.1
  8.6 0.1 copy.51
  8.7 0.1 reshape.270
  8.8 15.9 %gather_fusion.3 = bf16[2048]{0:T(1024)(128)(2,1)S(1)} fusion(bf16[128,8]{0,1:T(8,128)(2,1)S(1)} %copy-done.1, s32[2048]{0:T(1024)S(1)} %reshape.270), kind=kCustom, calls=%fused_computation.3 | custom fusion | bytes 24576 | tf_op jit(solution)/shard_map/jit(take_along_axis)/gather | solution.py:39
  24.8 0.1 reshape.273
  24.9 0.1 copy.52
  24.9 0.1 copy.49
  25.0 0.2 reduce_window_sum.11
  25.2 0.1 copy.50
  25.3 0.6 copy.53
  25.9 10.0 %all-to-all-start.1 = ((f32[16,2,128]{2,1,0:T(2,128)}), f32[16,2,128]{2,1,0:T(2,128)S(1)}, u32[]{:S(2)}, u32[]{:S(2)}) async-start(f32[16,2,128]{2,1,0:T(2,128)} %copy.53), calls=%async_computation.1 | async-start | bytes 32768 | tf_op jit(solution)/shard_map/all_to_all | solution.py:46
  35.9 0.0 all-gather.5.cloned.1.call-start
  36.0 0.9 convert_reduce_fusion
  36.9 0.1 add.160
  37.0 4.6 %gather_fusion = bf16[1152,768]{1,0:T(8,128)(2,1)S(1)} fusion(bf16[1024,768]{1,0:T(8,128)(2,1)S(1)} %bitcast.63, s32[2048]{0:T(1024)S(1)} %pad_clamp_fusion), kind=kCustom, calls=%fused_computation | custom fusion | bytes 3543552 | tf_op jit(solution)/shard_map/gather | solution.py:33
  41.6 1.4 broadcast_select_fusion
  43.0 0.2 all-to-all-done.1
  43.3 51.0 %all_to_all.22 = bf16[16,72,768]{2,1,0:T(8,128)(2,1)S(1)} all-to-all(bf16[16,72,768]{2,1,0:T(8,128)(2,1)} %broadcast_select_fusion), channel_id=1, replica_groups=mesh['dp'=16,'z'=8,'core'=2] {'z','core'}, dimensions={0} | all-to-all | bytes 3538944 | tf_op jit(solution)/shard_map/all_to_all | solution.py:45
  94.3 0.0 all-gather.5.cloned.1.call-update
  94.3 0.0 reduce-scatter.2.cloned.1.call-start
  94.3 91.0 %all-gather.5.cloned.1.call-done = bf16[1024,4096]{1,0:T(8,128)(2,1)} async-done(((bf16[128,4096]{1,0:T(8,128)(2,1)}), bf16[1024,4096]{1,0:T(8,128)(2,1)}) %all-gather.5.cloned.1.call-update) | async-done | bytes 8388624 | tf_op jit(solution)/shard_map/all_gather | solution.py:48
  185.3 0.7 collective-permute-start
  186.1 0.1 add.179
  186.1 5.4 %gather_fusion.2 = bf16[1024,768]{1,0:T(8,128)(2,1)} fusion(bf16[1152,768]{1,0:T(8,128)(2,1)S(1)} %bitcast.65, s32[1024]{0:T(1024)S(1)} %broadcast_clamp_fusion), kind=kCustom, calls=%fused_computation.2 | custom fusion | bytes 3149824 | tf_op jit(solution)/shard_map/gather | solution.py:63
  191.5 0.1 add.170
  191.6 5.2 %gather_fusion.1 = bf16[1024,768]{1,0:T(8,128)(2,1)} fusion(bf16[1152,768]{1,0:T(8,128)(2,1)S(1)} %bitcast.66, s32[1024]{0:T(1024)S(1)} %broadcast_clamp_fusion.1), kind=kCustom, calls=%fused_computation.1 | custom fusion | bytes 3149824 | tf_op jit(solution)/shard_map/gather | solution.py:63
  196.9 2.7 copy.55
  199.6 1.6 copy.56
  201.2 13.1 %fusion = f32[4096,768]{1,0:T(8,128)} fusion(bf16[1024,4096]{1,0:T(8,128)(2,1)} %all-gather.5.cloned.1.call-done, f32[1024]{0:T(1024)S(1)} %slice_bitcast_fusion.1, bf16[1024,768]{0,1:T(8,128)(2,1)} %copy.55, pred[1024]{0:T(1024)(128)(4,1)S(1)} %compare_bitcast_fusion.1), kind=kOutput, calls=%fused_computation.8 | convolution fusion | flops 6455820288 | bytes 22549504 | tf_op jit(solution)/shard_map/dot_general | solution.py:65
  214.3 0.0 collective-permute-done
  214.3 15.5 %add_convert_fusion = bf16[4096,768]{1,0:T(8,128)(2,1)} fusion(f32[4096,768]{1,0:T(8,128)} %fusion, bf16[1024,4096]{1,0:T(8,128)(2,1)} %collective-permute-done, f32[1024]{0:T(1024)S(1)} %slice_bitcast_fusion, bf16[1024,768]{0,1:T(8,128)(2,1)S(1)} %copy-done.3, pred[1024]{0:T(1024)(128)(4,1)S(1)} %compare_bitcast_fusion), kind=kOutput, calls=%fused_computation.7 | convolution fusion | flops 6462111744 | bytes 28840960 | tf_op jit(solution)/shard_map/dot_general | solution.py:65
  229.9 0.0 reduce-scatter.2.cloned.1.call-update
  229.9 11.5 %multiply_reduce_fusion.1 = f32[1024]{0:T(1024)S(1)} fusion(bf16[1024,4096]{1,0:T(8,128)(2,1)} %all-gather.5.cloned.1.call-done, bf16[4096,768]{1,0:T(8,128)(2,1)} %bitcast.83, bf16[1024,768]{0,1:T(8,128)(2,1)} %copy.55, pred[1024]{0:T(1024)(128)(4,1)S(1)} %compare_bitcast_fusion.1), kind=kOutput, calls=%fused_computation.13 | convolution fusion | flops 6445595648 | bytes 16258048 | tf_op jit(solution)/shard_map/dot_general | solution.py:68
  241.4 0.0 copy-start.4
  241.5 11.3 %multiply_reduce_fusion = f32[1024]{0:T(1024)S(1)} fusion(bf16[1024,4096]{1,0:T(8,128)(2,1)} %collective-permute-done, bf16[4096,768]{1,0:T(8,128)(2,1)} %bitcast.84, bf16[1024,768]{0,1:T(8,128)(2,1)S(1)} %copy-done.3, pred[1024]{0:T(1024)(128)(4,1)S(1)} %compare_bitcast_fusion), kind=kOutput, calls=%fused_computation.12 | convolution fusion | flops 6445595648 | bytes 16258048 | tf_op jit(solution)/shard_map/dot_general | solution.py:68
  252.8 0.6 pad_maximum_fusion.1
  253.4 4.7 %all-to-all-start.2 = ((f32[16,1,128]{2,1,0:T(1,128)}), f32[16,1,128]{2,1,0:T(1,128)S(1)}, u32[]{:S(2)}, u32[]{:S(2)}) async-start(f32[16,1,128]{2,1,0:T(1,128)} %bitcast.27), calls=%async_computation.3 | async-start | bytes 16384 | tf_op jit(solution)/shard_map/all_to_all | solution.py:80
  258.1 0.1 copy.57
  258.2 0.1 reshape.276
  258.3 6.7 %all-to-all-done.2 = f32[16,1,128]{2,1,0:T(1,128)S(1)} async-done(((f32[16,1,128]{2,1,0:T(1,128)}), f32[16,1,128]{2,1,0:T(1,128)S(1)}, u32[]{:S(2)}, u32[]{:S(2)}) %all-to-all-start.2) | async-done | bytes 8224 | tf_op jit(solution)/shard_map/all_to_all | solution.py:80
  265.1 7.0 %gather_fusion.4 = f32[1024]{0:T(1024)S(1)} fusion(f32[128,16]{0,1:T(8,128)S(1)} %bitcast.64, s32[1024]{0:T(1024)S(1)} %reshape.276), kind=kCustom, calls=%fused_computation.4 | custom fusion | bytes 16384 | tf_op jit(solution)/shard_map/jit(take_along_axis)/gather | solution.py:81
  272.1 0.1 reshape.279
  272.2 0.6 and_select_fusion.1
  272.8 40.6 %reduce-scatter.2.cloned.1.call-done = bf16[256,768]{1,0:T(8,128)(2,1)} async-done(((bf16[4096,768]{1,0:T(8,128)(2,1)}), bf16[256,768]{1,0:T(8,128)(2,1)}) %reduce-scatter.2.cloned.1.call-update) | async-done | bytes 393232 | tf_op jit(solution)/shard_map/reduce_scatter | solution.py:75
  313.4 1.9 bitcast_convert_fusion
  (35 shorter events, 0.3 us)
Async XLA Ops:
  7.2 29.9 %copy-start = (bf16[128,8,768]{2,1,0:T(8,128)(2,1)S(1)}, bf16[128,8,768]{2,1,0:T(8,128)(2,1)}, u32[]{:S(2)}) copy-start(bf16[128,8,768]{2,1,0:T(8,128)(2,1)} %param.5) | copy-start | bytes 4718596
  7.2 1.7 copy-start.1
  7.2 87.1 %all-gather.3.cloned.1.call-start = ((), (), s32[]{:S(2)}) async-start(), calls=%async_computation.4 | async-start | bytes 6684672 | tf_op jit(solution)/shard_map/all_gather | solution.py:44
  25.9 17.3 %all-to-all-start.1 = ((f32[16,2,128]{2,1,0:T(2,128)}), f32[16,2,128]{2,1,0:T(2,128)S(1)}, u32[]{:S(2)}, u32[]{:S(2)}) async-start(f32[16,2,128]{2,1,0:T(2,128)} %copy.53), calls=%async_computation.1 | async-start | bytes 32768 | tf_op jit(solution)/shard_map/all_to_all | solution.py:46
  35.9 149.4 %all-gather.5.cloned.1.call-start = ((), (), s32[]{:S(2)}) async-start(), calls=%async_computation.5 | async-start | bytes 9437184 | tf_op jit(solution)/shard_map/all_gather | solution.py:48
  94.3 219.1 %reduce-scatter.2.cloned.1.call-start = ((), (), s32[]{:S(2)}) async-start(), calls=%async_computation.6 | async-start | bytes 6684672 | tf_op jit(solution)/shard_map/reduce_scatter | solution.py:75
  185.3 29.0 %collective-permute-start = (bf16[1024,4096]{1,0:T(8,128)(2,1)}, bf16[1024,4096]{1,0:T(8,128)(2,1)}, u32[]{:S(2)}, u32[]{:S(2)}) collective-permute-start(bf16[1024,4096]{1,0:T(8,128)(2,1)} %all-gather.5.cloned.1.call-done), channel_id=1, source_target_pairs={{0,1},{1,0},{2,3},{3,2},{4,5},{5,4},{6,7},{7,6},{8,9},{9,8},{10,11... | collective-permute-start | bytes 25165832 | tf_op jit(solution)/shard_map/ppermute | solution.py:49
  196.9 2.7 copy-start.2
  201.2 13.1 %copy-start.3 = (bf16[1024,768]{0,1:T(8,128)(2,1)S(1)}, bf16[1024,768]{0,1:T(8,128)(2,1)}, u32[]{:S(2)}) copy-start(bf16[1024,768]{0,1:T(8,128)(2,1)} %copy.56) | copy-start | bytes 4718596
  241.4 16.7 %copy-start.4 = (s32[128,8]{0,1:T(8,128)S(1)}, s32[128,8]{0,1:T(8,128)}, u32[]{:S(2)}) copy-start(s32[128,8]{0,1:T(8,128)} %param.8) | copy-start | bytes 12292
  253.4 11.6 %all-to-all-start.2 = ((f32[16,1,128]{2,1,0:T(1,128)}), f32[16,1,128]{2,1,0:T(1,128)S(1)}, u32[]{:S(2)}, u32[]{:S(2)}) async-start(f32[16,1,128]{2,1,0:T(1,128)} %bitcast.27), calls=%async_computation.3 | async-start | bytes 16384 | tf_op jit(solution)/shard_map/all_to_all | solution.py:80
Sparse Core Ops, SparseCore 0:
  10.5 70.1 all-gather.2
  94.4 90.8 all-gather.4
  230.0 83.3 reduce-scatter.1

commit v6 on v5

--- a/solution.py
+++ b/solution.py
@@ -35,8 +35,8 @@
     )
     send_h = jnp.where(filled[:, :, None], picked_h, jnp.zeros_like(picked_h))
     routed = member == 1
-    p_tok = jnp.where(
-        routed, jnp.take_along_axis(probs, which_k, axis=1).astype(jnp.float32), jnp.float32(0.0)
+    p_tok = jnp.sum(
+        jnp.where(chosen == 1, probs.astype(jnp.float32)[:, :, None], jnp.float32(0.0)), axis=1
     )
     inv = jnp.where(routed, slot_place, -1).astype(jnp.float32)
     send_meta = jnp.stack([p_tok.T, inv.T], axis=1)
@@ -49,36 +49,60 @@
     dy_pair = lax.ppermute(dy_z, "core", perm=[(c, (c + 1) % n_core) for c in range(n_core)])
 
     my_core = lax.axis_index("core")
-    flat_h = recv_h.reshape(total_rows, hid_width)
+    other_core = (my_core + 1) % n_core
+    half_hid = hid_width // 2
 
-    def half(dy_c, c):
+    def inputs(c):
         meta = lax.dynamic_index_in_dim(
             recv_meta.reshape(n_z, n_core, 2, tok_rows), c, axis=1, keepdims=False
         )
         p_c = meta[:, 0, :].reshape(-1)
         slot = meta[:, 1, :].astype(jnp.int32)
-        live = (slot >= 0).reshape(-1)
-        src = (jnp.arange(n_z, dtype=jnp.int32) * n_core + c)[:, None]
-        row = (src * slots_per + jnp.maximum(slot, 0)).reshape(-1)
-        h_c = jnp.where(live[:, None], flat_h[row], jnp.zeros((), flat_h.dtype))
+        h_src = lax.dynamic_index_in_dim(
+            recv_h.reshape(n_z, n_core, slots_per, hid_width), c, axis=1, keepdims=False
+        )
+        pick = (slot[:, :, None] == jnp.arange(slots_per, dtype=jnp.int32)[None, None, :]).astype(
+            h_src.dtype
+        )
+        h_c = lax.dot_general(
+            pick, h_src, (((2,), (1,)), ((0,), (0,))), preferred_element_type=jnp.float32
+        ).astype(h_src.dtype)
+        return p_c, h_c.reshape(n_z * tok_rows, hid_width)
+
+    p_own, h_own = inputs(my_core)
+    p_pair, h_pair = inputs(other_core)
+
+    def part(dy_c, p_c, h_c, which):
         scaled = (p_c[:, None] * dy_c.astype(jnp.float32)).astype(jnp.bfloat16)
-        part = lax.dot_general(
-            scaled, h_c, (((0,), (0,)), ((), ())), preferred_element_type=jnp.float32
+        h_cols = h_c[:, which * half_hid:(which + 1) * half_hid]
+        return lax.dot_general(scaled, h_cols, (((0,), (0,)), ((), ())), preferred_element_type=jnp.float32)
+
+    def score(dy_c, h_c):
+        g = lax.dot_general(dy_c, w_full, (((1,), (0,)), ((), ())), preferred_element_type=jnp.float32)
+        return jnp.sum(g * h_c.astype(jnp.float32), axis=1).reshape(n_z, tok_rows)
+
+    pieces = []
+    for which in range(2):
+        total = part(dy_z, p_own, h_own, which) + part(dy_pair, p_pair, h_pair, which)
+        pieces.append(
+            lax.psum_scatter(total.astype(jnp.bfloat16), "dp", scatter_dimension=0, tiled=True)
         )
-        g = lax.dot_general(dy_c, w_full, (((1,), (0,)), ((), ())), preferred_element_type=jnp.float32)
-        score = jnp.sum(g * h_c.astype(jnp.float32), axis=1)
-        return part, score.reshape(n_z, tok_rows)
-
-    part_own, score_own = half(dy_z, my_core)
-    part_pair, score_pair = half(dy_pair, (my_core + 1) % n_core)
-    partial = (part_own + part_pair).astype(jnp.bfloat16)
-    grad_block = lax.psum_scatter(partial, "dp", scatter_dimension=0, tiled=True).astype(jnp.float32)
+    grad_block = jnp.concatenate(pieces, axis=1).astype(jnp.float32)
+    score_own = score(dy_z, h_own)
+    score_pair = score(dy_pair, h_pair)
 
     first = jnp.where(my_core == 0, score_own, score_pair)
     second = jnp.where(my_core == 0, score_pair, score_own)
     by_source = jnp.stack([first, second], axis=1).reshape(groups, tok_rows)
     returned = lax.all_to_all(by_source, ez, split_axis=0, concat_axis=0, tiled=True)
-    gate_grad = jnp.take_along_axis(returned.T, expert_ids, axis=1)
+    gate_grad = jnp.sum(
+        jnp.where(
+            expert_ids[:, :, None] == jnp.arange(groups, dtype=jnp.int32)[None, None, :],
+            returned.T[:, None, :],
+            jnp.float32(0.0),
+        ),
+        axis=2,
+    )
     return (grad_block[None], gate_grad)
 
 

time: 322 us -> 372 us (1.16)
  waiting for transfers between devices: 139 us -> 205 us
  local copies, waits for them, and re-layouts: 44.2 us -> 9.1 us
  blocking collectives: 51 us -> 62.7 us
  matrix products: 51.5 us -> 61.4 us
  starting transfers between devices: 15.5 us -> 11 us
    reduce_scatter x1 -> x2, waiting for transfers between devices: 40.6 us -> 104 us  [body(): lax.psum_scatter(total.astype(jnp.bfloat16), 'dp', scatter_dimension=0, t...]
    gather x14 -> x0, local copies, waits for them, and re-layouts: 38.5 us -> none  [the longest x5 16.3 us: body(): jnp.take_along_axis(probs, which_k, axis=1).astype(jnp.float32)]
    all_to_all x0 -> x1, blocking collectives: none -> 11.6 us  [body(): lax.all_to_all(by_source, ez, split_axis=0, concat_axis=0, tiled=True)]
    dot_general x4 -> x8, matrix products: 51.5 us -> 61.4 us  [the longest x4 37.6 us: part(): lax.dot_general(scaled, h_cols, (((0,), (0,)), ((), ())), preferred_eleme...]
    all_to_all x1 -> x0, waiting for transfers between devices: 6.73 us -> none  [body(): lax.all_to_all(by_source, ez, split_axis=0, concat_axis=0, tiled=True)]
    all_to_all x1 -> x0, starting transfers between devices: 4.7 us -> none  [body(): lax.all_to_all(by_source, ez, split_axis=0, concat_axis=0, tiled=True)]
    all_gather x1, waiting for transfers between devices: 91 us -> 95.6 us  [body(): dy_z = lax.all_gather(upstream, 'z', axis=0, tiled=True)]
    ppermute x1, waiting for transfers between devices: 0.01 us -> 3.84 us  [body(): lax.ppermute(dy_z, 'core', perm=[(c, (c + 1) % n_core) for c in range(n_c...]
  transfers between devices with their start and end apart: 6 -> 6, of which waited for: 4 -> 6; matrix products, arithmetic and copies ran while one was open for 26% -> 17% of each run, Pallas kernels for 0% -> 0%
where the time goes in v6:
time: 372 us; the launch traced here: 371 us
  waiting for transfers between devices  205 us (55%)
  blocking collectives  62.7 us (17%)
  matrix products  61.4 us (17%)
  between operations  14 us (4%)
  starting transfers between devices  11 us (3%)
  local copies, waits for them, and re-layouts  9.1 us (2%)
  other arithmetic  7.27 us (2%)
    reduce_scatter x2, waiting for transfers between devices, body(): lax.psum_scatter(total.astype(jnp.bfloat16), 'dp', scatter_dimension=0, t...  104 us
    all_gather x1, waiting for transfers between devices, body(): dy_z = lax.all_gather(upstream, 'z', axis=0, tiled=True)  95.6 us
    all_to_all x1, blocking collectives, body(): recv_h = lax.all_to_all(send_h, ez, split_axis=0, concat_axis=0, tiled=True)  51.2 us
    dot_general x4, matrix products, part(): lax.dot_general(scaled, h_cols, (((0,), (0,)), ((), ())), preferred_eleme...  37.6 us
    dot_general x2, matrix products, score(): lax.dot_general(dy_c, w_full, (((1,), (0,)), ((), ())), preferred_element...  22.5 us
    all_to_all x1, blocking collectives, body(): lax.all_to_all(by_source, ez, split_axis=0, concat_axis=0, tiled=True)  11.6 us
    all_to_all x1, starting transfers between devices, body(): lax.all_to_all(send_meta, ez, split_axis=0, concat_axis=0, tiled=True)  9.98 us
  transfers between devices with their start and end apart: 6, of which 6 were waited for; matrix products, arithmetic and copies ran while one was open for 17% of the time, Pallas kernels for 0%

profile of v6, /device:TPU:1, one launch (start us, length us, event | category | flops | bytes accessed | tf_op | source)
XLA Modules:
  0.0 370.9 jit_solution(9906726790194780572)
XLA Ops:
  7.2 0.0 copy-start
  7.2 0.0 all-gather.3.cloned.1.call-start
  7.2 0.7 all-gather.3.cloned.1.call-update
  7.9 0.7 convert_reduce_fusion.1
  8.6 0.1 copy.28
  8.7 0.7 convert_element_type.84
  9.4 0.7 select_reduce_fusion.3
  10.1 0.1 copy.32
  10.2 0.2 reduce_window_sum.11
  10.4 0.7 copy.33
  11.1 10.0 %all-to-all-start.1 = ((f32[16,2,128]{2,1,0:T(2,128)}), f32[16,2,128]{2,1,0:T(2,128)S(1)}, u32[]{:S(2)}, u32[]{:S(2)}) async-start(f32[16,2,128]{2,1,0:T(2,128)} %copy.33), calls=%async_computation.1 | async-start | bytes 32768 | tf_op jit(solution)/shard_map/all_to_all | solution.py:46
  21.1 0.0 all-gather.5.cloned.1.call-start
  21.1 0.1 copy.31
  21.2 0.1 copy.29
  21.3 0.9 convert_reduce_fusion
  22.2 0.1 add.62
  22.3 0.0 copy-done
  22.3 4.6 %gather_fusion = bf16[1152,768]{1,0:T(8,128)(2,1)S(1)} fusion(bf16[1024,768]{1,0:T(8,128)(2,1)S(1)} %bitcast.46, s32[2048]{0:T(1024)S(1)} %pad_clamp_fusion), kind=kCustom, calls=%fused_computation | custom fusion | bytes 3543552 | tf_op jit(solution)/shard_map/gather | solution.py:33
  26.9 1.4 broadcast_select_fusion
  28.4 0.1 all-to-all-done.1
  28.4 51.2 %all_to_all.22 = bf16[16,72,768]{2,1,0:T(8,128)(2,1)S(1)} all-to-all(bf16[16,72,768]{2,1,0:T(8,128)(2,1)} %broadcast_select_fusion), channel_id=1, replica_groups=mesh['dp'=16,'z'=8,'core'=2] {'z','core'}, dimensions={0} | all-to-all | bytes 3538944 | tf_op jit(solution)/shard_map/all_to_all | solution.py:45
  79.6 1.1 all-gather.3.cloned.1.call-done
  80.7 0.0 all-gather.5.cloned.1.call-update
  80.7 0.0 reduce-scatter.3.cloned.1.call-start
  80.8 95.6 %all-gather.5.cloned.1.call-done = bf16[1024,4096]{1,0:T(8,128)(2,1)} async-done(((bf16[128,4096]{1,0:T(8,128)(2,1)}), bf16[1024,4096]{1,0:T(8,128)(2,1)}) %all-gather.5.cloned.1.call-update) | async-done | bytes 8388624 | tf_op jit(solution)/shard_map/all_gather | solution.py:48
  176.4 0.7 collective-permute-start
  177.1 0.6 convolution_convert_fusion
  177.8 0.0 copy-start.1
  177.8 0.6 convolution_convert_fusion.1
  178.4 0.0 copy-start.3
  178.4 7.9 %fusion.1 = f32[4096,384]{1,0:T(8,128)S(1)} fusion(bf16[1024,4096]{1,0:T(8,128)(2,1)} %all-gather.5.cloned.1.call-done, f32[1024]{0:T(1024)S(1)} %get-tuple-element.25, bf16[1024,768]{1,0:T(8,128)(2,1)S(1)} %bitcast.53), kind=kOutput, calls=%fused_computation.6 | convolution fusion | flops 3233808384 | bytes 15470592 | tf_op jit(solution)/shard_map/dot_general | solution.py:78
  186.4 3.8 %collective-permute-done = bf16[1024,4096]{1,0:T(8,128)(2,1)} collective-permute-done((bf16[1024,4096]{1,0:T(8,128)(2,1)}, bf16[1024,4096]{1,0:T(8,128)(2,1)}, u32[]{:S(2)}, u32[]{:S(2)}) %collective-permute-start) | collective-permute-done | bytes 8388640 | tf_op jit(solution)/shard_map/ppermute | solution.py:49
  190.2 10.9 %add_convert_fusion.1 = bf16[4096,384]{1,0:T(8,128)(2,1)} fusion(f32[4096,384]{1,0:T(8,128)S(1)} %fusion.1, bf16[1024,4096]{1,0:T(8,128)(2,1)} %collective-permute-done, f32[1024]{0:T(1024)S(1)} %get-tuple-element.23, bf16[1024,768]{1,0:T(8,128)(2,1)S(1)} %bitcast.50), kind=kOutput, calls=%fused_computation.4 | convolution fusion | flops 3236954112 | bytes 18616320 | tf_op jit(solution)/shard_map/dot_general | solution.py:78
  201.1 0.0 reduce-scatter.3.cloned.1.call-update
  201.2 0.2 reduce-scatter.5.cloned.1.call-start
  201.4 7.7 %fusion = f32[4096,384]{1,0:T(8,128)S(1)} fusion(bf16[1024,4096]{1,0:T(8,128)(2,1)} %all-gather.5.cloned.1.call-done, f32[1024]{0:T(1024)S(1)} %get-tuple-element.25, bf16[1024,768]{1,0:T(8,128)(2,1)} %bitcast.54), kind=kOutput, calls=%fused_computation.5 | convolution fusion | flops 3233808384 | bytes 15470592 | tf_op jit(solution)/shard_map/dot_general | solution.py:78
  209.1 11.0 %add_convert_fusion = bf16[4096,384]{1,0:T(8,128)(2,1)} fusion(f32[4096,384]{1,0:T(8,128)S(1)} %fusion, bf16[1024,4096]{1,0:T(8,128)(2,1)} %collective-permute-done, f32[1024]{0:T(1024)S(1)} %get-tuple-element.23, bf16[1024,768]{1,0:T(8,128)(2,1)S(1)} %bitcast.51), kind=kOutput, calls=%fused_computation.3 | convolution fusion | flops 3236954112 | bytes 18616320 | tf_op jit(solution)/shard_map/dot_general | solution.py:78
  220.1 0.0 reduce-scatter.5.cloned.1.call-update
  220.2 1.6 copy.36
  221.8 1.7 copy.35
  223.6 11.2 %multiply_reduce_fusion.1 = f32[1024]{0:T(1024)S(1)} fusion(bf16[1024,768]{0,1:T(8,128)(2,1)S(1)} %copy.35, bf16[1024,4096]{1,0:T(8,128)(2,1)} %all-gather.5.cloned.1.call-done, bf16[4096,768]{1,0:T(8,128)(2,1)} %bitcast.64), kind=kOutput, calls=%fused_computation.8 | convolution fusion | flops 6444809216 | bytes 16257024 | tf_op jit(solution)/shard_map/dot_general | solution.py:81
  234.8 0.0 copy-start.5
  234.8 11.3 %multiply_reduce_fusion = f32[1024]{0:T(1024)S(1)} fusion(bf16[1024,768]{0,1:T(8,128)(2,1)S(1)} %copy-done.4, bf16[1024,4096]{1,0:T(8,128)(2,1)} %collective-permute-done, bf16[4096,768]{1,0:T(8,128)(2,1)} %bitcast.65), kind=kOutput, calls=%fused_computation.7 | convolution fusion | flops 6444809216 | bytes 16257024 | tf_op jit(solution)/shard_map/dot_general | solution.py:81
  246.2 11.6 %all_to_all.23 = f32[16,1,128]{2,1,0:T(1,128)S(1)} all-to-all(f32[16,1,128]{2,1,0:T(1,128)S(1)} %bitcast.60), channel_id=1, replica_groups=mesh['dp'=16,'z'=8,'core'=2] {'z','core'}, dimensions={0} | all-to-all | bytes 16384 | tf_op jit(solution)/shard_map/all_to_all | solution.py:97
  257.7 0.6 select_reduce_fusion.2
  258.3 20.4 %reduce-scatter.3.cloned.1.call-done = bf16[256,384]{1,0:T(8,128)(2,1)} async-done(((bf16[4096,384]{1,0:T(8,128)(2,1)}), bf16[256,384]{1,0:T(8,128)(2,1)}) %reduce-scatter.3.cloned.1.call-update) | async-done | bytes 196624 | tf_op jit(solution)/shard_map/reduce_scatter | solution.py:88
  278.8 83.6 %reduce-scatter.5.cloned.1.call-done = bf16[256,384]{1,0:T(8,128)(2,1)} async-done(((bf16[4096,384]{1,0:T(8,128)(2,1)}), bf16[256,384]{1,0:T(8,128)(2,1)}) %reduce-scatter.5.cloned.1.call-update) | async-done | bytes 196624 | tf_op jit(solution)/shard_map/reduce_scatter | solution.py:88
  362.4 2.0 maximum_convert_fusion
  (20 shorter events, 0.1 us)
Async XLA Ops:
  7.2 15.2 %copy-start = (bf16[128,8,768]{2,1,0:T(8,128)(2,1)S(1)}, bf16[128,8,768]{2,1,0:T(8,128)(2,1)}, u32[]{:S(2)}) copy-start(bf16[128,8,768]{2,1,0:T(8,128)(2,1)} %param.5) | copy-start | bytes 4718596
  7.2 73.5 %all-gather.3.cloned.1.call-start = ((), (), s32[]{:S(2)}) async-start(), calls=%async_computation.5 | async-start | bytes 6684672 | tf_op jit(solution)/shard_map/all_gather | solution.py:44
  11.1 17.3 %all-to-all-start.1 = ((f32[16,2,128]{2,1,0:T(2,128)}), f32[16,2,128]{2,1,0:T(2,128)S(1)}, u32[]{:S(2)}, u32[]{:S(2)}) async-start(f32[16,2,128]{2,1,0:T(2,128)} %copy.33), calls=%async_computation.1 | async-start | bytes 32768 | tf_op jit(solution)/shard_map/all_to_all | solution.py:46
  21.1 155.3 %all-gather.5.cloned.1.call-start = ((), (), s32[]{:S(2)}) async-start(), calls=%async_computation.6 | async-start | bytes 9437184 | tf_op jit(solution)/shard_map/all_gather | solution.py:48
  80.7 198.0 %reduce-scatter.3.cloned.1.call-start = ((), (), s32[]{:S(2)}) async-start(), calls=%async_computation.7 | async-start | bytes 3342336 | tf_op jit(solution)/shard_map/reduce_scatter | solution.py:88
  176.4 13.8 %collective-permute-start = (bf16[1024,4096]{1,0:T(8,128)(2,1)}, bf16[1024,4096]{1,0:T(8,128)(2,1)}, u32[]{:S(2)}, u32[]{:S(2)}) collective-permute-start(bf16[1024,4096]{1,0:T(8,128)(2,1)} %all-gather.5.cloned.1.call-done), channel_id=1, source_target_pairs={{0,1},{1,0},{2,3},{3,2},{4,5},{5,4},{6,7},{7,6},{8,9},{9,8},{10,11... | collective-permute-start | bytes 25165832 | tf_op jit(solution)/shard_map/ppermute | solution.py:49
  177.8 12.4 %copy-start.1 = (bf16[8,128,768]{2,1,0:T(8,128)(2,1)}, bf16[8,128,768]{2,1,0:T(8,128)(2,1)S(1)}, u32[]{:S(2)}) copy-start(bf16[8,128,768]{2,1,0:T(8,128)(2,1)S(1)} %convolution_convert_fusion) | copy-start | bytes 4718596
  178.4 8.0 %copy-start.3 = (bf16[8,128,768]{2,1,0:T(8,128)(2,1)}, bf16[8,128,768]{2,1,0:T(8,128)(2,1)S(1)}, u32[]{:S(2)}) copy-start(bf16[8,128,768]{2,1,0:T(8,128)(2,1)S(1)} %convolution_convert_fusion.1) | copy-start | bytes 4718596
  201.1 7.9 %copy-start.2 = (bf16[8,128,768]{2,1,0:T(8,128)(2,1)S(1)}, bf16[8,128,768]{2,1,0:T(8,128)(2,1)}, u32[]{:S(2)}) copy-start(bf16[8,128,768]{2,1,0:T(8,128)(2,1)} %copy-done.1) | copy-start | bytes 4718596
  201.2 161.2 %reduce-scatter.5.cloned.1.call-start = ((), (), s32[]{:S(2)}) async-start(), calls=%async_computation.8 | async-start | bytes 3342336 | tf_op jit(solution)/shard_map/reduce_scatter | solution.py:88
  223.5 11.2 %copy-start.4 = (bf16[1024,768]{0,1:T(8,128)(2,1)S(1)}, bf16[1024,768]{0,1:T(8,128)(2,1)}, u32[]{:S(2)}) copy-start(bf16[1024,768]{0,1:T(8,128)(2,1)} %copy.36) | copy-start | bytes 4718596
  234.8 23.0 %copy-start.5 = (s32[128,8]{0,1:T(8,128)S(1)}, s32[128,8]{0,1:T(8,128)}, u32[]{:S(2)}) copy-start(s32[128,8]{0,1:T(8,128)} %param.8) | copy-start | bytes 12292
Sparse Core Ops, SparseCore 0:
  10.5 70.1 all-gather.2
  82.5 93.8 all-gather.4
  201.3 77.4 reduce-scatter.2
  282.2 80.1 reduce-scatter.4

commit v7 on v6

--- a/solution.py
+++ b/solution.py
@@ -50,7 +50,6 @@
 
     my_core = lax.axis_index("core")
     other_core = (my_core + 1) % n_core
-    half_hid = hid_width // 2
 
     def inputs(c):
         meta = lax.dynamic_index_in_dim(
@@ -72,22 +71,16 @@
     p_own, h_own = inputs(my_core)
     p_pair, h_pair = inputs(other_core)
 
-    def part(dy_c, p_c, h_c, which):
+    def part(dy_c, p_c, h_c):
         scaled = (p_c[:, None] * dy_c.astype(jnp.float32)).astype(jnp.bfloat16)
-        h_cols = h_c[:, which * half_hid:(which + 1) * half_hid]
-        return lax.dot_general(scaled, h_cols, (((0,), (0,)), ((), ())), preferred_element_type=jnp.float32)
+        return lax.dot_general(scaled, h_c, (((0,), (0,)), ((), ())), preferred_element_type=jnp.float32)
 
     def score(dy_c, h_c):
         g = lax.dot_general(dy_c, w_full, (((1,), (0,)), ((), ())), preferred_element_type=jnp.float32)
         return jnp.sum(g * h_c.astype(jnp.float32), axis=1).reshape(n_z, tok_rows)
 
-    pieces = []
-    for which in range(2):
-        total = part(dy_z, p_own, h_own, which) + part(dy_pair, p_pair, h_pair, which)
-        pieces.append(
-            lax.psum_scatter(total.astype(jnp.bfloat16), "dp", scatter_dimension=0, tiled=True)
-        )
-    grad_block = jnp.concatenate(pieces, axis=1).astype(jnp.float32)
+    partial = (part(dy_z, p_own, h_own) + part(dy_pair, p_pair, h_pair)).astype(jnp.bfloat16)
+    grad_block = lax.psum_scatter(partial, "dp", scatter_dimension=0, tiled=True).astype(jnp.float32)
     score_own = score(dy_z, h_own)
     score_pair = score(dy_pair, h_pair)
 

time: 372 us -> 302 us (0.81)
  waiting for transfers between devices: 205 us -> 142 us
  matrix products: 61.4 us -> 54.5 us
    reduce_scatter x2 -> x1, waiting for transfers between devices: 104 us -> 44.2 us  [body(): lax.psum_scatter(partial, 'dp', scatter_dimension=0, tiled=True)]
    dot_general x4 -> x2, matrix products: 37.6 us -> 30.8 us  [part(): lax.dot_general(scaled, h_c, (((0,), (0,)), ((), ())), preferred_element_...]
    ppermute x1, waiting for transfers between devices: 3.84 us -> 0.01 us  [body(): lax.ppermute(dy_z, 'core', perm=[(c, (c + 1) % n_core) for c in range(n_c...]
  transfers between devices with their start and end apart: 6 -> 5, of which waited for: 6 -> 4; matrix products, arithmetic and copies ran while one was open for 17% -> 18% of each run, Pallas kernels for 0% -> 0%
where the time goes in v7:
time: 302 us; the launch traced here: 301 us
  waiting for transfers between devices  142 us (47%)
  blocking collectives  62.5 us (21%)
  matrix products  54.5 us (18%)
  between operations  13.9 us (5%)
  starting transfers between devices  10.8 us (4%)
  local copies, waits for them, and re-layouts  10.4 us (3%)
  other arithmetic  7.24 us (2%)
    all_gather x1, waiting for transfers between devices, body(): dy_z = lax.all_gather(upstream, 'z', axis=0, tiled=True)  95.6 us
    all_to_all x1, blocking collectives, body(): recv_h = lax.all_to_all(send_h, ez, split_axis=0, concat_axis=0, tiled=True)  51.2 us
    reduce_scatter x1, waiting for transfers between devices, body(): lax.psum_scatter(partial, 'dp', scatter_dimension=0, tiled=True)  44.2 us
    dot_general x2, matrix products, part(): lax.dot_general(scaled, h_c, (((0,), (0,)), ((), ())), preferred_element_...  30.8 us
    dot_general x2, matrix products, score(): lax.dot_general(dy_c, w_full, (((1,), (0,)), ((), ())), preferred_element...  22.4 us
    all_to_all x1, blocking collectives, body(): lax.all_to_all(by_source, ez, split_axis=0, concat_axis=0, tiled=True)  11.3 us
    all_to_all x1, starting transfers between devices, body(): lax.all_to_all(send_meta, ez, split_axis=0, concat_axis=0, tiled=True)  9.98 us
  transfers between devices with their start and end apart: 5, of which 4 were waited for; matrix products, arithmetic and copies ran while one was open for 18% of the time, Pallas kernels for 0%

profile of v7, /device:TPU:1, one launch (start us, length us, event | category | flops | bytes accessed | tf_op | source)
XLA Modules:
  0.0 301.1 jit_solution(13296048800358125083)
XLA Ops:
  7.2 0.0 copy-start
  7.2 0.0 all-gather.3.cloned.1.call-start
  7.2 0.7 all-gather.3.cloned.1.call-update
  7.9 0.7 convert_element_type.68
  8.6 0.7 convert_reduce_fusion.1
  9.3 0.1 copy.28
  9.4 0.7 select_reduce_fusion.3
  10.1 0.1 copy.32
  10.2 0.2 reduce_window_sum.11
  10.4 0.7 copy.33
  11.1 10.0 %all-to-all-start.1 = ((f32[16,2,128]{2,1,0:T(2,128)}), f32[16,2,128]{2,1,0:T(2,128)S(1)}, u32[]{:S(2)}, u32[]{:S(2)}) async-start(f32[16,2,128]{2,1,0:T(2,128)} %copy.33), calls=%async_computation.1 | async-start | bytes 32768 | tf_op jit(solution)/shard_map/all_to_all | solution.py:46
  21.1 0.0 all-gather.5.cloned.1.call-start
  21.1 0.1 copy.29
  21.2 0.1 copy.31
  21.3 0.9 convert_reduce_fusion
  22.2 0.1 add.57
  22.3 0.0 copy-done
  22.3 4.6 %gather_fusion = bf16[1152,768]{1,0:T(8,128)(2,1)S(1)} fusion(bf16[1024,768]{1,0:T(8,128)(2,1)S(1)} %bitcast.49, s32[2048]{0:T(1024)S(1)} %pad_clamp_fusion), kind=kCustom, calls=%fused_computation | custom fusion | bytes 3543552 | tf_op jit(solution)/shard_map/gather | solution.py:33
  26.9 1.4 broadcast_select_fusion
  28.4 0.1 all-to-all-done.1
  28.4 51.2 %all_to_all.22 = bf16[16,72,768]{2,1,0:T(8,128)(2,1)S(1)} all-to-all(bf16[16,72,768]{2,1,0:T(8,128)(2,1)} %broadcast_select_fusion), channel_id=1, replica_groups=mesh['dp'=16,'z'=8,'core'=2] {'z','core'}, dimensions={0} | all-to-all | bytes 3538944 | tf_op jit(solution)/shard_map/all_to_all | solution.py:45
  79.6 1.1 all-gather.3.cloned.1.call-done
  80.7 0.0 all-gather.5.cloned.1.call-update
  80.7 0.0 reduce-scatter.2.cloned.1.call-start
  80.8 95.6 %all-gather.5.cloned.1.call-done = bf16[1024,4096]{1,0:T(8,128)(2,1)} async-done(((bf16[128,4096]{1,0:T(8,128)(2,1)}), bf16[1024,4096]{1,0:T(8,128)(2,1)}) %all-gather.5.cloned.1.call-update) | async-done | bytes 8388624 | tf_op jit(solution)/shard_map/all_gather | solution.py:48
  176.4 0.7 collective-permute-start
  177.1 0.6 convolution_convert_fusion
  177.8 0.0 copy-start.1
  177.8 0.6 convolution_convert_fusion.1
  178.4 0.0 copy-start.3
  178.4 15.3 %fusion = f32[4096,768]{1,0:T(8,128)} fusion(bf16[1024,768]{1,0:T(8,128)(2,1)S(1)} %bitcast.55, bf16[1024,4096]{1,0:T(8,128)(2,1)} %all-gather.5.cloned.1.call-done, f32[1024]{0:T(1024)S(1)} %get-tuple-element.24), kind=kOutput, calls=%fused_computation.4 | convolution fusion | flops 6455033856 | bytes 22548480 | tf_op jit(solution)/shard_map/dot_general | solution.py:76
  193.7 0.0 copy-done.3
  193.7 0.0 collective-permute-done
  193.7 0.0 copy-done.1
  193.7 15.5 %add_convert_fusion = bf16[4096,768]{1,0:T(8,128)(2,1)} fusion(f32[4096,768]{1,0:T(8,128)} %fusion, bf16[1024,768]{1,0:T(8,128)(2,1)S(1)} %bitcast.53, bf16[1024,4096]{1,0:T(8,128)(2,1)} %collective-permute-done, f32[1024]{0:T(1024)S(1)} %get-tuple-element.22), kind=kOutput, calls=%fused_computation.3 | convolution fusion | flops 6461325312 | bytes 28839936 | tf_op jit(solution)/shard_map/dot_general | solution.py:76
  209.2 0.0 reduce-scatter.2.cloned.1.call-update
  209.3 1.4 copy-done.2
  210.6 1.6 copy.36
  212.3 1.7 copy.35
  214.0 11.1 %multiply_reduce_fusion.1 = f32[1024]{0:T(1024)S(1)} fusion(bf16[1024,768]{0,1:T(8,128)(2,1)S(1)} %copy.35, bf16[1024,4096]{1,0:T(8,128)(2,1)} %all-gather.5.cloned.1.call-done, bf16[4096,768]{1,0:T(8,128)(2,1)} %bitcast.63), kind=kOutput, calls=%fused_computation.9 | convolution fusion | flops 6444809216 | bytes 16257024 | tf_op jit(solution)/shard_map/dot_general | solution.py:79
  225.1 0.0 copy-done.4
  225.1 0.0 copy-start.5
  225.2 11.3 %multiply_reduce_fusion = f32[1024]{0:T(1024)S(1)} fusion(bf16[1024,768]{0,1:T(8,128)(2,1)S(1)} %copy-done.4, bf16[1024,4096]{1,0:T(8,128)(2,1)} %collective-permute-done, bf16[4096,768]{1,0:T(8,128)(2,1)} %bitcast.64), kind=kOutput, calls=%fused_computation.8 | convolution fusion | flops 6444809216 | bytes 16257024 | tf_op jit(solution)/shard_map/dot_general | solution.py:79
  236.5 11.3 %all_to_all.23 = f32[16,1,128]{2,1,0:T(1,128)S(1)} all-to-all(f32[16,1,128]{2,1,0:T(1,128)S(1)} %bitcast.59), channel_id=1, replica_groups=mesh['dp'=16,'z'=8,'core'=2] {'z','core'}, dimensions={0} | all-to-all | bytes 16384 | tf_op jit(solution)/shard_map/all_to_all | solution.py:90
  247.9 0.0 copy-done.5
  247.9 0.6 select_reduce_fusion.2
  248.5 44.2 %reduce-scatter.2.cloned.1.call-done = bf16[256,768]{1,0:T(8,128)(2,1)} async-done(((bf16[4096,768]{1,0:T(8,128)(2,1)}), bf16[256,768]{1,0:T(8,128)(2,1)}) %reduce-scatter.2.cloned.1.call-update) | async-done | bytes 393232 | tf_op jit(solution)/shard_map/reduce_scatter | solution.py:83
  292.7 1.9 bitcast_convert_fusion
  (15 shorter events, 0.1 us)
Async XLA Ops:
  7.2 15.2 %copy-start = (bf16[128,8,768]{2,1,0:T(8,128)(2,1)S(1)}, bf16[128,8,768]{2,1,0:T(8,128)(2,1)}, u32[]{:S(2)}) copy-start(bf16[128,8,768]{2,1,0:T(8,128)(2,1)} %param.5) | copy-start | bytes 4718596
  7.2 73.5 %all-gather.3.cloned.1.call-start = ((), (), s32[]{:S(2)}) async-start(), calls=%async_computation.4 | async-start | bytes 6684672 | tf_op jit(solution)/shard_map/all_gather | solution.py:44
  11.1 17.3 %all-to-all-start.1 = ((f32[16,2,128]{2,1,0:T(2,128)}), f32[16,2,128]{2,1,0:T(2,128)S(1)}, u32[]{:S(2)}, u32[]{:S(2)}) async-start(f32[16,2,128]{2,1,0:T(2,128)} %copy.33), calls=%async_computation.1 | async-start | bytes 32768 | tf_op jit(solution)/shard_map/all_to_all | solution.py:46
  21.1 155.3 %all-gather.5.cloned.1.call-start = ((), (), s32[]{:S(2)}) async-start(), calls=%async_computation.5 | async-start | bytes 9437184 | tf_op jit(solution)/shard_map/all_gather | solution.py:48
  80.7 211.9 %reduce-scatter.2.cloned.1.call-start = ((), (), s32[]{:S(2)}) async-start(), calls=%async_computation.6 | async-start | bytes 6684672 | tf_op jit(solution)/shard_map/reduce_scatter | solution.py:83
  176.4 17.3 %collective-permute-start = (bf16[1024,4096]{1,0:T(8,128)(2,1)}, bf16[1024,4096]{1,0:T(8,128)(2,1)}, u32[]{:S(2)}, u32[]{:S(2)}) collective-permute-start(bf16[1024,4096]{1,0:T(8,128)(2,1)} %all-gather.5.cloned.1.call-done), channel_id=1, source_target_pairs={{0,1},{1,0},{2,3},{3,2},{4,5},{5,4},{6,7},{7,6},{8,9},{9,8},{10,11... | collective-permute-start | bytes 25165832 | tf_op jit(solution)/shard_map/ppermute | solution.py:49
  177.8 15.9 %copy-start.1 = (bf16[8,128,768]{2,1,0:T(8,128)(2,1)}, bf16[8,128,768]{2,1,0:T(8,128)(2,1)S(1)}, u32[]{:S(2)}) copy-start(bf16[8,128,768]{2,1,0:T(8,128)(2,1)S(1)} %convolution_convert_fusion) | copy-start | bytes 4718596
  178.4 15.3 %copy-start.3 = (bf16[8,128,768]{2,1,0:T(8,128)(2,1)}, bf16[8,128,768]{2,1,0:T(8,128)(2,1)S(1)}, u32[]{:S(2)}) copy-start(bf16[8,128,768]{2,1,0:T(8,128)(2,1)S(1)} %convolution_convert_fusion.1) | copy-start | bytes 4718596
  209.2 1.4 copy-start.2
  214.0 11.1 %copy-start.4 = (bf16[1024,768]{0,1:T(8,128)(2,1)S(1)}, bf16[1024,768]{0,1:T(8,128)(2,1)}, u32[]{:S(2)}) copy-start(bf16[1024,768]{0,1:T(8,128)(2,1)} %copy.36) | copy-start | bytes 4718596
  225.1 22.7 %copy-start.5 = (s32[128,8]{0,1:T(8,128)S(1)}, s32[128,8]{0,1:T(8,128)}, u32[]{:S(2)}) copy-start(s32[128,8]{0,1:T(8,128)} %param.8) | copy-start | bytes 12292
Sparse Core Ops, SparseCore 0:
  10.5 70.1 all-gather.2
  82.5 93.8 all-gather.4
  209.4 83.2 reduce-scatter.1

commit v8 on v7

--- a/solution.py
+++ b/solution.py
@@ -41,11 +41,19 @@
     inv = jnp.where(routed, slot_place, -1).astype(jnp.float32)
     send_meta = jnp.stack([p_tok.T, inv.T], axis=1)
 
-    w_full = lax.all_gather(w_down, "dp", axis=1, tiled=True)[0]
+    dy_z = lax.all_gather(upstream, "z", axis=0, tiled=True)
     recv_h = lax.all_to_all(send_h, ez, split_axis=0, concat_axis=0, tiled=True)
     recv_meta = lax.all_to_all(send_meta, ez, split_axis=0, concat_axis=0, tiled=True)
-    upstream, w_full, recv_h, recv_meta = lax.optimization_barrier((upstream, w_full, recv_h, recv_meta))
-    dy_z = lax.all_gather(upstream, "z", axis=0, tiled=True)
+    n_cut = 8
+    cut = hid_width // n_cut
+    w_full = jnp.concatenate(
+        [
+            lax.all_gather(w_down[0, :, i * cut:(i + 1) * cut], "dp", axis=0, tiled=True)
+            for i in range(n_cut)
+        ],
+        axis=1,
+    )
+    dy_z, w_full, recv_h, recv_meta = lax.optimization_barrier((dy_z, w_full, recv_h, recv_meta))
     dy_pair = lax.ppermute(dy_z, "core", perm=[(c, (c + 1) % n_core) for c in range(n_core)])
 
     my_core = lax.axis_index("core")

time: 302 us -> 374 us (1.24)
  blocking collectives: 62.5 us -> 184 us
  waiting for transfers between devices: 142 us -> 46 us
  starting transfers between devices: 10.8 us -> 51.6 us
  local copies, waits for them, and re-layouts: 10.4 us -> 20.7 us
  matrix products: 54.5 us -> 49.3 us
    all_gather x0 -> x8, blocking collectives: none -> 170 us  [body(): lax.all_gather(w_down[0, :, i * cut:(i + 1) * cut], 'dp', axis=0, tiled=T...]
    all_gather x1, waiting for transfers between devices: 95.6 us -> 0.02 us  [body(): dy_z = lax.all_gather(upstream, 'z', axis=0, tiled=True)]
    all_to_all x1 -> x0, blocking collectives: 51.2 us -> none  [body(): recv_h = lax.all_to_all(send_h, ez, split_axis=0, concat_axis=0, tiled=True)]
    ppermute x1, starting transfers between devices: 0.68 us -> 34.4 us  [body(): lax.ppermute(dy_z, 'core', perm=[(c, (c + 1) % n_core) for c in range(n_c...]
    concatenate x0 -> x1, local copies, waits for them, and re-layouts: none -> 12.4 us  [body(): jnp.concatenate([lax.all_gather(w_down[0, :, i * cut:(i + 1) * cut], 'dp'...]
    all_to_all x0 -> x1, starting transfers between devices: none -> 7.18 us  [body(): recv_h = lax.all_to_all(send_h, ez, split_axis=0, concat_axis=0, tiled=True)]
    dot_general x2, matrix products: 30.8 us -> 25.5 us  [part(): lax.dot_general(scaled, h_c, (((0,), (0,)), ((), ())), preferred_element_...]
  transfers between devices with their start and end apart: 5 -> 5, of which waited for: 4 -> 2; matrix products, arithmetic and copies ran while one was open for 18% -> 16% of each run, Pallas kernels for 0% -> 0%
where the time goes in v8:
time: 374 us; the launch traced here: 373 us
  blocking collectives  184 us (49%)
  starting transfers between devices  51.6 us (14%)
  matrix products  49.3 us (13%)
  waiting for transfers between devices  46 us (12%)
  local copies, waits for them, and re-layouts  20.7 us (6%)
  between operations  14.3 us (4%)
  other arithmetic  7.3 us (2%)
    all_gather x8, blocking collectives, body(): lax.all_gather(w_down[0, :, i * cut:(i + 1) * cut], 'dp', axis=0, tiled=T...  170 us
    reduce_scatter x1, waiting for transfers between devices, body(): lax.psum_scatter(partial, 'dp', scatter_dimension=0, tiled=True)  44.2 us
    ppermute x1, starting transfers between devices, body(): lax.ppermute(dy_z, 'core', perm=[(c, (c + 1) % n_core) for c in range(n_c...  34.4 us
    dot_general x2, matrix products, part(): lax.dot_general(scaled, h_c, (((0,), (0,)), ((), ())), preferred_element_...  25.5 us
    dot_general x2, matrix products, score(): lax.dot_general(dy_c, w_full, (((1,), (0,)), ((), ())), preferred_element...  22.6 us
    all_to_all x1, blocking collectives, body(): lax.all_to_all(by_source, ez, split_axis=0, concat_axis=0, tiled=True)  13.7 us
    concatenate x1, local copies, waits for them, and re-layouts, body(): jnp.concatenate([lax.all_gather(w_down[0, :, i * cut:(i + 1) * cut], 'dp'...  12.4 us
    all_to_all x1, starting transfers between devices, body(): lax.all_to_all(send_meta, ez, split_axis=0, concat_axis=0, tiled=True)  9.98 us
  transfers between devices with their start and end apart: 5, of which 2 were waited for; matrix products, arithmetic and copies ran while one was open for 16% of the time, Pallas kernels for 0%

profile of v8, /device:TPU:1, one launch (start us, length us, event | category | flops | bytes accessed | tf_op | source)
XLA Modules:
  0.0 372.9 jit_solution(7854062820497724740)
XLA Ops:
  7.2 0.0 copy-start
  7.2 0.0 all-gather.10.cloned.1.call-start
  7.2 0.7 all-gather.10.cloned.1.call-update
  7.9 0.7 convert_element_type.68
  8.6 0.7 convert_reduce_fusion.1
  9.3 0.1 copy.28
  9.4 0.7 select_reduce_fusion.3
  10.1 0.1 copy.32
  10.2 0.2 reduce_window_sum.11
  10.4 0.7 copy.33
  11.1 10.0 %all-to-all-start.1 = ((f32[16,2,128]{2,1,0:T(2,128)}), f32[16,2,128]{2,1,0:T(2,128)S(1)}, u32[]{:S(2)}, u32[]{:S(2)}) async-start(f32[16,2,128]{2,1,0:T(2,128)} %copy.33), calls=%async_computation.1 | async-start | bytes 32768 | tf_op jit(solution)/shard_map/all_to_all | solution.py:46
  21.1 0.1 copy.29
  21.2 0.1 copy.31
  21.2 0.9 convert_reduce_fusion
  22.1 0.1 add.57
  22.3 4.6 %gather_fusion = bf16[1152,768]{1,0:T(8,128)(2,1)S(1)} fusion(bf16[1024,768]{1,0:T(8,128)(2,1)S(1)} %bitcast.56, s32[2048]{0:T(1024)S(1)} %pad_clamp_fusion), kind=kCustom, calls=%fused_computation | custom fusion | bytes 3543552 | tf_op jit(solution)/shard_map/gather | solution.py:33
  26.9 0.0 copy-start.5
  26.9 1.5 broadcast_select_fusion
  28.4 0.0 all-to-all-done.1
  28.4 7.2 %all-to-all-start = ((bf16[16,72,768]{2,1,0:T(8,128)(2,1)}), bf16[16,72,768]{2,1,0:T(8,128)(2,1)S(1)}, u32[]{:S(2)}, u32[]{:S(2)}) async-start(bf16[16,72,768]{2,1,0:T(8,128)(2,1)} %broadcast_select_fusion), calls=%async_computation | async-start | bytes 3538944 | tf_op jit(solution)/shard_map/all_to_all | solution.py:45
  35.6 0.0 reduce-scatter.2.cloned.1.call-start
  35.7 0.2 fusion.16
  35.8 22.6 %all-gather.7 = bf16[1,4096,96]{2,1,0:T(8,128)(2,1)S(1)} all-gather(bf16[1,256,96]{2,1,0:T(8,128)(2,1)S(1)} %get-tuple-element.17), channel_id=9, replica_groups=mesh['dp'=16,'z'=8,'core'=2] {'dp'}, dimensions={1}, use_global_device_ids=true | all-gather | bytes 835584 | tf_op jit(solution)/shard_map/all_gather | solution.py:51
  58.4 21.9 %all-gather.5 = bf16[1,4096,96]{2,1,0:T(8,128)(2,1)} all-gather(bf16[1,256,96]{2,1,0:T(8,128)(2,1)S(1)} %get-tuple-element.18), channel_id=7, replica_groups=mesh['dp'=16,'z'=8,'core'=2] {'dp'}, dimensions={1}, use_global_device_ids=true | all-gather | bytes 835584 | tf_op jit(solution)/shard_map/all_gather | solution.py:51
  80.3 21.1 %all-gather.4 = bf16[1,4096,96]{2,1,0:T(8,128)(2,1)} all-gather(bf16[1,256,96]{2,1,0:T(8,128)(2,1)S(1)} %get-tuple-element.19), channel_id=6, replica_groups=mesh['dp'=16,'z'=8,'core'=2] {'dp'}, dimensions={1}, use_global_device_ids=true | all-gather | bytes 835584 | tf_op jit(solution)/shard_map/all_gather | solution.py:51
  101.4 21.9 %all-gather.3 = bf16[1,4096,96]{2,1,0:T(8,128)(2,1)} all-gather(bf16[1,256,96]{2,1,0:T(8,128)(2,1)S(1)} %get-tuple-element.20), channel_id=5, replica_groups=mesh['dp'=16,'z'=8,'core'=2] {'dp'}, dimensions={1}, use_global_device_ids=true | all-gather | bytes 835584 | tf_op jit(solution)/shard_map/all_gather | solution.py:51
  123.3 21.4 %all-gather.2 = bf16[1,4096,96]{2,1,0:T(8,128)(2,1)} all-gather(bf16[1,256,96]{2,1,0:T(8,128)(2,1)S(1)} %get-tuple-element.21), channel_id=4, replica_groups=mesh['dp'=16,'z'=8,'core'=2] {'dp'}, dimensions={1}, use_global_device_ids=true | all-gather | bytes 835584 | tf_op jit(solution)/shard_map/all_gather | solution.py:51
  144.7 20.5 %all-gather.1 = bf16[1,4096,96]{2,1,0:T(8,128)(2,1)} all-gather(bf16[1,256,96]{2,1,0:T(8,128)(2,1)S(1)} %get-tuple-element.22), channel_id=3, replica_groups=mesh['dp'=16,'z'=8,'core'=2] {'dp'}, dimensions={1}, use_global_device_ids=true | all-gather | bytes 835584 | tf_op jit(solution)/shard_map/all_gather | solution.py:51
  165.2 20.3 %all-gather = bf16[1,4096,96]{2,1,0:T(8,128)(2,1)} all-gather(bf16[1,256,96]{2,1,0:T(8,128)(2,1)S(1)} %get-tuple-element.23), channel_id=2, replica_groups=mesh['dp'=16,'z'=8,'core'=2] {'dp'}, dimensions={1}, use_global_device_ids=true | all-gather | bytes 835584 | tf_op jit(solution)/shard_map/all_gather | solution.py:51
  185.5 20.4 %all-gather.6 = bf16[1,4096,96]{2,1,0:T(8,128)(2,1)} all-gather(bf16[1,256,96]{2,1,0:T(8,128)(2,1)S(1)} %get-tuple-element.24), channel_id=8, replica_groups=mesh['dp'=16,'z'=8,'core'=2] {'dp'}, dimensions={1}, use_global_device_ids=true | all-gather | bytes 835584 | tf_op jit(solution)/shard_map/all_gather | solution.py:51
  205.9 12.4 %concatenate.3 = bf16[4096,768]{1,0:T(8,128)(2,1)} concatenate(bf16[4096,96]{1,0:T(8,128)(2,1)} %bitcast.70, bf16[4096,96]{1,0:T(8,128)(2,1)} %bitcast.69, bf16[4096,96]{1,0:T(8,128)(2,1)} %bitcast.68, bf16[4096,96]{1,0:T(8,128)(2,1)} %bitcast.67, bf16[4096,96]{1,0:T(8,128)(2,1)} %bitcast.66, bf16[4096,96]{1,0:T(8,128)(2,1)} %bitcast.65, bf16[4096,96]{1,0:T(8,128)(2,1)} %bitcast.71, ...), dimensions={1} | concatenate | bytes 12582912 | tf_op jit(solution)/shard_map/concatenate | solution.py:49
  218.3 0.0 all-gather.10.cloned.1.call-done
  218.3 34.4 %collective-permute-start = (bf16[1024,4096]{1,0:T(8,128)(2,1)}, bf16[1024,4096]{1,0:T(8,128)(2,1)}, u32[]{:S(2)}, u32[]{:S(2)}) collective-permute-start(bf16[1024,4096]{1,0:T(8,128)(2,1)} %all-gather.10.cloned.1.call-done), channel_id=1, source_target_pairs={{0,1},{1,0},{2,3},{3,2},{4,5},{5,4},{6,7},{7,6},{8,9},{9,8},{10,11... | collective-permute-start | bytes 25165832 | tf_op jit(solution)/shard_map/ppermute | solution.py:57
  252.7 0.6 convolution_convert_fusion
  253.4 0.6 convolution_convert_fusion.1
  254.0 10.8 %fusion = f32[4096,768]{1,0:T(8,128)S(1)} fusion(bf16[1024,768]{1,0:T(8,128)(2,1)S(1)} %bitcast.62, bf16[1024,4096]{1,0:T(8,128)(2,1)} %all-gather.10.cloned.1.call-done, f32[1024]{0:T(1024)S(1)} %get-tuple-element.32), kind=kOutput, calls=%fused_computation.4 | convolution fusion | flops 6455033856 | bytes 22548480 | tf_op jit(solution)/shard_map/dot_general | solution.py:84
  264.8 1.0 collective-permute-done
  265.8 14.7 %add_convert_fusion = bf16[4096,768]{1,0:T(8,128)(2,1)} fusion(f32[4096,768]{1,0:T(8,128)S(1)} %fusion, bf16[1024,768]{1,0:T(8,128)(2,1)S(1)} %bitcast.60, bf16[1024,4096]{1,0:T(8,128)(2,1)} %collective-permute-done, f32[1024]{0:T(1024)S(1)} %get-tuple-element.30), kind=kOutput, calls=%fused_computation.3 | convolution fusion | flops 6461325312 | bytes 28839936 | tf_op jit(solution)/shard_map/dot_general | solution.py:84
  280.5 0.0 reduce-scatter.2.cloned.1.call-update
  280.6 1.6 copy.36
  282.2 0.7 copy.35
  283.0 11.1 %multiply_reduce_fusion.1 = f32[1024]{0:T(1024)S(1)} fusion(bf16[1024,768]{0,1:T(8,128)(2,1)S(1)} %copy.35, bf16[1024,4096]{1,0:T(8,128)(2,1)} %all-gather.10.cloned.1.call-done, bf16[4096,768]{1,0:T(8,128)(2,1)} %concatenate.3), kind=kOutput, calls=%fused_computation.9 | convolution fusion | flops 6444809216 | bytes 16257024 | tf_op jit(solution)/shard_map/dot_general | solution.py:87
  294.1 0.0 copy-start.1
  294.1 11.5 %multiply_reduce_fusion = f32[1024]{0:T(1024)S(1)} fusion(bf16[1024,768]{0,1:T(8,128)(2,1)S(1)} %copy-done.4, bf16[1024,4096]{1,0:T(8,128)(2,1)} %collective-permute-done, bf16[4096,768]{1,0:T(8,128)(2,1)} %concatenate.3), kind=kOutput, calls=%fused_computation.8 | convolution fusion | flops 6444809216 | bytes 16257024 | tf_op jit(solution)/shard_map/dot_general | solution.py:87
  305.7 13.7 %all_to_all.22 = f32[16,1,128]{2,1,0:T(1,128)S(1)} all-to-all(f32[16,1,128]{2,1,0:T(1,128)S(1)} %bitcast.74), channel_id=1, replica_groups=mesh['dp'=16,'z'=8,'core'=2] {'z','core'}, dimensions={0} | all-to-all | bytes 16384 | tf_op jit(solution)/shard_map/all_to_all | solution.py:98
  319.3 0.6 select_reduce_fusion.2
  319.9 44.2 %reduce-scatter.2.cloned.1.call-done = bf16[256,768]{1,0:T(8,128)(2,1)} async-done(((bf16[4096,768]{1,0:T(8,128)(2,1)}), bf16[256,768]{1,0:T(8,128)(2,1)}) %reduce-scatter.2.cloned.1.call-update) | async-done | bytes 393232 | tf_op jit(solution)/shard_map/reduce_scatter | solution.py:91
  364.1 1.9 bitcast_convert_fusion
  (25 shorter events, 0.1 us)
Async XLA Ops:
  7.2 15.1 %copy-start = (bf16[128,8,768]{2,1,0:T(8,128)(2,1)S(1)}, bf16[128,8,768]{2,1,0:T(8,128)(2,1)}, u32[]{:S(2)}) copy-start(bf16[128,8,768]{2,1,0:T(8,128)(2,1)} %param.5) | copy-start | bytes 4718596
  7.2 211.1 %all-gather.10.cloned.1.call-start = ((), (), s32[]{:S(2)}) async-start(), calls=%async_computation.4 | async-start | bytes 9437184 | tf_op jit(solution)/shard_map/all_gather | solution.py:44
  11.1 17.3 %all-to-all-start.1 = ((f32[16,2,128]{2,1,0:T(2,128)}), f32[16,2,128]{2,1,0:T(2,128)S(1)}, u32[]{:S(2)}, u32[]{:S(2)}) async-start(f32[16,2,128]{2,1,0:T(2,128)} %copy.33), calls=%async_computation.1 | async-start | bytes 32768 | tf_op jit(solution)/shard_map/all_to_all | solution.py:46
  26.9 8.8 %copy-start.5 = (bf16[1,256,768]{2,1,0:T(8,128)(2,1)S(1)}, bf16[1,256,768]{2,1,0:T(8,128)(2,1)}, u32[]{:S(2)}) copy-start(bf16[1,256,768]{2,1,0:T(8,128)(2,1)} %param.9) | copy-start | bytes 1179652
  28.4 189.8 %all-to-all-start = ((bf16[16,72,768]{2,1,0:T(8,128)(2,1)}), bf16[16,72,768]{2,1,0:T(8,128)(2,1)S(1)}, u32[]{:S(2)}, u32[]{:S(2)}) async-start(bf16[16,72,768]{2,1,0:T(8,128)(2,1)} %broadcast_select_fusion), calls=%async_computation | async-start | bytes 3538944 | tf_op jit(solution)/shard_map/all_to_all | solution.py:45
  35.6 328.5 %reduce-scatter.2.cloned.1.call-start = ((), (), s32[]{:S(2)}) async-start(), calls=%async_computation.5 | async-start | bytes 6684672 | tf_op jit(solution)/shard_map/reduce_scatter | solution.py:91
  218.3 47.5 %collective-permute-start = (bf16[1024,4096]{1,0:T(8,128)(2,1)}, bf16[1024,4096]{1,0:T(8,128)(2,1)}, u32[]{:S(2)}, u32[]{:S(2)}) collective-permute-start(bf16[1024,4096]{1,0:T(8,128)(2,1)} %all-gather.10.cloned.1.call-done), channel_id=1, source_target_pairs={{0,1},{1,0},{2,3},{3,2},{4,5},{5,4},{6,7},{7,6},{8,9},{9,8},{10,11... | collective-permute-start | bytes 25165832 | tf_op jit(solution)/shard_map/ppermute | solution.py:57
  254.0 10.8 %copy-start.2 = (bf16[8,128,768]{2,1,0:T(8,128)(2,1)}, bf16[8,128,768]{2,1,0:T(8,128)(2,1)S(1)}, u32[]{:S(2)}) copy-start(bf16[8,128,768]{2,1,0:T(8,128)(2,1)S(1)} %convolution_convert_fusion.1) | copy-start | bytes 4718596
  280.5 1.7 copy-start.3
  283.0 11.1 %copy-start.4 = (bf16[1024,768]{0,1:T(8,128)(2,1)S(1)}, bf16[1024,768]{0,1:T(8,128)(2,1)}, u32[]{:S(2)}) copy-start(bf16[1024,768]{0,1:T(8,128)(2,1)} %copy.36) | copy-start | bytes 4718596
  294.1 25.2 %copy-start.6 = (s32[128,8]{0,1:T(8,128)S(1)}, s32[128,8]{0,1:T(8,128)}, u32[]{:S(2)}) copy-start(s32[128,8]{0,1:T(8,128)} %param.8) | copy-start | bytes 12292
  294.1 72.0 %copy-start.1 = (bf16[128,8,768]{2,1,0:T(8,128)(2,1)S(1)}, bf16[128,8,768]{2,1,0:T(8,128)(2,1)}, u32[]{:S(2)}) copy-start(bf16[128,8,768]{2,1,0:T(8,128)(2,1)} %param.5) | copy-start | bytes 4718596
Sparse Core Ops, SparseCore 0:
  9.8 135.8 all-gather.9
  280.7 83.4 reduce-scatter.1

commit v9 on v7

--- a/solution.py
+++ b/solution.py
@@ -41,11 +41,16 @@
     inv = jnp.where(routed, slot_place, -1).astype(jnp.float32)
     send_meta = jnp.stack([p_tok.T, inv.T], axis=1)
 
-    w_full = lax.all_gather(w_down, "dp", axis=1, tiled=True)[0]
+    dy_z = lax.all_gather(upstream, "z", axis=0, tiled=True)
     recv_h = lax.all_to_all(send_h, ez, split_axis=0, concat_axis=0, tiled=True)
     recv_meta = lax.all_to_all(send_meta, ez, split_axis=0, concat_axis=0, tiled=True)
-    upstream, w_full, recv_h, recv_meta = lax.optimization_barrier((upstream, w_full, recv_h, recv_meta))
-    dy_z = lax.all_gather(upstream, "z", axis=0, tiled=True)
+    w_pieces = [w_down[0]] + [
+        lax.ppermute(w_down[0], "dp", perm=[(i, (i - d) % n_dp) for i in range(n_dp)])
+        for d in range(1, n_dp)
+    ]
+    w_full = jnp.stack(w_pieces)
+    dy_z, w_full, recv_h, recv_meta = lax.optimization_barrier((dy_z, w_full, recv_h, recv_meta))
+    w_full = jnp.roll(w_full, lax.axis_index("dp"), axis=0).reshape(-1, hid_width)
     dy_pair = lax.ppermute(dy_z, "core", perm=[(c, (c + 1) % n_core) for c in range(n_core)])
 
     my_core = lax.axis_index("core")

time: 302 us -> 286 us (0.947)
  starting transfers between devices: 10.8 us -> 53 us
  waiting for transfers between devices: 142 us -> 105 us
  blocking collectives: 62.5 us -> 28.2 us
  local copies, waits for them, and re-layouts: 10.4 us -> 26.6 us
  matrix products: 54.5 us -> 45.6 us
  other arithmetic: 7.24 us -> 12 us
    all_gather x1, waiting for transfers between devices: 95.6 us -> 0.01 us  [body(): dy_z = lax.all_gather(upstream, 'z', axis=0, tiled=True)]
    ppermute x0 -> x15, waiting for transfers between devices: none -> 62.1 us  [body(): lax.ppermute(w_down[0], 'dp', perm=[(i, (i - d) % n_dp) for i in range(n_...]
    all_to_all x1 -> x0, blocking collectives: 51.2 us -> none  [body(): recv_h = lax.all_to_all(send_h, ez, split_axis=0, concat_axis=0, tiled=True)]
    ppermute x0 -> x15, starting transfers between devices: none -> 31.6 us  [body(): lax.ppermute(w_down[0], 'dp', perm=[(i, (i - d) % n_dp) for i in range(n_...]
    all_to_all x1, blocking collectives: 11.3 us -> 28.2 us  [body(): lax.all_to_all(by_source, ez, split_axis=0, concat_axis=0, tiled=True)]
    unnamed x12 -> x29, local copies, waits for them, and re-layouts: 1.41 us -> 16.8 us
    all_to_all x0 -> x1, starting transfers between devices: none -> 10.4 us  [body(): recv_h = lax.all_to_all(send_h, ez, split_axis=0, concat_axis=0, tiled=True)]
    dot_general x2, matrix products: 30.8 us -> 25.4 us  [part(): lax.dot_general(scaled, h_c, (((0,), (0,)), ((), ())), preferred_element_...]
  transfers between devices with their start and end apart: 5 -> 20, of which waited for: 4 -> 11; matrix products, arithmetic and copies ran while one was open for 18% -> 24% of each run, Pallas kernels for 0% -> 0%
where the time goes in v9:
time: 286 us; the launch traced here: 285 us
  waiting for transfers between devices  105 us (37%)
  starting transfers between devices  53 us (19%)
  matrix products  45.6 us (16%)
  blocking collectives  28.2 us (10%)
  local copies, waits for them, and re-layouts  26.6 us (9%)
  between operations  14.3 us (5%)
  other arithmetic  12 us (4%)
    ppermute x15, waiting for transfers between devices, body(): lax.ppermute(w_down[0], 'dp', perm=[(i, (i - d) % n_dp) for i in range(n_...  62.1 us
    reduce_scatter x1, waiting for transfers between devices, body(): lax.psum_scatter(partial, 'dp', scatter_dimension=0, tiled=True)  41.6 us
    ppermute x15, starting transfers between devices, body(): lax.ppermute(w_down[0], 'dp', perm=[(i, (i - d) % n_dp) for i in range(n_...  31.6 us
    all_to_all x1, blocking collectives, body(): lax.all_to_all(by_source, ez, split_axis=0, concat_axis=0, tiled=True)  28.2 us
    dot_general x2, matrix products, part(): lax.dot_general(scaled, h_c, (((0,), (0,)), ((), ())), preferred_element_...  25.4 us
    dot_general x2, matrix products, score(): lax.dot_general(dy_c, w_full, (((1,), (0,)), ((), ())), preferred_element...  19 us
    unnamed x29, local copies, waits for them, and re-layouts  16.8 us
    all_to_all x1, starting transfers between devices, body(): lax.all_to_all(send_meta, ez, split_axis=0, concat_axis=0, tiled=True)  10.6 us
  transfers between devices with their start and end apart: 20, of which 11 were waited for; matrix products, arithmetic and copies ran while one was open for 24% of the time, Pallas kernels for 0%

profile of v9, /device:TPU:1, one launch (start us, length us, event | category | flops | bytes accessed | tf_op | source)
XLA Modules:
  0.0 285.3 jit_solution(3107578101115694914)
XLA Ops:
  7.9 2.2 collective-permute-start.14
  10.1 2.6 collective-permute-start.13
  12.7 2.0 collective-permute-start.12
  14.7 2.2 collective-permute-start.1
  16.9 1.8 collective-permute-start
  21.9 10.6 %all-to-all-start.1 = ((f32[16,2,128]{2,1,0:T(2,128)}), f32[16,2,128]{2,1,0:T(2,128)S(1)}, u32[]{:S(2)}, u32[]{:S(2)}) async-start(f32[16,2,128]{2,1,0:T(2,128)} %copy.33), calls=%async_computation.1 | async-start | bytes 32768 | tf_op jit(solution)/shard_map/all_to_all | solution.py:46
  32.6 0.9 convert_reduce_fusion
  33.7 4.6 %gather_fusion = bf16[1152,768]{1,0:T(8,128)(2,1)S(1)} fusion(bf16[1024,768]{1,0:T(8,128)(2,1)S(1)} %bitcast.80, s32[2048]{0:T(1024)S(1)} %pad_clamp_fusion), kind=kCustom, calls=%fused_computation | custom fusion | bytes 3543552 | tf_op jit(solution)/shard_map/gather | solution.py:33
  38.2 1.5 broadcast_select_fusion
  39.7 1.8 constant_dynamic-update-slice_fusion
  41.5 9.9 %collective-permute-done = bf16[256,768]{1,0:T(8,128)(2,1)} collective-permute-done((bf16[256,768]{1,0:T(8,128)(2,1)}, bf16[256,768]{1,0:T(8,128)(2,1)}, u32[]{:S(2)}, u32[]{:S(2)}) %collective-permute-start) | collective-permute-done | bytes 393248 | tf_op jit(solution)/shard_map/ppermute | solution.py:48
  51.4 2.3 collective-permute-start.2
  53.7 1.8 bitcast_dynamic-update-slice_fusion.14
  56.0 10.4 %all-to-all-start = ((bf16[16,72,768]{2,1,0:T(8,128)(2,1)}), bf16[16,72,768]{2,1,0:T(8,128)(2,1)S(1)}, u32[]{:S(2)}, u32[]{:S(2)}) async-start(bf16[16,72,768]{2,1,0:T(8,128)(2,1)} %broadcast_select_fusion), calls=%async_computation | async-start | bytes 3538944 | tf_op jit(solution)/shard_map/all_to_all | solution.py:45
  66.4 1.8 bitcast_dynamic-update-slice_fusion.13
  68.2 4.4 %collective-permute-start.4 = (bf16[256,768]{1,0:T(8,128)(2,1)S(1)}, bf16[256,768]{1,0:T(8,128)(2,1)S(1)}, u32[]{:S(2)}, u32[]{:S(2)}) collective-permute-start(bf16[256,768]{1,0:T(8,128)(2,1)S(1)} %bitcast.97), channel_id=1, source_target_pairs={{0,176},{16,192},{32,208},{48,224},{64,240},{80,0},{96,16},{112,32... | collective-permute-start | bytes 1179656 | tf_op jit(solution)/shard_map/ppermute | solution.py:48
  73.3 4.8 %collective-permute-start.5 = (bf16[256,768]{1,0:T(8,128)(2,1)S(1)}, bf16[256,768]{1,0:T(8,128)(2,1)S(1)}, u32[]{:S(2)}, u32[]{:S(2)}) collective-permute-start(bf16[256,768]{1,0:T(8,128)(2,1)S(1)} %bitcast.98), channel_id=1, source_target_pairs={{0,160},{16,176},{32,192},{48,208},{64,224},{80,240},{96,0},{112,1... | collective-permute-start | bytes 1179656 | tf_op jit(solution)/shard_map/ppermute | solution.py:48
  78.1 0.8 bitcast_dynamic-update-slice_fusion.11
  78.9 8.6 %collective-permute-done.4 = bf16[256,768]{1,0:T(8,128)(2,1)S(1)} collective-permute-done((bf16[256,768]{1,0:T(8,128)(2,1)S(1)}, bf16[256,768]{1,0:T(8,128)(2,1)S(1)}, u32[]{:S(2)}, u32[]{:S(2)}) %collective-permute-start.4) | collective-permute-done | bytes 393248 | tf_op jit(solution)/shard_map/ppermute | solution.py:48
  87.5 0.8 bitcast_dynamic-update-slice_fusion.10
  88.3 7.4 %collective-permute-done.5 = bf16[256,768]{1,0:T(8,128)(2,1)S(1)} collective-permute-done((bf16[256,768]{1,0:T(8,128)(2,1)S(1)}, bf16[256,768]{1,0:T(8,128)(2,1)S(1)}, u32[]{:S(2)}, u32[]{:S(2)}) %collective-permute-start.5) | collective-permute-done | bytes 393248 | tf_op jit(solution)/shard_map/ppermute | solution.py:48
  96.1 0.8 bitcast_dynamic-update-slice_fusion.9
  97.0 5.5 %collective-permute-done.6 = bf16[256,768]{1,0:T(8,128)(2,1)S(1)} collective-permute-done((bf16[256,768]{1,0:T(8,128)(2,1)S(1)}, bf16[256,768]{1,0:T(8,128)(2,1)S(1)}, u32[]{:S(2)}, u32[]{:S(2)}) %collective-permute-start.6) | collective-permute-done | bytes 393248 | tf_op jit(solution)/shard_map/ppermute | solution.py:48
  102.5 1.0 collective-permute-start.8
  103.5 0.8 bitcast_dynamic-update-slice_fusion.8
  104.2 5.4 %collective-permute-done.7 = bf16[256,768]{1,0:T(8,128)(2,1)S(1)} collective-permute-done((bf16[256,768]{1,0:T(8,128)(2,1)S(1)}, bf16[256,768]{1,0:T(8,128)(2,1)S(1)}, u32[]{:S(2)}, u32[]{:S(2)}) %collective-permute-start.7) | collective-permute-done | bytes 393248 | tf_op jit(solution)/shard_map/ppermute | solution.py:48
  109.7 2.3 collective-permute-start.9
  112.8 5.1 %collective-permute-done.8 = bf16[256,768]{1,0:T(8,128)(2,1)S(1)} collective-permute-done((bf16[256,768]{1,0:T(8,128)(2,1)S(1)}, bf16[256,768]{1,0:T(8,128)(2,1)S(1)}, u32[]{:S(2)}, u32[]{:S(2)}) %collective-permute-start.8) | collective-permute-done | bytes 393248 | tf_op jit(solution)/shard_map/ppermute | solution.py:48
  117.9 2.7 collective-permute-start.10
  121.4 5.6 %collective-permute-done.9 = bf16[256,768]{1,0:T(8,128)(2,1)S(1)} collective-permute-done((bf16[256,768]{1,0:T(8,128)(2,1)S(1)}, bf16[256,768]{1,0:T(8,128)(2,1)S(1)}, u32[]{:S(2)}, u32[]{:S(2)}) %collective-permute-start.9) | collective-permute-done | bytes 393248 | tf_op jit(solution)/shard_map/ppermute | solution.py:48
  127.0 2.5 collective-permute-start.11
  129.5 0.8 bitcast_dynamic-update-slice_fusion.5
  130.3 5.5 %collective-permute-done.10 = bf16[256,768]{1,0:T(8,128)(2,1)S(1)} collective-permute-done((bf16[256,768]{1,0:T(8,128)(2,1)S(1)}, bf16[256,768]{1,0:T(8,128)(2,1)S(1)}, u32[]{:S(2)}, u32[]{:S(2)}) %collective-permute-start.10) | collective-permute-done | bytes 393248 | tf_op jit(solution)/shard_map/ppermute | solution.py:48
  135.7 0.8 bitcast_dynamic-update-slice_fusion.4
  136.5 9.0 %collective-permute-done.11 = bf16[256,768]{1,0:T(8,128)(2,1)S(1)} collective-permute-done((bf16[256,768]{1,0:T(8,128)(2,1)S(1)}, bf16[256,768]{1,0:T(8,128)(2,1)S(1)}, u32[]{:S(2)}, u32[]{:S(2)}) %collective-permute-start.11) | collective-permute-done | bytes 393248 | tf_op jit(solution)/shard_map/ppermute | solution.py:48
  146.3 1.8 bitcast_dynamic-update-slice_fusion.2
  148.1 1.8 bitcast_dynamic-update-slice_fusion.1
  149.8 1.8 bitcast_dynamic-update-slice_fusion
  153.3 10.8 %fusion = f32[4096,768]{1,0:T(8,128)S(1)} fusion(bf16[1024,768]{1,0:T(8,128)(2,1)S(1)} %bitcast.88, bf16[1024,4096]{1,0:T(8,128)(2,1)} %all-gather.2.cloned.1.call-done, f32[1024]{0:T(1024)S(1)} %get-tuple-element.24), kind=kOutput, calls=%fused_computation.6 | convolution fusion | flops 6455033856 | bytes 22548480 | tf_op jit(solution)/shard_map/dot_general | solution.py:81
  164.1 1.0 collective-permute-done.15
  165.1 14.6 %add_convert_fusion = bf16[4096,768]{1,0:T(8,128)(2,1)} fusion(f32[4096,768]{1,0:T(8,128)S(1)} %fusion, bf16[1024,768]{1,0:T(8,128)(2,1)S(1)} %bitcast.86, bf16[1024,4096]{1,0:T(8,128)(2,1)} %collective-permute-done.15, f32[1024]{0:T(1024)S(1)} %get-tuple-element.22), kind=kOutput, calls=%fused_computation.5 | convolution fusion | flops 6461325312 | bytes 28839936 | tf_op jit(solution)/shard_map/dot_general | solution.py:81
  179.8 1.7 copy.36
  182.2 4.7 %fusion.4 = bf16[16,256,768]{2,1,0:T(8,128)(2,1)S(1)} fusion(s32[]{:T(128)S(6)} %select_n.98, bf16[16,256,768]{2,1,0:T(8,128)(2,1)} %bitcast_dynamic-update-slice_fusion), kind=kLoop, calls=%fused_computation.10 | loop fusion | flops 3145728 | bytes 12582916 | tf_op jit(solution)/shard_map/jit(_roll_dynamic)/concatenate | solution.py:53
  187.0 9.4 %multiply_reduce_fusion.1 = f32[1024]{0:T(1024)S(1)} fusion(bf16[1024,768]{0,1:T(8,128)(2,1)S(1)} %copy.35, bf16[1024,4096]{1,0:T(8,128)(2,1)} %all-gather.2.cloned.1.call-done, bf16[4096,768]{1,0:T(8,128)(2,1)S(1)} %bitcast.84), kind=kOutput, calls=%fused_computation.12 | convolution fusion | flops 6444809216 | bytes 16257024 | tf_op jit(solution)/shard_map/dot_general | solution.py:84
  196.4 9.7 %multiply_reduce_fusion = f32[1024]{0:T(1024)S(1)} fusion(bf16[1024,768]{0,1:T(8,128)(2,1)S(1)} %copy-done.4, bf16[1024,4096]{1,0:T(8,128)(2,1)} %collective-permute-done.15, bf16[4096,768]{1,0:T(8,128)(2,1)S(1)} %bitcast.85), kind=kOutput, calls=%fused_computation.11 | convolution fusion | flops 6444809216 | bytes 16257024 | tf_op jit(solution)/shard_map/dot_general | solution.py:84
  206.1 28.2 %all_to_all.22 = f32[16,1,128]{2,1,0:T(1,128)S(1)} all-to-all(f32[16,1,128]{2,1,0:T(1,128)S(1)} %bitcast.107), channel_id=1, replica_groups=mesh['dp'=16,'z'=8,'core'=2] {'z','core'}, dimensions={0} | all-to-all | bytes 16384 | tf_op jit(solution)/shard_map/all_to_all | solution.py:95
  234.9 41.6 %reduce-scatter.2.cloned.1.call-done = bf16[256,768]{1,0:T(8,128)(2,1)} async-done(((bf16[4096,768]{1,0:T(8,128)(2,1)}), bf16[256,768]{1,0:T(8,128)(2,1)}) %reduce-scatter.2.cloned.1.call-update) | async-done | bytes 393232 | tf_op jit(solution)/shard_map/reduce_scatter | solution.py:88
  276.5 1.9 bitcast_convert_fusion
  (62 shorter events, 11.2 us)
Async XLA Ops:
  7.2 26.5 %copy-start = (bf16[128,8,768]{2,1,0:T(8,128)(2,1)S(1)}, bf16[128,8,768]{2,1,0:T(8,128)(2,1)}, u32[]{:S(2)}) copy-start(bf16[128,8,768]{2,1,0:T(8,128)(2,1)} %param.5) | copy-start | bytes 4718596
  7.2 144.4 %all-gather.2.cloned.1.call-start = ((), (), s32[]{:S(2)}) async-start(), calls=%async_computation.4 | async-start | bytes 9437184 | tf_op jit(solution)/shard_map/all_gather | solution.py:44
  7.9 141.9 %collective-permute-start.14 = (bf16[256,768]{1,0:T(8,128)(2,1)}, bf16[256,768]{1,0:T(8,128)(2,1)}, u32[]{:S(2)}, u32[]{:S(2)}) collective-permute-start(bf16[256,768]{1,0:T(8,128)(2,1)} %bitcast.90), channel_id=1, source_target_pairs={{0,16},{16,32},{32,48},{48,64},{64,80},{80,96},{96,112},{112,128},... | collective-permute-start | bytes 1179656 | tf_op jit(solution)/shard_map/ppermute | solution.py:48
  10.1 137.9 %collective-permute-start.13 = (bf16[256,768]{1,0:T(8,128)(2,1)}, bf16[256,768]{1,0:T(8,128)(2,1)}, u32[]{:S(2)}, u32[]{:S(2)}) collective-permute-start(bf16[256,768]{1,0:T(8,128)(2,1)} %bitcast.91), channel_id=1, source_target_pairs={{0,32},{16,48},{32,64},{48,80},{64,96},{80,112},{96,128},{112,144}... | collective-permute-start | bytes 1179656 | tf_op jit(solution)/shard_map/ppermute | solution.py:48
  12.7 133.5 %collective-permute-start.12 = (bf16[256,768]{1,0:T(8,128)(2,1)}, bf16[256,768]{1,0:T(8,128)(2,1)}, u32[]{:S(2)}, u32[]{:S(2)}) collective-permute-start(bf16[256,768]{1,0:T(8,128)(2,1)} %bitcast.92), channel_id=1, source_target_pairs={{0,48},{16,64},{32,80},{48,96},{64,112},{80,128},{96,144},{112,160... | collective-permute-start | bytes 1179656 | tf_op jit(solution)/shard_map/ppermute | solution.py:48
  14.7 40.7 %collective-permute-start.1 = (bf16[256,768]{1,0:T(8,128)(2,1)}, bf16[256,768]{1,0:T(8,128)(2,1)}, u32[]{:S(2)}, u32[]{:S(2)}) collective-permute-start(bf16[256,768]{1,0:T(8,128)(2,1)} %bitcast.93), channel_id=1, source_target_pairs={{0,224},{16,240},{32,0},{48,16},{64,32},{80,48},{96,64},{112,80},{... | collective-permute-start | bytes 1179656 | tf_op jit(solution)/shard_map/ppermute | solution.py:48
  16.9 34.5 %collective-permute-start = (bf16[256,768]{1,0:T(8,128)(2,1)}, bf16[256,768]{1,0:T(8,128)(2,1)}, u32[]{:S(2)}, u32[]{:S(2)}) collective-permute-start(bf16[256,768]{1,0:T(8,128)(2,1)} %bitcast.94), channel_id=1, source_target_pairs={{0,240},{16,0},{32,16},{48,32},{64,48},{80,64},{96,80},{112,96},{1... | collective-permute-start | bytes 1179656 | tf_op jit(solution)/shard_map/ppermute | solution.py:48
  21.9 34.1 %all-to-all-start.1 = ((f32[16,2,128]{2,1,0:T(2,128)}), f32[16,2,128]{2,1,0:T(2,128)S(1)}, u32[]{:S(2)}, u32[]{:S(2)}) async-start(f32[16,2,128]{2,1,0:T(2,128)} %copy.33), calls=%async_computation.1 | async-start | bytes 32768 | tf_op jit(solution)/shard_map/all_to_all | solution.py:46
  38.2 30.0 %copy-start.5 = (bf16[1,256,768]{2,1,0:T(8,128)(2,1)S(1)}, bf16[1,256,768]{2,1,0:T(8,128)(2,1)}, u32[]{:S(2)}) copy-start(bf16[1,256,768]{2,1,0:T(8,128)(2,1)} %param.9) | copy-start | bytes 1179652
  51.4 16.8 %collective-permute-start.2 = (bf16[256,768]{1,0:T(8,128)(2,1)}, bf16[256,768]{1,0:T(8,128)(2,1)S(1)}, u32[]{:S(2)}, u32[]{:S(2)}) collective-permute-start(bf16[256,768]{1,0:T(8,128)(2,1)} %bitcast.95), channel_id=1, source_target_pairs={{0,208},{16,224},{32,240},{48,0},{64,16},{80,32},{96,48},{112,64},... | collective-permute-start | bytes 1179656 | tf_op jit(solution)/shard_map/ppermute | solution.py:48
  55.5 17.8 %collective-permute-start.3 = (bf16[256,768]{1,0:T(8,128)(2,1)}, bf16[256,768]{1,0:T(8,128)(2,1)S(1)}, u32[]{:S(2)}, u32[]{:S(2)}) collective-permute-start(bf16[256,768]{1,0:T(8,128)(2,1)} %bitcast.96), channel_id=1, source_target_pairs={{0,192},{16,208},{32,224},{48,240},{64,0},{80,16},{96,32},{112,48}... | collective-permute-start | bytes 1179656 | tf_op jit(solution)/shard_map/ppermute | solution.py:48
  56.0 95.6 %all-to-all-start = ((bf16[16,72,768]{2,1,0:T(8,128)(2,1)}), bf16[16,72,768]{2,1,0:T(8,128)(2,1)S(1)}, u32[]{:S(2)}, u32[]{:S(2)}) async-start(bf16[16,72,768]{2,1,0:T(8,128)(2,1)} %broadcast_select_fusion), calls=%async_computation | async-start | bytes 3538944 | tf_op jit(solution)/shard_map/all_to_all | solution.py:45
  66.3 210.2 %reduce-scatter.2.cloned.1.call-start = ((), (), s32[]{:S(2)}) async-start(), calls=%async_computation.5 | async-start | bytes 6684672 | tf_op jit(solution)/shard_map/reduce_scatter | solution.py:88
  68.2 19.4 %collective-permute-start.4 = (bf16[256,768]{1,0:T(8,128)(2,1)S(1)}, bf16[256,768]{1,0:T(8,128)(2,1)S(1)}, u32[]{:S(2)}, u32[]{:S(2)}) collective-permute-start(bf16[256,768]{1,0:T(8,128)(2,1)S(1)} %bitcast.97), channel_id=1, source_target_pairs={{0,176},{16,192},{32,208},{48,224},{64,240},{80,0},{96,16},{112,32... | collective-permute-start | bytes 1179656 | tf_op jit(solution)/shard_map/ppermute | solution.py:48
  73.3 22.5 %collective-permute-start.5 = (bf16[256,768]{1,0:T(8,128)(2,1)S(1)}, bf16[256,768]{1,0:T(8,128)(2,1)S(1)}, u32[]{:S(2)}, u32[]{:S(2)}) collective-permute-start(bf16[256,768]{1,0:T(8,128)(2,1)S(1)} %bitcast.98), channel_id=1, source_target_pairs={{0,160},{16,176},{32,192},{48,208},{64,224},{80,240},{96,0},{112,1... | collective-permute-start | bytes 1179656 | tf_op jit(solution)/shard_map/ppermute | solution.py:48
  87.5 14.9 %collective-permute-start.6 = (bf16[256,768]{1,0:T(8,128)(2,1)S(1)}, bf16[256,768]{1,0:T(8,128)(2,1)S(1)}, u32[]{:S(2)}, u32[]{:S(2)}) collective-permute-start(bf16[256,768]{1,0:T(8,128)(2,1)S(1)} %bitcast.99), channel_id=1, source_target_pairs={{0,144},{16,160},{32,176},{48,192},{64,208},{80,224},{96,240},{112... | collective-permute-start | bytes 1179656 | tf_op jit(solution)/shard_map/ppermute | solution.py:48
  95.8 13.9 %collective-permute-start.7 = (bf16[256,768]{1,0:T(8,128)(2,1)S(1)}, bf16[256,768]{1,0:T(8,128)(2,1)S(1)}, u32[]{:S(2)}, u32[]{:S(2)}) collective-permute-start(bf16[256,768]{1,0:T(8,128)(2,1)S(1)} %bitcast.100), channel_id=1, source_target_pairs={{0,128},{16,144},{32,160},{48,176},{64,192},{80,208},{96,224},{112... | collective-permute-start | bytes 1179656 | tf_op jit(solution)/shard_map/ppermute | solution.py:48
  102.5 15.4 %collective-permute-start.8 = (bf16[256,768]{1,0:T(8,128)(2,1)S(1)}, bf16[256,768]{1,0:T(8,128)(2,1)S(1)}, u32[]{:S(2)}, u32[]{:S(2)}) collective-permute-start(bf16[256,768]{1,0:T(8,128)(2,1)S(1)} %bitcast.101), channel_id=1, source_target_pairs={{0,112},{16,128},{32,144},{48,160},{64,176},{80,192},{96,208},{112... | collective-permute-start | bytes 1179656 | tf_op jit(solution)/shard_map/ppermute | solution.py:48
  109.7 17.3 %collective-permute-start.9 = (bf16[256,768]{1,0:T(8,128)(2,1)S(1)}, bf16[256,768]{1,0:T(8,128)(2,1)S(1)}, u32[]{:S(2)}, u32[]{:S(2)}) collective-permute-start(bf16[256,768]{1,0:T(8,128)(2,1)S(1)} %bitcast.102), channel_id=1, source_target_pairs={{0,96},{16,112},{32,128},{48,144},{64,160},{80,176},{96,192},{112,... | collective-permute-start | bytes 1179656 | tf_op jit(solution)/shard_map/ppermute | solution.py:48
  117.9 17.8 %collective-permute-start.10 = (bf16[256,768]{1,0:T(8,128)(2,1)S(1)}, bf16[256,768]{1,0:T(8,128)(2,1)S(1)}, u32[]{:S(2)}, u32[]{:S(2)}) collective-permute-start(bf16[256,768]{1,0:T(8,128)(2,1)S(1)} %bitcast.103), channel_id=1, source_target_pairs={{0,80},{16,96},{32,112},{48,128},{64,144},{80,160},{96,176},{112,1... | collective-permute-start | bytes 1179656 | tf_op jit(solution)/shard_map/ppermute | solution.py:48
  127.0 18.5 %collective-permute-start.11 = (bf16[256,768]{1,0:T(8,128)(2,1)S(1)}, bf16[256,768]{1,0:T(8,128)(2,1)S(1)}, u32[]{:S(2)}, u32[]{:S(2)}) collective-permute-start(bf16[256,768]{1,0:T(8,128)(2,1)S(1)} %bitcast.104), channel_id=1, source_target_pairs={{0,64},{16,80},{32,96},{48,112},{64,128},{80,144},{96,160},{112,17... | collective-permute-start | bytes 1179656 | tf_op jit(solution)/shard_map/ppermute | solution.py:48
  151.6 13.5 %collective-permute-start.15 = (bf16[1024,4096]{1,0:T(8,128)(2,1)}, bf16[1024,4096]{1,0:T(8,128)(2,1)}, u32[]{:S(2)}, u32[]{:S(2)}) collective-permute-start(bf16[1024,4096]{1,0:T(8,128)(2,1)} %all-gather.2.cloned.1.call-done), channel_id=1, source_target_pairs={{0,1},{1,0},{2,3},{3,2},{4,5},{5,4},{6,7},{7,6},{8,9},{9,8},{10,11... | collective-permute-start | bytes 25165832 | tf_op jit(solution)/shard_map/ppermute | solution.py:54
  153.3 10.8 %copy-start.2 = (bf16[8,128,768]{2,1,0:T(8,128)(2,1)}, bf16[8,128,768]{2,1,0:T(8,128)(2,1)S(1)}, u32[]{:S(2)}) copy-start(bf16[8,128,768]{2,1,0:T(8,128)(2,1)S(1)} %convolution_convert_fusion.1) | copy-start | bytes 4718596
  179.7 1.7 copy-start.3
  186.9 9.4 %copy-start.4 = (bf16[1024,768]{0,1:T(8,128)(2,1)S(1)}, bf16[1024,768]{0,1:T(8,128)(2,1)}, u32[]{:S(2)}) copy-start(bf16[1024,768]{0,1:T(8,128)(2,1)} %copy.36) | copy-start | bytes 4718596
  196.3 38.0 %copy-start.6 = (s32[128,8]{0,1:T(8,128)S(1)}, s32[128,8]{0,1:T(8,128)}, u32[]{:S(2)}) copy-start(s32[128,8]{0,1:T(8,128)} %param.8) | copy-start | bytes 12292
  196.4 82.1 %copy-start.1 = (bf16[128,8,768]{2,1,0:T(8,128)(2,1)S(1)}, bf16[128,8,768]{2,1,0:T(8,128)(2,1)}, u32[]{:S(2)}) copy-start(bf16[128,8,768]{2,1,0:T(8,128)(2,1)} %param.5) | copy-start | bytes 4718596
Sparse Core Ops, SparseCore 0:
  9.8 136.2 all-gather.1
  179.9 96.6 reduce-scatter.1

commit v10 on v7

--- a/solution.py
+++ b/solution.py
@@ -10,7 +10,7 @@
     model_width = upstream.shape[1]
     n_z = lax.axis_size("z")
     n_core = lax.axis_size("core")
-    n_dp = lax.axis_size("dp")
+    n_dp = lax.axis_size("x") * lax.axis_size("y")
     groups = n_z * n_core
     slots_per = max(tok_rows * 9 // 16, tok_rows * top_k // groups)
     total_rows = groups * slots_per
@@ -41,11 +41,17 @@
     inv = jnp.where(routed, slot_place, -1).astype(jnp.float32)
     send_meta = jnp.stack([p_tok.T, inv.T], axis=1)
 
-    w_full = lax.all_gather(w_down, "dp", axis=1, tiled=True)[0]
+    dy_z = lax.all_gather(upstream, "z", axis=0, tiled=True)
     recv_h = lax.all_to_all(send_h, ez, split_axis=0, concat_axis=0, tiled=True)
     recv_meta = lax.all_to_all(send_meta, ez, split_axis=0, concat_axis=0, tiled=True)
-    upstream, w_full, recv_h, recv_meta = lax.optimization_barrier((upstream, w_full, recv_h, recv_meta))
-    dy_z = lax.all_gather(upstream, "z", axis=0, tiled=True)
+    def ring_gather(x, axis):
+        n = lax.axis_size(axis)
+        got = [x] + [lax.ppermute(x, axis, perm=[(i, (i - d) % n) for i in range(n)]) for d in range(1, n)]
+        return jnp.roll(jnp.stack(got), lax.axis_index(axis), axis=0)
+
+    w_full = ring_gather(ring_gather(w_down[0], "y"), "x")
+    dy_z, w_full, recv_h, recv_meta = lax.optimization_barrier((dy_z, w_full, recv_h, recv_meta))
+    w_full = w_full.reshape(-1, hid_width)
     dy_pair = lax.ppermute(dy_z, "core", perm=[(c, (c + 1) % n_core) for c in range(n_core)])
 
     my_core = lax.axis_index("core")
@@ -80,7 +86,7 @@
         return jnp.sum(g * h_c.astype(jnp.float32), axis=1).reshape(n_z, tok_rows)
 
     partial = (part(dy_z, p_own, h_own) + part(dy_pair, p_pair, h_pair)).astype(jnp.bfloat16)
-    grad_block = lax.psum_scatter(partial, "dp", scatter_dimension=0, tiled=True).astype(jnp.float32)
+    grad_block = lax.psum_scatter(partial, ("x", "y"), scatter_dimension=0, tiled=True).astype(jnp.float32)
     score_own = score(dy_z, h_own)
     score_pair = score(dy_pair, h_pair)
 
@@ -101,14 +107,17 @@
 
 def solution(mesh):
     n_dp, n_expert = mesh.devices.shape
-    sub = Mesh(mesh.devices.reshape(n_dp, n_expert // 2, 2), ("dp", "z", "core"))
-    tok = ("dp", "z", "core")
+    side = 4 if n_dp % 4 == 0 else 1
+    sub = Mesh(
+        mesh.devices.reshape(n_dp // side, side, n_expert // 2, 2), ("x", "y", "z", "core")
+    )
+    tok = ("x", "y", "z", "core")
     in_specs = (
         P(tok, None, None),
         P(tok, None),
         P(tok, None),
         P(tok, None),
-        P(("z", "core"), "dp", None),
+        P(("z", "core"), ("x", "y"), None),
     )
-    out_specs = (P(("z", "core"), "dp", None), P(tok, None))
+    out_specs = (P(("z", "core"), ("x", "y"), None), P(tok, None))
     return jax.shard_map(body, mesh=sub, in_specs=in_specs, out_specs=out_specs, check_vma=False)

time: 302 us -> 268 us (0.89)
  blocking collectives: 62.5 us -> 11.4 us
  local copies, waits for them, and re-layouts: 10.4 us -> 33.2 us
  waiting for transfers between devices: 142 us -> 123 us
  starting transfers between devices: 10.8 us -> 28.9 us
  matrix products: 54.5 us -> 49.3 us
    all_gather x1, waiting for transfers between devices: 95.6 us -> 19.4 us  [body(): dy_z = lax.all_gather(upstream, 'z', axis=0, tiled=True)]
    ppermute x0 -> x6, waiting for transfers between devices: none -> 54.9 us  [ring_gather(): lax.ppermute(x, axis, perm=[(i, (i - d) % n) for i in range(n)])]
    all_to_all x1 -> x0, blocking collectives: 51.2 us -> none  [body(): recv_h = lax.all_to_all(send_h, ez, split_axis=0, concat_axis=0, tiled=True)]
    unnamed x12 -> x28, local copies, waits for them, and re-layouts: 1.41 us -> 17.8 us
    all_to_all x0 -> x1, starting transfers between devices: none -> 9.71 us  [body(): recv_h = lax.all_to_all(send_h, ez, split_axis=0, concat_axis=0, tiled=True)]
    ppermute x0 -> x6, starting transfers between devices: none -> 8.45 us  [ring_gather(): lax.ppermute(x, axis, perm=[(i, (i - d) % n) for i in range(n)])]
    dynamic_slice x0 -> x1, local copies, waits for them, and re-layouts: none -> 6.09 us  [ring_gather(): return jnp.roll(jnp.stack(got), lax.axis_index(axis), axis=0)]
    dot_general x2, matrix products: 30.8 us -> 25.4 us  [part(): lax.dot_general(scaled, h_c, (((0,), (0,)), ((), ())), preferred_element_...]
  transfers between devices with their start and end apart: 5 -> 11, of which waited for: 4 -> 5; matrix products, arithmetic and copies ran while one was open for 18% -> 27% of each run, Pallas kernels for 0% -> 0%
where the time goes in v10:
time: 268 us; the launch traced here: 267 us
  waiting for transfers between devices  123 us (46%)
  matrix products  49.3 us (18%)
  local copies, waits for them, and re-layouts  33.2 us (12%)
  starting transfers between devices  28.9 us (11%)
  between operations  14.4 us (5%)
  blocking collectives  11.4 us (4%)
  other arithmetic  7.23 us (3%)
    ppermute x6, waiting for transfers between devices, ring_gather(): lax.ppermute(x, axis, perm=[(i, (i - d) % n) for i in range(n)])  54.9 us
    reduce_scatter x1, waiting for transfers between devices, body(): lax.psum_scatter(partial, ('x', 'y'), scatter_dimension=0, tiled=True)  46.6 us
    dot_general x2, matrix products, part(): lax.dot_general(scaled, h_c, (((0,), (0,)), ((), ())), preferred_element_...  25.4 us
    dot_general x2, matrix products, score(): lax.dot_general(dy_c, w_full, (((1,), (0,)), ((), ())), preferred_element...  22.6 us
    all_gather x1, waiting for transfers between devices, body(): dy_z = lax.all_gather(upstream, 'z', axis=0, tiled=True)  19.4 us
    unnamed x28, local copies, waits for them, and re-layouts  17.8 us
    all_to_all x1, blocking collectives, body(): lax.all_to_all(by_source, ez, split_axis=0, concat_axis=0, tiled=True)  11.4 us
    all_to_all x1, starting transfers between devices, body(): lax.all_to_all(send_meta, ez, split_axis=0, concat_axis=0, tiled=True)  9.99 us
  transfers between devices with their start and end apart: 11, of which 5 were waited for; matrix products, arithmetic and copies ran while one was open for 27% of the time, Pallas kernels for 0%

profile of v10, /device:TPU:1, one launch (start us, length us, event | category | flops | bytes accessed | tf_op | source)
XLA Modules:
  0.0 267.1 jit_solution(8966174074436116329)
XLA Ops:
  7.2 0.7 all-gather.2.cloned.1.call-update
  7.9 3.6 %collective-permute-start = (bf16[256,768]{1,0:T(8,128)(2,1)}, bf16[256,768]{1,0:T(8,128)(2,1)S(1)}, u32[]{:S(2)}, u32[]{:S(2)}) collective-permute-start(bf16[256,768]{1,0:T(8,128)(2,1)} %bitcast.81), channel_id=1, source_target_pairs={{0,48},{16,0},{32,16},{48,32},{1,49},{17,1},{33,17},{49,33},{2,50}... | collective-permute-start | bytes 1179656 | tf_op jit(solution)/shard_map/ppermute | solution.py:49
  11.6 0.3 collective-permute-start.1
  11.9 0.7 collective-permute-start.2
  12.6 0.7 convert_reduce_fusion.1
  13.3 0.1 copy.28
  13.4 0.7 convert_element_type.68
  14.1 0.7 select_reduce_fusion.3
  14.8 0.1 copy.32
  14.9 0.2 reduce_window_sum.11
  15.1 0.7 copy.33
  15.8 10.0 %all-to-all-start.1 = ((f32[16,2,128]{2,1,0:T(2,128)}), f32[16,2,128]{2,1,0:T(2,128)S(1)}, u32[]{:S(2)}, u32[]{:S(2)}) async-start(f32[16,2,128]{2,1,0:T(2,128)} %copy.33), calls=%async_computation.1 | async-start | bytes 32768 | tf_op jit(solution)/shard_map/all_to_all | solution.py:46
  25.8 0.1 copy.29
  25.9 0.9 convert_reduce_fusion
  26.9 0.1 add.80
  27.0 1.0 constant_dynamic-update-slice_fusion.1
  28.1 4.8 %collective-permute-done.2 = bf16[256,768]{1,0:T(8,128)(2,1)S(1)} collective-permute-done((bf16[256,768]{1,0:T(8,128)(2,1)}, bf16[256,768]{1,0:T(8,128)(2,1)S(1)}, u32[]{:S(2)}, u32[]{:S(2)}) %collective-permute-start.2) | collective-permute-done | bytes 393248 | tf_op jit(solution)/shard_map/ppermute | solution.py:49
  33.0 1.9 bitcast_dynamic-update-slice_fusion.6
  34.9 2.5 collective-permute-start.3
  37.4 0.6 collective-permute-start.4
  38.1 4.6 %gather_fusion = bf16[1152,768]{1,0:T(8,128)(2,1)S(1)} fusion(bf16[1024,768]{1,0:T(8,128)(2,1)S(1)} %bitcast.71, s32[2048]{0:T(1024)S(1)} %pad_clamp_fusion), kind=kCustom, calls=%fused_computation | custom fusion | bytes 3543552 | tf_op jit(solution)/shard_map/gather | solution.py:33
  42.6 0.7 collective-permute-start.5
  43.3 1.4 broadcast_select_fusion
  44.7 9.7 %all-to-all-start = ((bf16[16,72,768]{2,1,0:T(8,128)(2,1)}), bf16[16,72,768]{2,1,0:T(8,128)(2,1)S(1)}, u32[]{:S(2)}, u32[]{:S(2)}) async-start(bf16[16,72,768]{2,1,0:T(8,128)(2,1)} %broadcast_select_fusion), calls=%async_computation | async-start | bytes 3538944 | tf_op jit(solution)/shard_map/all_to_all | solution.py:45
  54.5 50.2 %collective-permute-done.3 = bf16[4,256,768]{2,1,0:T(8,128)(2,1)} collective-permute-done((bf16[4,256,768]{2,1,0:T(8,128)(2,1)}, bf16[4,256,768]{2,1,0:T(8,128)(2,1)}, u32[]{:S(2)}, u32[]{:S(2)}) %collective-permute-start.3) | collective-permute-done | bytes 1572896 | tf_op jit(solution)/shard_map/ppermute | solution.py:49
  104.7 2.7 bitcast_dynamic-update-slice_fusion.4
  107.3 2.6 bitcast_dynamic-update-slice_fusion.2
  110.0 1.3 bitcast_dynamic-update-slice_fusion
  111.3 2.7 %bitcast_dynamic-update-slice_fusion.7 = bf16[8,4,256,768]{3,2,1,0:T(8,128)(2,1)} fusion(bf16[8,4,256,768]{3,2,1,0:T(8,128)(2,1)} %bitcast_dynamic-update-slice_fusion, bf16[4,256,768]{2,1,0:T(8,128)(2,1)} %get-tuple-element.18), kind=kLoop, calls=%fused_computation.20 | loop fusion | bytes 3145728
  113.9 2.7 %bitcast_dynamic-update-slice_fusion.5 = bf16[8,4,256,768]{3,2,1,0:T(8,128)(2,1)} fusion(bf16[8,4,256,768]{3,2,1,0:T(8,128)(2,1)} %bitcast_dynamic-update-slice_fusion.7, bf16[4,256,768]{2,1,0:T(8,128)(2,1)} %collective-permute-done.3), kind=kLoop, calls=%fused_computation.18 | loop fusion | bytes 3145728
  116.7 2.7 %bitcast_dynamic-update-slice_fusion.3 = bf16[8,4,256,768]{3,2,1,0:T(8,128)(2,1)} fusion(bf16[8,4,256,768]{3,2,1,0:T(8,128)(2,1)} %bitcast_dynamic-update-slice_fusion.5, bf16[4,256,768]{2,1,0:T(8,128)(2,1)} %collective-permute-done.4), kind=kLoop, calls=%fused_computation.16 | loop fusion | bytes 3145728
  119.4 1.2 bitcast_dynamic-update-slice_fusion.1
  120.6 6.1 %constant_dynamic-slice_fusion.2 = bf16[4,4,256,768]{3,2,1,0:T(8,128)(2,1)} fusion(bf16[8,4,256,768]{3,2,1,0:T(8,128)(2,1)} %bitcast_dynamic-update-slice_fusion.1, s32[]{:T(128)S(6)} %select_n.102), kind=kLoop, calls=%fused_computation.71 | loop fusion | bytes 12582916 | tf_op jit(solution)/shard_map/jit(_roll_dynamic)/dynamic_slice | solution.py:50
  126.7 19.4 %all-gather.2.cloned.1.call-done = bf16[1024,4096]{1,0:T(8,128)(2,1)} async-done(((bf16[128,4096]{1,0:T(8,128)(2,1)}), bf16[1024,4096]{1,0:T(8,128)(2,1)}) %all-gather.2.cloned.1.call-update) | async-done | bytes 8388624 | tf_op jit(solution)/shard_map/all_gather | solution.py:44
  146.1 0.7 collective-permute-start.6
  146.8 0.6 convolution_convert_fusion
  147.4 0.6 convolution_convert_fusion.1
  148.1 10.8 %fusion = f32[4096,768]{1,0:T(8,128)S(1)} fusion(bf16[1024,768]{1,0:T(8,128)(2,1)S(1)} %bitcast.79, bf16[1024,4096]{1,0:T(8,128)(2,1)} %all-gather.2.cloned.1.call-done, f32[1024]{0:T(1024)S(1)} %get-tuple-element.26), kind=kOutput, calls=%fused_computation.4 | convolution fusion | flops 6455033856 | bytes 22548480 | tf_op jit(solution)/shard_map/dot_general | solution.py:82
  158.8 1.0 collective-permute-done.6
  159.9 14.7 %add_convert_fusion = bf16[4096,768]{1,0:T(8,128)(2,1)} fusion(f32[4096,768]{1,0:T(8,128)S(1)} %fusion, bf16[1024,768]{1,0:T(8,128)(2,1)S(1)} %bitcast.77, bf16[1024,4096]{1,0:T(8,128)(2,1)} %collective-permute-done.6, f32[1024]{0:T(1024)S(1)} %get-tuple-element.24), kind=kOutput, calls=%fused_computation.3 | convolution fusion | flops 6461325312 | bytes 28839936 | tf_op jit(solution)/shard_map/dot_general | solution.py:82
  174.6 1.6 copy.36
  176.2 0.7 copy.35
  177.0 11.1 %multiply_reduce_fusion.1 = f32[1024]{0:T(1024)S(1)} fusion(bf16[1024,768]{0,1:T(8,128)(2,1)S(1)} %copy.35, bf16[1024,4096]{1,0:T(8,128)(2,1)} %all-gather.2.cloned.1.call-done, bf16[4096,768]{1,0:T(8,128)(2,1)} %bitcast.75), kind=kOutput, calls=%fused_computation.9 | convolution fusion | flops 6444809216 | bytes 16257024 | tf_op jit(solution)/shard_map/dot_general | solution.py:85
  188.2 11.5 %multiply_reduce_fusion = f32[1024]{0:T(1024)S(1)} fusion(bf16[1024,768]{0,1:T(8,128)(2,1)S(1)} %copy-done.4, bf16[1024,4096]{1,0:T(8,128)(2,1)} %collective-permute-done.6, bf16[4096,768]{1,0:T(8,128)(2,1)} %bitcast.76), kind=kOutput, calls=%fused_computation.8 | convolution fusion | flops 6444809216 | bytes 16257024 | tf_op jit(solution)/shard_map/dot_general | solution.py:85
  199.7 11.4 %all_to_all.22 = f32[16,1,128]{2,1,0:T(1,128)S(1)} all-to-all(f32[16,1,128]{2,1,0:T(1,128)S(1)} %bitcast.86), channel_id=1, replica_groups=mesh['x'=4,'y'=4,'z'=8,'core'=2] {'z','core'}, dimensions={0} | all-to-all | bytes 16384 | tf_op jit(solution)/shard_map/all_to_all | solution.py:96
  211.1 0.6 select_reduce_fusion.2
  211.7 46.6 %reduce-scatter.2.cloned.1.call-done = bf16[256,768]{1,0:T(8,128)(2,1)} async-done(((bf16[4096,768]{1,0:T(8,128)(2,1)}), bf16[256,768]{1,0:T(8,128)(2,1)}) %reduce-scatter.2.cloned.1.call-update) | async-done | bytes 393232 | tf_op jit(solution)/shard_map/reduce_scatter | solution.py:89
  258.3 1.9 bitcast_convert_fusion
  (44 shorter events, 0.5 us)
Async XLA Ops:
  7.2 30.9 %copy-start = (bf16[128,8,768]{2,1,0:T(8,128)(2,1)S(1)}, bf16[128,8,768]{2,1,0:T(8,128)(2,1)}, u32[]{:S(2)}) copy-start(bf16[128,8,768]{2,1,0:T(8,128)(2,1)} %param.5) | copy-start | bytes 4718596
  7.2 25.7 %copy-start.5 = (bf16[1,256,768]{2,1,0:T(8,128)(2,1)S(1)}, bf16[1,256,768]{2,1,0:T(8,128)(2,1)}, u32[]{:S(2)}) copy-start(bf16[1,256,768]{2,1,0:T(8,128)(2,1)} %param.9) | copy-start | bytes 1179652
  7.2 138.9 %all-gather.2.cloned.1.call-start = ((), (), s32[]{:S(2)}) async-start(), calls=%async_computation.4 | async-start | bytes 9437184 | tf_op jit(solution)/shard_map/all_gather | solution.py:44
  7.9 20.1 %collective-permute-start = (bf16[256,768]{1,0:T(8,128)(2,1)}, bf16[256,768]{1,0:T(8,128)(2,1)S(1)}, u32[]{:S(2)}, u32[]{:S(2)}) collective-permute-start(bf16[256,768]{1,0:T(8,128)(2,1)} %bitcast.81), channel_id=1, source_target_pairs={{0,48},{16,0},{32,16},{48,32},{1,49},{17,1},{33,17},{49,33},{2,50}... | collective-permute-start | bytes 1179656 | tf_op jit(solution)/shard_map/ppermute | solution.py:49
  11.6 16.5 %collective-permute-start.1 = (bf16[256,768]{1,0:T(8,128)(2,1)}, bf16[256,768]{1,0:T(8,128)(2,1)S(1)}, u32[]{:S(2)}, u32[]{:S(2)}) collective-permute-start(bf16[256,768]{1,0:T(8,128)(2,1)} %bitcast.82), channel_id=1, source_target_pairs={{0,32},{16,48},{32,0},{48,16},{1,33},{17,49},{33,1},{49,17},{2,34}... | collective-permute-start | bytes 1179656 | tf_op jit(solution)/shard_map/ppermute | solution.py:49
  11.9 20.9 %collective-permute-start.2 = (bf16[256,768]{1,0:T(8,128)(2,1)}, bf16[256,768]{1,0:T(8,128)(2,1)S(1)}, u32[]{:S(2)}, u32[]{:S(2)}) collective-permute-start(bf16[256,768]{1,0:T(8,128)(2,1)} %bitcast.83), channel_id=1, source_target_pairs={{0,16},{16,32},{32,48},{48,0},{1,17},{17,33},{33,49},{49,1},{2,18}... | collective-permute-start | bytes 1179656 | tf_op jit(solution)/shard_map/ppermute | solution.py:49
  15.8 28.9 %all-to-all-start.1 = ((f32[16,2,128]{2,1,0:T(2,128)}), f32[16,2,128]{2,1,0:T(2,128)S(1)}, u32[]{:S(2)}, u32[]{:S(2)}) async-start(f32[16,2,128]{2,1,0:T(2,128)} %copy.33), calls=%async_computation.1 | async-start | bytes 32768 | tf_op jit(solution)/shard_map/all_to_all | solution.py:46
  34.9 69.7 %collective-permute-start.3 = (bf16[4,256,768]{2,1,0:T(8,128)(2,1)}, bf16[4,256,768]{2,1,0:T(8,128)(2,1)}, u32[]{:S(2)}, u32[]{:S(2)}) collective-permute-start(bf16[4,256,768]{2,1,0:T(8,128)(2,1)} %get-tuple-element.18), channel_id=1, source_target_pairs={{0,192},{64,0},{128,64},{192,128},{1,193},{65,1},{129,65},{193,129... | collective-permute-start | bytes 4718600 | tf_op jit(solution)/shard_map/ppermute | solution.py:49
  37.4 69.9 %collective-permute-start.4 = (bf16[4,256,768]{2,1,0:T(8,128)(2,1)}, bf16[4,256,768]{2,1,0:T(8,128)(2,1)}, u32[]{:S(2)}, u32[]{:S(2)}) collective-permute-start(bf16[4,256,768]{2,1,0:T(8,128)(2,1)} %get-tuple-element.18), channel_id=1, source_target_pairs={{0,128},{64,192},{128,0},{192,64},{1,129},{65,193},{129,1},{193,65... | collective-permute-start | bytes 4718600 | tf_op jit(solution)/shard_map/ppermute | solution.py:49
  42.6 67.4 %collective-permute-start.5 = (bf16[4,256,768]{2,1,0:T(8,128)(2,1)}, bf16[4,256,768]{2,1,0:T(8,128)(2,1)S(1)}, u32[]{:S(2)}, u32[]{:S(2)}) collective-permute-start(bf16[4,256,768]{2,1,0:T(8,128)(2,1)} %get-tuple-element.18), channel_id=1, source_target_pairs={{0,64},{64,128},{128,192},{192,0},{1,65},{65,129},{129,193},{193,1... | collective-permute-start | bytes 4718600 | tf_op jit(solution)/shard_map/ppermute | solution.py:49
  44.7 81.9 %all-to-all-start = ((bf16[16,72,768]{2,1,0:T(8,128)(2,1)}), bf16[16,72,768]{2,1,0:T(8,128)(2,1)S(1)}, u32[]{:S(2)}, u32[]{:S(2)}) async-start(bf16[16,72,768]{2,1,0:T(8,128)(2,1)} %broadcast_select_fusion), calls=%async_computation | async-start | bytes 3538944 | tf_op jit(solution)/shard_map/all_to_all | solution.py:45
  54.5 203.9 %reduce-scatter.2.cloned.1.call-start = ((), (), s32[]{:S(2)}) async-start(), calls=%async_computation.5 | async-start | bytes 6684672 | tf_op jit(solution)/shard_map/reduce_scatter | solution.py:89
  146.1 13.8 %collective-permute-start.6 = (bf16[1024,4096]{1,0:T(8,128)(2,1)}, bf16[1024,4096]{1,0:T(8,128)(2,1)}, u32[]{:S(2)}, u32[]{:S(2)}) collective-permute-start(bf16[1024,4096]{1,0:T(8,128)(2,1)} %all-gather.2.cloned.1.call-done), channel_id=1, source_target_pairs={{0,1},{1,0},{2,3},{3,2},{4,5},{5,4},{6,7},{7,6},{8,9},{9,8},{10,11... | collective-permute-start | bytes 25165832 | tf_op jit(solution)/shard_map/ppermute | solution.py:55
  148.0 10.8 %copy-start.2 = (bf16[8,128,768]{2,1,0:T(8,128)(2,1)}, bf16[8,128,768]{2,1,0:T(8,128)(2,1)S(1)}, u32[]{:S(2)}) copy-start(bf16[8,128,768]{2,1,0:T(8,128)(2,1)S(1)} %convolution_convert_fusion.1) | copy-start | bytes 4718596
  174.6 1.7 copy-start.3
  177.0 11.1 %copy-start.4 = (bf16[1024,768]{0,1:T(8,128)(2,1)S(1)}, bf16[1024,768]{0,1:T(8,128)(2,1)}, u32[]{:S(2)}) copy-start(bf16[1024,768]{0,1:T(8,128)(2,1)} %copy.36) | copy-start | bytes 4718596
  188.1 23.0 %copy-start.6 = (s32[128,8]{0,1:T(8,128)S(1)}, s32[128,8]{0,1:T(8,128)}, u32[]{:S(2)}) copy-start(s32[128,8]{0,1:T(8,128)} %param.8) | copy-start | bytes 12292
  188.1 72.1 %copy-start.1 = (bf16[128,8,768]{2,1,0:T(8,128)(2,1)S(1)}, bf16[128,8,768]{2,1,0:T(8,128)(2,1)}, u32[]{:S(2)}) copy-start(bf16[128,8,768]{2,1,0:T(8,128)(2,1)} %param.5) | copy-start | bytes 4718596
Sparse Core Ops, SparseCore 0:
  9.8 136.2 all-gather.1
  174.7 83.5 reduce-scatter.1

commit v11 on v10

--- a/solution.py
+++ b/solution.py
@@ -50,10 +50,6 @@
         return jnp.roll(jnp.stack(got), lax.axis_index(axis), axis=0)
 
     w_full = ring_gather(ring_gather(w_down[0], "y"), "x")
-    dy_z, w_full, recv_h, recv_meta = lax.optimization_barrier((dy_z, w_full, recv_h, recv_meta))
-    w_full = w_full.reshape(-1, hid_width)
-    dy_pair = lax.ppermute(dy_z, "core", perm=[(c, (c + 1) % n_core) for c in range(n_core)])
-
     my_core = lax.axis_index("core")
     other_core = (my_core + 1) % n_core
 
@@ -76,6 +72,12 @@
 
     p_own, h_own = inputs(my_core)
     p_pair, h_pair = inputs(other_core)
+
+    dy_z, w_full, p_own, h_own, p_pair, h_pair = lax.optimization_barrier(
+        (dy_z, w_full, p_own, h_own, p_pair, h_pair)
+    )
+    w_full = w_full.reshape(-1, hid_width)
+    dy_pair = lax.ppermute(dy_z, "core", perm=[(c, (c + 1) % n_core) for c in range(n_core)])
 
     def part(dy_c, p_c, h_c):
         scaled = (p_c[:, None] * dy_c.astype(jnp.float32)).astype(jnp.bfloat16)

time: 268 us -> 269 us (level)
  waiting for transfers between devices: 123 us -> 119 us
  local copies, waits for them, and re-layouts: 33.2 us -> 36.5 us
    unnamed x28, local copies, waits for them, and re-layouts: 17.8 us -> 21.1 us
  transfers between devices with their start and end apart: 11 -> 11, of which waited for: 5 -> 6; matrix products, arithmetic and copies ran while one was open for 27% -> 29% of each run, Pallas kernels for 0% -> 0%
where the time goes in v11:
time: 269 us; the launch traced here: 268 us
  waiting for transfers between devices  119 us (44%)
  matrix products  50.5 us (19%)
  local copies, waits for them, and re-layouts  36.5 us (14%)
  starting transfers between devices  28.9 us (11%)
  between operations  14.4 us (5%)
  blocking collectives  11.4 us (4%)
  other arithmetic  7.25 us (3%)
    ppermute x6, waiting for transfers between devices, ring_gather(): lax.ppermute(x, axis, perm=[(i, (i - d) % n) for i in range(n)])  54.2 us
    reduce_scatter x1, waiting for transfers between devices, body(): lax.psum_scatter(partial, ('x', 'y'), scatter_dimension=0, tiled=True)  46.7 us
    dot_general x2, matrix products, part(): lax.dot_general(scaled, h_c, (((0,), (0,)), ((), ())), preferred_element_...  25.5 us
    dot_general x2, matrix products, score(): lax.dot_general(dy_c, w_full, (((1,), (0,)), ((), ())), preferred_element...  22.6 us
    unnamed x28, local copies, waits for them, and re-layouts  21.1 us
    all_gather x1, waiting for transfers between devices, body(): dy_z = lax.all_gather(upstream, 'z', axis=0, tiled=True)  17.6 us
    all_to_all x1, blocking collectives, body(): lax.all_to_all(by_source, ez, split_axis=0, concat_axis=0, tiled=True)  11.4 us
    all_to_all x1, starting transfers between devices, body(): lax.all_to_all(send_meta, ez, split_axis=0, concat_axis=0, tiled=True)  9.99 us
  transfers between devices with their start and end apart: 11, of which 6 were waited for; matrix products, arithmetic and copies ran while one was open for 29% of the time, Pallas kernels for 0%

profile of v11, /device:TPU:1, one launch (start us, length us, event | category | flops | bytes accessed | tf_op | source)
XLA Modules:
  0.0 268.1 jit_solution(6632619445155518405)
XLA Ops:
  7.2 0.7 all-gather.2.cloned.1.call-update
  7.9 3.6 %collective-permute-start = (bf16[256,768]{1,0:T(8,128)(2,1)}, bf16[256,768]{1,0:T(8,128)(2,1)S(1)}, u32[]{:S(2)}, u32[]{:S(2)}) collective-permute-start(bf16[256,768]{1,0:T(8,128)(2,1)} %bitcast.81), channel_id=1, source_target_pairs={{0,48},{16,0},{32,16},{48,32},{1,49},{17,1},{33,17},{49,33},{2,50}... | collective-permute-start | bytes 1179656 | tf_op jit(solution)/shard_map/ppermute | solution.py:49
  11.6 0.3 collective-permute-start.1
  11.9 0.7 collective-permute-start.2
  12.6 0.7 select_reduce_fusion.3
  13.3 0.1 copy.29
  13.4 0.7 convert_element_type.67
  14.1 0.7 select_reduce_fusion.4
  14.8 0.1 copy.28
  14.9 0.2 reduce_window_sum.11
  15.1 0.7 copy.31
  15.8 10.0 %all-to-all-start = ((f32[16,2,128]{2,1,0:T(2,128)}), f32[16,2,128]{2,1,0:T(2,128)S(1)}, u32[]{:S(2)}, u32[]{:S(2)}) async-start(f32[16,2,128]{2,1,0:T(2,128)} %copy.31), calls=%async_computation | async-start | bytes 32768 | tf_op jit(solution)/shard_map/all_to_all | solution.py:46
  25.9 0.9 convert_reduce_fusion
  27.0 1.0 constant_dynamic-update-slice_fusion.1
  28.1 4.8 %collective-permute-done.2 = bf16[256,768]{1,0:T(8,128)(2,1)S(1)} collective-permute-done((bf16[256,768]{1,0:T(8,128)(2,1)}, bf16[256,768]{1,0:T(8,128)(2,1)S(1)}, u32[]{:S(2)}, u32[]{:S(2)}) %collective-permute-start.2) | collective-permute-done | bytes 393248 | tf_op jit(solution)/shard_map/ppermute | solution.py:49
  33.0 1.9 bitcast_dynamic-update-slice_fusion.6
  34.9 2.5 collective-permute-start.3
  37.4 0.6 collective-permute-start.4
  38.0 4.6 %gather_fusion = bf16[1152,768]{1,0:T(8,128)(2,1)S(1)} fusion(bf16[1024,768]{1,0:T(8,128)(2,1)S(1)} %bitcast.71, s32[2048]{0:T(1024)S(1)} %pad_clamp_fusion), kind=kCustom, calls=%fused_computation | custom fusion | bytes 3543552 | tf_op jit(solution)/shard_map/gather | solution.py:33
  42.6 0.7 collective-permute-start.5
  43.3 1.5 broadcast_select_fusion
  44.7 9.7 %all-to-all-start.1 = ((bf16[16,72,768]{2,1,0:T(8,128)(2,1)}), bf16[16,72,768]{2,1,0:T(8,128)(2,1)S(1)}, u32[]{:S(2)}, u32[]{:S(2)}) async-start(bf16[16,72,768]{2,1,0:T(8,128)(2,1)} %broadcast_select_fusion), calls=%async_computation.1 | async-start | bytes 3538944 | tf_op jit(solution)/shard_map/all_to_all | solution.py:45
  54.6 17.2 %collective-permute-done.3 = bf16[4,256,768]{2,1,0:T(8,128)(2,1)} collective-permute-done((bf16[4,256,768]{2,1,0:T(8,128)(2,1)}, bf16[4,256,768]{2,1,0:T(8,128)(2,1)}, u32[]{:S(2)}, u32[]{:S(2)}) %collective-permute-start.3) | collective-permute-done | bytes 1572896 | tf_op jit(solution)/shard_map/ppermute | solution.py:49
  71.8 2.7 bitcast_dynamic-update-slice_fusion.4
  74.5 0.2 collective-permute-done.4
  74.6 2.6 bitcast_dynamic-update-slice_fusion.2
  77.3 32.1 %collective-permute-done.5 = bf16[4,256,768]{2,1,0:T(8,128)(2,1)S(1)} collective-permute-done((bf16[4,256,768]{2,1,0:T(8,128)(2,1)}, bf16[4,256,768]{2,1,0:T(8,128)(2,1)S(1)}, u32[]{:S(2)}, u32[]{:S(2)}) %collective-permute-start.5) | collective-permute-done | bytes 1572896 | tf_op jit(solution)/shard_map/ppermute | solution.py:49
  109.4 1.3 bitcast_dynamic-update-slice_fusion
  110.6 2.7 bitcast_dynamic-update-slice_fusion.7
  113.3 2.7 %bitcast_dynamic-update-slice_fusion.5 = bf16[8,4,256,768]{3,2,1,0:T(8,128)(2,1)} fusion(bf16[8,4,256,768]{3,2,1,0:T(8,128)(2,1)} %bitcast_dynamic-update-slice_fusion.7, bf16[4,256,768]{2,1,0:T(8,128)(2,1)} %collective-permute-done.3), kind=kLoop, calls=%fused_computation.18 | loop fusion | bytes 3145728
  116.0 2.7 %bitcast_dynamic-update-slice_fusion.3 = bf16[8,4,256,768]{3,2,1,0:T(8,128)(2,1)} fusion(bf16[8,4,256,768]{3,2,1,0:T(8,128)(2,1)} %bitcast_dynamic-update-slice_fusion.5, bf16[4,256,768]{2,1,0:T(8,128)(2,1)} %collective-permute-done.4), kind=kLoop, calls=%fused_computation.16 | loop fusion | bytes 3145728
  118.7 1.2 bitcast_dynamic-update-slice_fusion.1
  120.0 6.1 %constant_dynamic-slice_fusion.2 = bf16[4,4,256,768]{3,2,1,0:T(8,128)(2,1)} fusion(bf16[8,4,256,768]{3,2,1,0:T(8,128)(2,1)} %bitcast_dynamic-update-slice_fusion.1, s32[]{:T(128)S(6)} %select_n.102), kind=kLoop, calls=%fused_computation.71 | loop fusion | bytes 12582916 | tf_op jit(solution)/shard_map/jit(_roll_dynamic)/dynamic_slice | solution.py:50
  126.0 0.6 convolution_convert_fusion
  126.6 1.8 convolution_convert_fusion.1
  128.4 17.6 %all-gather.2.cloned.1.call-done = bf16[1024,4096]{1,0:T(8,128)(2,1)} async-done(((bf16[128,4096]{1,0:T(8,128)(2,1)}), bf16[1024,4096]{1,0:T(8,128)(2,1)}) %all-gather.2.cloned.1.call-update) | async-done | bytes 8388624 | tf_op jit(solution)/shard_map/all_gather | solution.py:44
  146.1 0.7 collective-permute-start.6
  146.7 13.0 %fusion = f32[4096,768]{1,0:T(8,128)} fusion(bf16[1024,768]{1,0:T(8,128)(2,1)} %bitcast.79, bf16[1024,4096]{1,0:T(8,128)(2,1)} %all-gather.2.cloned.1.call-done, f32[1024]{0:T(1024)S(1)} %get-tuple-element.8), kind=kOutput, calls=%fused_computation.4 | convolution fusion | flops 6455033856 | bytes 22548480 | tf_op jit(solution)/shard_map/dot_general | solution.py:84
  159.8 3.3 %copy-done.6 = bf16[1024,4096]{1,0:T(8,128)(2,1)} copy-done((bf16[1024,4096]{1,0:T(8,128)(2,1)}, bf16[1024,4096]{1,0:T(8,128)(2,1)S(1)}, u32[]{:S(2)}) %copy-start.6) | copy-done | bytes 8388632
  163.1 12.4 %add_convert_fusion = bf16[4096,768]{1,0:T(8,128)(2,1)} fusion(f32[4096,768]{1,0:T(8,128)} %fusion, bf16[1024,768]{1,0:T(8,128)(2,1)S(1)} %bitcast.77, bf16[1024,4096]{1,0:T(8,128)(2,1)S(1)} %collective-permute-done.6, f32[1024]{0:T(1024)S(1)} %get-tuple-element.11), kind=kOutput, calls=%fused_computation.3 | convolution fusion | flops 6461325312 | bytes 28839936 | tf_op jit(solution)/shard_map/dot_general | solution.py:84
  175.5 1.7 copy.36
  177.2 0.7 copy.35
  178.0 11.1 %multiply_reduce_fusion.1 = f32[1024]{0:T(1024)S(1)} fusion(bf16[1024,768]{0,1:T(8,128)(2,1)S(1)} %copy.35, bf16[1024,4096]{1,0:T(8,128)(2,1)} %all-gather.2.cloned.1.call-done, bf16[4096,768]{1,0:T(8,128)(2,1)} %bitcast.75), kind=kOutput, calls=%fused_computation.9 | convolution fusion | flops 6444809216 | bytes 16257024 | tf_op jit(solution)/shard_map/dot_general | solution.py:87
  189.1 11.5 %multiply_reduce_fusion = f32[1024]{0:T(1024)S(1)} fusion(bf16[1024,768]{0,1:T(8,128)(2,1)S(1)} %copy-done.3, bf16[1024,4096]{1,0:T(8,128)(2,1)} %copy-done.6, bf16[4096,768]{1,0:T(8,128)(2,1)} %bitcast.76), kind=kOutput, calls=%fused_computation.8 | convolution fusion | flops 6444809216 | bytes 16257024 | tf_op jit(solution)/shard_map/dot_general | solution.py:87
  200.7 11.4 %all_to_all.22 = f32[16,1,128]{2,1,0:T(1,128)S(1)} all-to-all(f32[16,1,128]{2,1,0:T(1,128)S(1)} %bitcast.86), channel_id=1, replica_groups=mesh['x'=4,'y'=4,'z'=8,'core'=2] {'z','core'}, dimensions={0} | all-to-all | bytes 16384 | tf_op jit(solution)/shard_map/all_to_all | solution.py:98
  212.0 0.6 select_reduce_fusion.2
  212.6 46.7 %reduce-scatter.2.cloned.1.call-done = bf16[256,768]{1,0:T(8,128)(2,1)} async-done(((bf16[4096,768]{1,0:T(8,128)(2,1)}), bf16[256,768]{1,0:T(8,128)(2,1)}) %reduce-scatter.2.cloned.1.call-update) | async-done | bytes 393232 | tf_op jit(solution)/shard_map/reduce_scatter | solution.py:91
  259.3 1.9 bitcast_convert_fusion
  (43 shorter events, 0.7 us)
Async XLA Ops:
  7.2 30.9 %copy-start = (bf16[128,8,768]{2,1,0:T(8,128)(2,1)S(1)}, bf16[128,8,768]{2,1,0:T(8,128)(2,1)}, u32[]{:S(2)}) copy-start(bf16[128,8,768]{2,1,0:T(8,128)(2,1)} %param.5) | copy-start | bytes 4718596
  7.2 25.7 %copy-start.4 = (bf16[1,256,768]{2,1,0:T(8,128)(2,1)S(1)}, bf16[1,256,768]{2,1,0:T(8,128)(2,1)}, u32[]{:S(2)}) copy-start(bf16[1,256,768]{2,1,0:T(8,128)(2,1)} %param.9) | copy-start | bytes 1179652
  7.2 138.9 %all-gather.2.cloned.1.call-start = ((), (), s32[]{:S(2)}) async-start(), calls=%async_computation.4 | async-start | bytes 9437184 | tf_op jit(solution)/shard_map/all_gather | solution.py:44
  7.9 20.1 %collective-permute-start = (bf16[256,768]{1,0:T(8,128)(2,1)}, bf16[256,768]{1,0:T(8,128)(2,1)S(1)}, u32[]{:S(2)}, u32[]{:S(2)}) collective-permute-start(bf16[256,768]{1,0:T(8,128)(2,1)} %bitcast.81), channel_id=1, source_target_pairs={{0,48},{16,0},{32,16},{48,32},{1,49},{17,1},{33,17},{49,33},{2,50}... | collective-permute-start | bytes 1179656 | tf_op jit(solution)/shard_map/ppermute | solution.py:49
  11.6 16.5 %collective-permute-start.1 = (bf16[256,768]{1,0:T(8,128)(2,1)}, bf16[256,768]{1,0:T(8,128)(2,1)S(1)}, u32[]{:S(2)}, u32[]{:S(2)}) collective-permute-start(bf16[256,768]{1,0:T(8,128)(2,1)} %bitcast.82), channel_id=1, source_target_pairs={{0,32},{16,48},{32,0},{48,16},{1,33},{17,49},{33,1},{49,17},{2,34}... | collective-permute-start | bytes 1179656 | tf_op jit(solution)/shard_map/ppermute | solution.py:49
  11.9 20.9 %collective-permute-start.2 = (bf16[256,768]{1,0:T(8,128)(2,1)}, bf16[256,768]{1,0:T(8,128)(2,1)S(1)}, u32[]{:S(2)}, u32[]{:S(2)}) collective-permute-start(bf16[256,768]{1,0:T(8,128)(2,1)} %bitcast.83), channel_id=1, source_target_pairs={{0,16},{16,32},{32,48},{48,0},{1,17},{17,33},{33,49},{49,1},{2,18}... | collective-permute-start | bytes 1179656 | tf_op jit(solution)/shard_map/ppermute | solution.py:49
  15.8 28.9 %all-to-all-start = ((f32[16,2,128]{2,1,0:T(2,128)}), f32[16,2,128]{2,1,0:T(2,128)S(1)}, u32[]{:S(2)}, u32[]{:S(2)}) async-start(f32[16,2,128]{2,1,0:T(2,128)} %copy.31), calls=%async_computation | async-start | bytes 32768 | tf_op jit(solution)/shard_map/all_to_all | solution.py:46
  34.9 36.9 %collective-permute-start.3 = (bf16[4,256,768]{2,1,0:T(8,128)(2,1)}, bf16[4,256,768]{2,1,0:T(8,128)(2,1)}, u32[]{:S(2)}, u32[]{:S(2)}) collective-permute-start(bf16[4,256,768]{2,1,0:T(8,128)(2,1)} %get-tuple-element.22), channel_id=1, source_target_pairs={{0,192},{64,0},{128,64},{192,128},{1,193},{65,1},{129,65},{193,129... | collective-permute-start | bytes 4718600 | tf_op jit(solution)/shard_map/ppermute | solution.py:49
  37.4 37.2 %collective-permute-start.4 = (bf16[4,256,768]{2,1,0:T(8,128)(2,1)}, bf16[4,256,768]{2,1,0:T(8,128)(2,1)}, u32[]{:S(2)}, u32[]{:S(2)}) collective-permute-start(bf16[4,256,768]{2,1,0:T(8,128)(2,1)} %get-tuple-element.22), channel_id=1, source_target_pairs={{0,128},{64,192},{128,0},{192,64},{1,129},{65,193},{129,1},{193,65... | collective-permute-start | bytes 4718600 | tf_op jit(solution)/shard_map/ppermute | solution.py:49
  42.6 66.7 %collective-permute-start.5 = (bf16[4,256,768]{2,1,0:T(8,128)(2,1)}, bf16[4,256,768]{2,1,0:T(8,128)(2,1)S(1)}, u32[]{:S(2)}, u32[]{:S(2)}) collective-permute-start(bf16[4,256,768]{2,1,0:T(8,128)(2,1)} %get-tuple-element.22), channel_id=1, source_target_pairs={{0,64},{64,128},{128,192},{192,0},{1,65},{65,129},{129,193},{193,1... | collective-permute-start | bytes 4718600 | tf_op jit(solution)/shard_map/ppermute | solution.py:49
  44.7 81.3 %all-to-all-start.1 = ((bf16[16,72,768]{2,1,0:T(8,128)(2,1)}), bf16[16,72,768]{2,1,0:T(8,128)(2,1)S(1)}, u32[]{:S(2)}, u32[]{:S(2)}) async-start(bf16[16,72,768]{2,1,0:T(8,128)(2,1)} %broadcast_select_fusion), calls=%async_computation.1 | async-start | bytes 3538944 | tf_op jit(solution)/shard_map/all_to_all | solution.py:45
  54.5 204.8 %reduce-scatter.2.cloned.1.call-start = ((), (), s32[]{:S(2)}) async-start(), calls=%async_computation.5 | async-start | bytes 6684672 | tf_op jit(solution)/shard_map/reduce_scatter | solution.py:91
  146.1 13.7 %collective-permute-start.6 = (bf16[1024,4096]{1,0:T(8,128)(2,1)}, bf16[1024,4096]{1,0:T(8,128)(2,1)S(1)}, u32[]{:S(2)}, u32[]{:S(2)}) collective-permute-start(bf16[1024,4096]{1,0:T(8,128)(2,1)} %all-gather.2.cloned.1.call-done), channel_id=1, source_target_pairs={{0,1},{1,0},{2,3},{3,2},{4,5},{5,4},{6,7},{7,6},{8,9},{9,8},{10,11... | collective-permute-start | bytes 25165832 | tf_op jit(solution)/shard_map/ppermute | solution.py:80
  159.8 3.3 %copy-start.6 = (bf16[1024,4096]{1,0:T(8,128)(2,1)}, bf16[1024,4096]{1,0:T(8,128)(2,1)S(1)}, u32[]{:S(2)}) copy-start(bf16[1024,4096]{1,0:T(8,128)(2,1)S(1)} %collective-permute-done.6) | copy-start | bytes 25165828
  175.5 1.7 copy-start.2
  177.9 11.1 %copy-start.3 = (bf16[1024,768]{0,1:T(8,128)(2,1)S(1)}, bf16[1024,768]{0,1:T(8,128)(2,1)}, u32[]{:S(2)}) copy-start(bf16[1024,768]{0,1:T(8,128)(2,1)} %copy.36) | copy-start | bytes 4718596
  189.1 22.9 %copy-start.5 = (s32[128,8]{0,1:T(8,128)S(1)}, s32[128,8]{0,1:T(8,128)}, u32[]{:S(2)}) copy-start(s32[128,8]{0,1:T(8,128)} %param.8) | copy-start | bytes 12292
  189.1 72.1 %copy-start.1 = (bf16[128,8,768]{2,1,0:T(8,128)(2,1)S(1)}, bf16[128,8,768]{2,1,0:T(8,128)(2,1)}, u32[]{:S(2)}) copy-start(bf16[128,8,768]{2,1,0:T(8,128)(2,1)} %param.5) | copy-start | bytes 4718596
Sparse Core Ops, SparseCore 0:
  9.8 136.2 all-gather.1
  175.6 83.6 reduce-scatter.1

commit v12 on v10

--- a/solution.py
+++ b/solution.py
@@ -42,7 +42,14 @@
     send_meta = jnp.stack([p_tok.T, inv.T], axis=1)
 
     dy_z = lax.all_gather(upstream, "z", axis=0, tiled=True)
-    recv_h = lax.all_to_all(send_h, ez, split_axis=0, concat_axis=0, tiled=True)
+    mine = lax.axis_index("core")
+    by_core = send_h.reshape(n_z, n_core, slots_per, hid_width)
+    for_pair = lax.dynamic_index_in_dim(by_core, (mine + 1) % n_core, axis=1, keepdims=False)
+    for_me = lax.dynamic_index_in_dim(by_core, mine, axis=1, keepdims=False)
+    from_pair = lax.ppermute(for_pair, "core", perm=[(c, (c + 1) % n_core) for c in range(n_core)])
+    recv_h = lax.all_to_all(
+        jnp.stack([for_me, from_pair], axis=1), "z", split_axis=0, concat_axis=0, tiled=True
+    )
     recv_meta = lax.all_to_all(send_meta, ez, split_axis=0, concat_axis=0, tiled=True)
     def ring_gather(x, axis):
         n = lax.axis_size(axis)
@@ -57,15 +64,13 @@
     my_core = lax.axis_index("core")
     other_core = (my_core + 1) % n_core
 
-    def inputs(c):
+    def inputs(c, own):
         meta = lax.dynamic_index_in_dim(
             recv_meta.reshape(n_z, n_core, 2, tok_rows), c, axis=1, keepdims=False
         )
         p_c = meta[:, 0, :].reshape(-1)
         slot = meta[:, 1, :].astype(jnp.int32)
-        h_src = lax.dynamic_index_in_dim(
-            recv_h.reshape(n_z, n_core, slots_per, hid_width), c, axis=1, keepdims=False
-        )
+        h_src = recv_h[:, 0] if own else recv_h[:, 1]
         pick = (slot[:, :, None] == jnp.arange(slots_per, dtype=jnp.int32)[None, None, :]).astype(
             h_src.dtype
         )
@@ -74,8 +79,8 @@
         ).astype(h_src.dtype)
         return p_c, h_c.reshape(n_z * tok_rows, hid_width)
 
-    p_own, h_own = inputs(my_core)
-    p_pair, h_pair = inputs(other_core)
+    p_own, h_own = inputs(my_core, True)
+    p_pair, h_pair = inputs(other_core, False)
 
     def part(dy_c, p_c, h_c):
         scaled = (p_c[:, None] * dy_c.astype(jnp.float32)).astype(jnp.bfloat16)

time: 268 us -> 272 us (1.015)
  local copies, waits for them, and re-layouts: 33.2 us -> 45.4 us
  waiting for transfers between devices: 123 us -> 117 us
  starting transfers between devices: 28.9 us -> 24 us
    ppermute x6, waiting for transfers between devices: 54.9 us -> 47.9 us  [ring_gather(): lax.ppermute(x, axis, perm=[(i, (i - d) % n) for i in range(n)])]
    unnamed x28 -> x32, local copies, waits for them, and re-layouts: 17.8 us -> 24.6 us
    all_to_all x1, starting transfers between devices: 9.71 us -> 3.6 us  [body(): lax.all_to_all(jnp.stack([for_me, from_pair], axis=1), 'z', split_axis=0,...]
    all_to_all x1, waiting for transfers between devices: 0.01 us -> 6 us  [body(): lax.all_to_all(send_meta, ez, split_axis=0, concat_axis=0, tiled=True)]
    all_gather x1, waiting for transfers between devices: 19.4 us -> 15.6 us  [body(): dy_z = lax.all_gather(upstream, 'z', axis=0, tiled=True)]
  transfers between devices with their start and end apart: 11 -> 12, of which waited for: 5 -> 8; matrix products, arithmetic and copies ran while one was open for 27% -> 32% of each run, Pallas kernels for 0% -> 0%
where the time goes in v12:
time: 272 us; the launch traced here: 271 us
  waiting for transfers between devices  117 us (43%)
  matrix products  51.6 us (19%)
  local copies, waits for them, and re-layouts  45.4 us (17%)
  starting transfers between devices  24 us (9%)
  between operations  14.3 us (5%)
  blocking collectives  11.2 us (4%)
  other arithmetic  8.1 us (3%)
    ppermute x6, waiting for transfers between devices, ring_gather(): lax.ppermute(x, axis, perm=[(i, (i - d) % n) for i in range(n)])  47.9 us
    reduce_scatter x1, waiting for transfers between devices, body(): lax.psum_scatter(partial, ('x', 'y'), scatter_dimension=0, tiled=True)  46.7 us
    dot_general x2, matrix products, part(): lax.dot_general(scaled, h_c, (((0,), (0,)), ((), ())), preferred_element_...  27.8 us
    unnamed x32, local copies, waits for them, and re-layouts  24.6 us
    dot_general x2, matrix products, score(): lax.dot_general(dy_c, w_full, (((1,), (0,)), ((), ())), preferred_element...  22.6 us
    all_gather x1, waiting for transfers between devices, body(): dy_z = lax.all_gather(upstream, 'z', axis=0, tiled=True)  15.6 us
    all_to_all x1, blocking collectives, body(): lax.all_to_all(by_source, ez, split_axis=0, concat_axis=0, tiled=True)  11.2 us
    all_to_all x1, starting transfers between devices, body(): lax.all_to_all(send_meta, ez, split_axis=0, concat_axis=0, tiled=True)  9.8 us
  transfers between devices with their start and end apart: 12, of which 8 were waited for; matrix products, arithmetic and copies ran while one was open for 32% of the time, Pallas kernels for 0%

profile of v12, /device:TPU:1, one launch (start us, length us, event | category | flops | bytes accessed | tf_op | source)
XLA Modules:
  0.0 271.5 jit_solution(3712684910375143976)
XLA Ops:
  7.2 0.7 all-gather.2.cloned.1.call-update
  7.9 3.6 %collective-permute-start = (bf16[256,768]{1,0:T(8,128)(2,1)}, bf16[256,768]{1,0:T(8,128)(2,1)}, u32[]{:S(2)}, u32[]{:S(2)}) collective-permute-start(bf16[256,768]{1,0:T(8,128)(2,1)} %bitcast.81), channel_id=1, source_target_pairs={{0,48},{16,0},{32,16},{48,32},{1,49},{17,1},{33,17},{49,33},{2,50}... | collective-permute-start | bytes 1179656 | tf_op jit(solution)/shard_map/ppermute | solution.py:56
  11.9 0.7 collective-permute-start.2
  12.6 0.7 convert_reduce_fusion.1
  13.7 0.9 convert_reduce_fusion
  14.8 4.6 %gather_fusion = bf16[1152,768]{1,0:T(8,128)(2,1)S(1)} fusion(bf16[1024,768]{1,0:T(8,128)(2,1)S(1)} %bitcast.73, s32[2048]{0:T(1024)S(1)} %pad_clamp_fusion), kind=kCustom, calls=%fused_computation | custom fusion | bytes 3543552 | tf_op jit(solution)/shard_map/gather | solution.py:33
  19.4 1.5 broadcast_select_fusion
  20.9 2.5 constant_dynamic-slice_fusion.1
  23.3 1.5 collective-permute-start.6
  24.9 3.1 %collective-permute-done = bf16[256,768]{1,0:T(8,128)(2,1)} collective-permute-done((bf16[256,768]{1,0:T(8,128)(2,1)}, bf16[256,768]{1,0:T(8,128)(2,1)}, u32[]{:S(2)}, u32[]{:S(2)}) %collective-permute-start) | collective-permute-done | bytes 393248 | tf_op jit(solution)/shard_map/ppermute | solution.py:56
  27.9 1.0 bitcast_dynamic-update-slice_fusion.12
  29.0 1.0 bitcast_dynamic-update-slice_fusion.10
  30.0 2.8 %collective-permute-done.2 = bf16[256,768]{1,0:T(8,128)(2,1)} collective-permute-done((bf16[256,768]{1,0:T(8,128)(2,1)}, bf16[256,768]{1,0:T(8,128)(2,1)}, u32[]{:S(2)}, u32[]{:S(2)}) %collective-permute-start.2) | collective-permute-done | bytes 393248 | tf_op jit(solution)/shard_map/ppermute | solution.py:56
  32.8 1.0 bitcast_dynamic-update-slice_fusion.8
  33.9 1.0 bitcast_dynamic-update-slice_fusion.13
  35.0 1.0 bitcast_dynamic-update-slice_fusion.11
  36.0 1.0 bitcast_dynamic-update-slice_fusion.9
  37.0 1.4 bitcast_dynamic-update-slice_fusion.6
  38.4 2.5 collective-permute-start.3
  41.4 0.7 copy.36
  42.8 0.9 pad_maximum_fusion.1
  43.6 0.7 copy.37
  44.3 9.8 %all-to-all-start.1 = ((f32[16,2,128]{2,1,0:T(2,128)}), f32[16,2,128]{2,1,0:T(2,128)S(1)}, u32[]{:S(2)}, u32[]{:S(2)}) async-start(f32[16,2,128]{2,1,0:T(2,128)} %copy.37), calls=%async_computation.1 | async-start | bytes 32768 | tf_op jit(solution)/shard_map/all_to_all | solution.py:53
  54.1 1.4 pad_maximum_fusion
  55.5 6.0 %all-to-all-done.1 = f32[16,2,128]{2,1,0:T(2,128)S(1)} async-done(((f32[16,2,128]{2,1,0:T(2,128)}), f32[16,2,128]{2,1,0:T(2,128)S(1)}, u32[]{:S(2)}, u32[]{:S(2)}) %all-to-all-start.1) | async-done | bytes 16416 | tf_op jit(solution)/shard_map/all_to_all | solution.py:53
  61.5 3.6 %all-to-all-start = ((bf16[8,2,72,768]{3,2,1,0:T(8,128)(2,1)}), bf16[8,2,72,768]{3,2,1,0:T(8,128)(2,1)S(1)}, u32[]{:S(2)}, u32[]{:S(2)}) async-start(bf16[8,2,72,768]{3,2,1,0:T(8,128)(2,1)} %pad_maximum_fusion), calls=%async_computation | async-start | bytes 3538944 | tf_op jit(solution)/shard_map/all_to_all | solution.py:50
  65.2 9.8 %collective-permute-done.3 = bf16[4,256,768]{2,1,0:T(8,128)(2,1)} collective-permute-done((bf16[4,256,768]{2,1,0:T(8,128)(2,1)S(1)}, bf16[4,256,768]{2,1,0:T(8,128)(2,1)}, u32[]{:S(2)}, u32[]{:S(2)}) %collective-permute-start.3) | collective-permute-done | bytes 1572896 | tf_op jit(solution)/shard_map/ppermute | solution.py:56
  74.9 2.7 bitcast_dynamic-update-slice_fusion.4
  77.7 2.7 bitcast_dynamic-update-slice_fusion.2
  80.3 32.2 %collective-permute-done.5 = bf16[4,256,768]{2,1,0:T(8,128)(2,1)} collective-permute-done((bf16[4,256,768]{2,1,0:T(8,128)(2,1)S(1)}, bf16[4,256,768]{2,1,0:T(8,128)(2,1)}, u32[]{:S(2)}, u32[]{:S(2)}) %collective-permute-start.5) | collective-permute-done | bytes 1572896 | tf_op jit(solution)/shard_map/ppermute | solution.py:56
  112.5 2.7 bitcast_dynamic-update-slice_fusion
  115.2 1.2 bitcast_dynamic-update-slice_fusion.7
  116.4 2.7 %bitcast_dynamic-update-slice_fusion.5 = bf16[8,4,256,768]{3,2,1,0:T(8,128)(2,1)} fusion(bf16[8,4,256,768]{3,2,1,0:T(8,128)(2,1)} %bitcast_dynamic-update-slice_fusion.7, bf16[4,256,768]{2,1,0:T(8,128)(2,1)} %collective-permute-done.3), kind=kLoop, calls=%fused_computation.19 | loop fusion | bytes 3145728
  119.2 2.7 bitcast_dynamic-update-slice_fusion.3
  121.9 2.7 bitcast_dynamic-update-slice_fusion.1
  124.5 6.0 %constant_dynamic-slice_fusion.3 = bf16[4,4,256,768]{3,2,1,0:T(8,128)(2,1)} fusion(bf16[8,4,256,768]{3,2,1,0:T(8,128)(2,1)} %bitcast_dynamic-update-slice_fusion.1, s32[]{:T(128)S(6)} %select_n.105), kind=kLoop, calls=%fused_computation.70 | loop fusion | bytes 12582916 | tf_op jit(solution)/shard_map/jit(_roll_dynamic)/dynamic_slice | solution.py:57
  130.5 15.6 %all-gather.2.cloned.1.call-done = bf16[1024,4096]{1,0:T(8,128)(2,1)} async-done(((bf16[128,4096]{1,0:T(8,128)(2,1)}), bf16[1024,4096]{1,0:T(8,128)(2,1)}) %all-gather.2.cloned.1.call-update) | async-done | bytes 8388624 | tf_op jit(solution)/shard_map/all_gather | solution.py:44
  146.1 0.7 collective-permute-start.7
  148.0 15.3 %fusion = f32[4096,768]{1,0:T(8,128)} fusion(bf16[1024,768]{1,0:T(8,128)(2,1)S(1)} %bitcast.79, bf16[1024,4096]{1,0:T(8,128)(2,1)} %all-gather.2.cloned.1.call-done, f32[1024]{0:T(1024)S(1)} %get-tuple-element.28), kind=kOutput, calls=%fused_computation.4 | convolution fusion | flops 6455033856 | bytes 22548480 | tf_op jit(solution)/shard_map/dot_general | solution.py:87
  163.3 3.3 %copy-done.8 = bf16[1024,4096]{1,0:T(8,128)(2,1)} copy-done((bf16[1024,4096]{1,0:T(8,128)(2,1)}, bf16[1024,4096]{1,0:T(8,128)(2,1)S(1)}, u32[]{:S(2)}) %copy-start.8) | copy-done | bytes 8388632
  166.6 12.5 %add_convert_fusion = bf16[4096,768]{1,0:T(8,128)(2,1)} fusion(f32[4096,768]{1,0:T(8,128)} %fusion, bf16[1024,768]{1,0:T(8,128)(2,1)S(1)} %bitcast.77, bf16[1024,4096]{1,0:T(8,128)(2,1)S(1)} %collective-permute-done.7, f32[1024]{0:T(1024)S(1)} %get-tuple-element.26), kind=kOutput, calls=%fused_computation.3 | convolution fusion | flops 6461325312 | bytes 28839936 | tf_op jit(solution)/shard_map/dot_general | solution.py:87
  179.1 1.6 copy.42
  180.8 0.7 copy.41
  181.5 11.1 %multiply_reduce_fusion.1 = f32[1024]{0:T(1024)S(1)} fusion(bf16[1024,768]{0,1:T(8,128)(2,1)S(1)} %copy.41, bf16[1024,4096]{1,0:T(8,128)(2,1)} %all-gather.2.cloned.1.call-done, bf16[4096,768]{1,0:T(8,128)(2,1)} %bitcast.75), kind=kOutput, calls=%fused_computation.9 | convolution fusion | flops 6444809216 | bytes 16257024 | tf_op jit(solution)/shard_map/dot_general | solution.py:90
  192.7 11.5 %multiply_reduce_fusion = f32[1024]{0:T(1024)S(1)} fusion(bf16[1024,768]{0,1:T(8,128)(2,1)S(1)} %copy-done.4, bf16[1024,4096]{1,0:T(8,128)(2,1)} %copy-done.8, bf16[4096,768]{1,0:T(8,128)(2,1)} %bitcast.76), kind=kOutput, calls=%fused_computation.8 | convolution fusion | flops 6444809216 | bytes 16257024 | tf_op jit(solution)/shard_map/dot_general | solution.py:90
  204.2 11.2 %all_to_all.22 = f32[16,1,128]{2,1,0:T(1,128)S(1)} all-to-all(f32[16,1,128]{2,1,0:T(1,128)S(1)} %bitcast.87), channel_id=1, replica_groups=mesh['x'=4,'y'=4,'z'=8,'core'=2] {'z','core'}, dimensions={0} | all-to-all | bytes 16384 | tf_op jit(solution)/shard_map/all_to_all | solution.py:101
  216.0 46.7 %reduce-scatter.2.cloned.1.call-done = bf16[256,768]{1,0:T(8,128)(2,1)} async-done(((bf16[4096,768]{1,0:T(8,128)(2,1)}), bf16[256,768]{1,0:T(8,128)(2,1)}) %reduce-scatter.2.cloned.1.call-update) | async-done | bytes 393232 | tf_op jit(solution)/shard_map/reduce_scatter | solution.py:94
  262.7 1.9 bitcast_convert_fusion
  (53 shorter events, 4.2 us)
Async XLA Ops:
  7.2 7.7 %copy-start = (bf16[128,8,768]{2,1,0:T(8,128)(2,1)S(1)}, bf16[128,8,768]{2,1,0:T(8,128)(2,1)}, u32[]{:S(2)}) copy-start(bf16[128,8,768]{2,1,0:T(8,128)(2,1)} %param.5) | copy-start | bytes 4718596
  7.2 138.9 %all-gather.2.cloned.1.call-start = ((), (), s32[]{:S(2)}) async-start(), calls=%async_computation.4 | async-start | bytes 9437184 | tf_op jit(solution)/shard_map/all_gather | solution.py:44
  7.9 20.0 %collective-permute-start = (bf16[256,768]{1,0:T(8,128)(2,1)}, bf16[256,768]{1,0:T(8,128)(2,1)}, u32[]{:S(2)}, u32[]{:S(2)}) collective-permute-start(bf16[256,768]{1,0:T(8,128)(2,1)} %bitcast.81), channel_id=1, source_target_pairs={{0,48},{16,0},{32,16},{48,32},{1,49},{17,1},{33,17},{49,33},{2,50}... | collective-permute-start | bytes 1179656 | tf_op jit(solution)/shard_map/ppermute | solution.py:56
  11.6 17.4 %collective-permute-start.1 = (bf16[256,768]{1,0:T(8,128)(2,1)}, bf16[256,768]{1,0:T(8,128)(2,1)}, u32[]{:S(2)}, u32[]{:S(2)}) collective-permute-start(bf16[256,768]{1,0:T(8,128)(2,1)} %bitcast.82), channel_id=1, source_target_pairs={{0,32},{16,48},{32,0},{48,16},{1,33},{17,49},{33,1},{49,17},{2,34}... | collective-permute-start | bytes 1179656 | tf_op jit(solution)/shard_map/ppermute | solution.py:56
  11.9 20.9 %collective-permute-start.2 = (bf16[256,768]{1,0:T(8,128)(2,1)}, bf16[256,768]{1,0:T(8,128)(2,1)}, u32[]{:S(2)}, u32[]{:S(2)}) collective-permute-start(bf16[256,768]{1,0:T(8,128)(2,1)} %bitcast.83), channel_id=1, source_target_pairs={{0,16},{16,32},{32,48},{48,0},{1,17},{17,33},{33,49},{49,1},{2,18}... | collective-permute-start | bytes 1179656 | tf_op jit(solution)/shard_map/ppermute | solution.py:56
  19.4 5.5 %copy-start.5 = (bf16[1,256,768]{2,1,0:T(8,128)(2,1)S(1)}, bf16[1,256,768]{2,1,0:T(8,128)(2,1)}, u32[]{:S(2)}) copy-start(bf16[1,256,768]{2,1,0:T(8,128)(2,1)} %param.9) | copy-start | bytes 1179652
  23.3 30.8 %collective-permute-start.6 = (bf16[8,72,768]{2,1,0:T(8,128)(2,1)}, bf16[8,72,768]{2,1,0:T(8,128)(2,1)S(1)}, u32[]{:S(2)}, u32[]{:S(2)}) collective-permute-start(bf16[8,72,768]{2,1,0:T(8,128)(2,1)} %get-tuple-element.20), channel_id=1, source_target_pairs={{0,1},{1,0},{2,3},{3,2},{4,5},{5,4},{6,7},{7,6},{8,9},{9,8},{10,11... | collective-permute-start | bytes 2654216 | tf_op jit(solution)/shard_map/ppermute | solution.py:49
  34.9 6.5 %copy-start.7 = (bf16[128,8]{0,1:T(8,128)(2,1)S(1)}, bf16[128,8]{0,1:T(8,128)(2,1)}, u32[]{:S(2)}) copy-start(bf16[128,8]{0,1:T(8,128)(2,1)} %param.7) | copy-start | bytes 6148
  34.9 6.5 %copy-start.6 = (s32[128,8]{0,1:T(8,128)S(1)}, s32[128,8]{0,1:T(8,128)}, u32[]{:S(2)}) copy-start(s32[128,8]{0,1:T(8,128)} %param.8) | copy-start | bytes 12292
  38.4 36.5 %collective-permute-start.3 = (bf16[4,256,768]{2,1,0:T(8,128)(2,1)S(1)}, bf16[4,256,768]{2,1,0:T(8,128)(2,1)}, u32[]{:S(2)}, u32[]{:S(2)}) collective-permute-start(bf16[4,256,768]{2,1,0:T(8,128)(2,1)S(1)} %get-tuple-element.18), channel_id=1, source_target_pairs={{0,192},{64,0},{128,64},{192,128},{1,193},{65,1},{129,65},{193,129... | collective-permute-start | bytes 4718600 | tf_op jit(solution)/shard_map/ppermute | solution.py:56
  40.9 36.8 %collective-permute-start.4 = (bf16[4,256,768]{2,1,0:T(8,128)(2,1)S(1)}, bf16[4,256,768]{2,1,0:T(8,128)(2,1)}, u32[]{:S(2)}, u32[]{:S(2)}) collective-permute-start(bf16[4,256,768]{2,1,0:T(8,128)(2,1)S(1)} %get-tuple-element.18), channel_id=1, source_target_pairs={{0,128},{64,192},{128,0},{192,64},{1,129},{65,193},{129,1},{193,65... | collective-permute-start | bytes 4718600 | tf_op jit(solution)/shard_map/ppermute | solution.py:56
  42.2 70.4 %collective-permute-start.5 = (bf16[4,256,768]{2,1,0:T(8,128)(2,1)S(1)}, bf16[4,256,768]{2,1,0:T(8,128)(2,1)}, u32[]{:S(2)}, u32[]{:S(2)}) collective-permute-start(bf16[4,256,768]{2,1,0:T(8,128)(2,1)S(1)} %get-tuple-element.18), channel_id=1, source_target_pairs={{0,64},{64,128},{128,192},{192,0},{1,65},{65,129},{129,193},{193,1... | collective-permute-start | bytes 4718600 | tf_op jit(solution)/shard_map/ppermute | solution.py:56
  44.3 17.2 %all-to-all-start.1 = ((f32[16,2,128]{2,1,0:T(2,128)}), f32[16,2,128]{2,1,0:T(2,128)S(1)}, u32[]{:S(2)}, u32[]{:S(2)}) async-start(f32[16,2,128]{2,1,0:T(2,128)} %copy.37), calls=%async_computation.1 | async-start | bytes 32768 | tf_op jit(solution)/shard_map/all_to_all | solution.py:53
  61.5 69.0 %all-to-all-start = ((bf16[8,2,72,768]{3,2,1,0:T(8,128)(2,1)}), bf16[8,2,72,768]{3,2,1,0:T(8,128)(2,1)S(1)}, u32[]{:S(2)}, u32[]{:S(2)}) async-start(bf16[8,2,72,768]{3,2,1,0:T(8,128)(2,1)} %pad_maximum_fusion), calls=%async_computation | async-start | bytes 3538944 | tf_op jit(solution)/shard_map/all_to_all | solution.py:50
  65.1 197.6 %reduce-scatter.2.cloned.1.call-start = ((), (), s32[]{:S(2)}) async-start(), calls=%async_computation.5 | async-start | bytes 6684672 | tf_op jit(solution)/shard_map/reduce_scatter | solution.py:94
  146.1 17.3 %collective-permute-start.7 = (bf16[1024,4096]{1,0:T(8,128)(2,1)}, bf16[1024,4096]{1,0:T(8,128)(2,1)S(1)}, u32[]{:S(2)}, u32[]{:S(2)}) collective-permute-start(bf16[1024,4096]{1,0:T(8,128)(2,1)} %all-gather.2.cloned.1.call-done), channel_id=1, source_target_pairs={{0,1},{1,0},{2,3},{3,2},{4,5},{5,4},{6,7},{7,6},{8,9},{9,8},{10,11... | collective-permute-start | bytes 25165832 | tf_op jit(solution)/shard_map/ppermute | solution.py:62
  148.0 15.3 %copy-start.2 = (bf16[8,128,768]{2,1,0:T(8,128)(2,1)}, bf16[8,128,768]{2,1,0:T(8,128)(2,1)S(1)}, u32[]{:S(2)}) copy-start(bf16[8,128,768]{2,1,0:T(8,128)(2,1)S(1)} %convolution_convert_fusion.1) | copy-start | bytes 4718596
  163.3 3.3 %copy-start.8 = (bf16[1024,4096]{1,0:T(8,128)(2,1)}, bf16[1024,4096]{1,0:T(8,128)(2,1)S(1)}, u32[]{:S(2)}) copy-start(bf16[1024,4096]{1,0:T(8,128)(2,1)S(1)} %collective-permute-done.7) | copy-start | bytes 25165828
  179.1 1.7 copy-start.3
  181.5 11.1 %copy-start.4 = (bf16[1024,768]{0,1:T(8,128)(2,1)S(1)}, bf16[1024,768]{0,1:T(8,128)(2,1)}, u32[]{:S(2)}) copy-start(bf16[1024,768]{0,1:T(8,128)(2,1)} %copy.42) | copy-start | bytes 4718596
  192.7 72.0 %copy-start.1 = (bf16[128,8,768]{2,1,0:T(8,128)(2,1)S(1)}, bf16[128,8,768]{2,1,0:T(8,128)(2,1)}, u32[]{:S(2)}) copy-start(bf16[128,8,768]{2,1,0:T(8,128)(2,1)} %param.5) | copy-start | bytes 4718596
Sparse Core Ops, SparseCore 0:
  9.8 136.2 all-gather.1
  179.2 83.4 reduce-scatter.1

commit v13 on v10

--- a/solution.py
+++ b/solution.py
@@ -43,6 +43,7 @@
 
     dy_z = lax.all_gather(upstream, "z", axis=0, tiled=True)
     recv_h = lax.all_to_all(send_h, ez, split_axis=0, concat_axis=0, tiled=True)
+    recv_h, send_meta = lax.optimization_barrier((recv_h, send_meta))
     recv_meta = lax.all_to_all(send_meta, ez, split_axis=0, concat_axis=0, tiled=True)
     def ring_gather(x, axis):
         n = lax.axis_size(axis)

time: 268 us -> 268 us (level)
  waiting for transfers between devices: 123 us -> 126 us
    ppermute x6, waiting for transfers between devices: 54.9 us -> 72.8 us  [ring_gather(): lax.ppermute(x, axis, perm=[(i, (i - d) % n) for i in range(n)])]
    all_gather x1, waiting for transfers between devices: 19.4 us -> 3.09 us  [body(): dy_z = lax.all_gather(upstream, 'z', axis=0, tiled=True)]
    unnamed x28 -> x30, local copies, waits for them, and re-layouts: 17.8 us -> 16.4 us
  transfers between devices with their start and end apart: 11 -> 11, of which waited for: 5 -> 9; matrix products, arithmetic and copies ran while one was open for 27% -> 27% of each run, Pallas kernels for 0% -> 0%
where the time goes in v13:
time: 268 us; the launch traced here: 267 us
  waiting for transfers between devices  126 us (47%)
  matrix products  49.5 us (18%)
  local copies, waits for them, and re-layouts  33 us (12%)
  starting transfers between devices  27.6 us (10%)
  between operations  14.4 us (5%)
  blocking collectives  11.4 us (4%)
  other arithmetic  5.88 us (2%)
    ppermute x6, waiting for transfers between devices, ring_gather(): lax.ppermute(x, axis, perm=[(i, (i - d) % n) for i in range(n)])  72.8 us
    reduce_scatter x1, waiting for transfers between devices, body(): lax.psum_scatter(partial, ('x', 'y'), scatter_dimension=0, tiled=True)  46.7 us
    dot_general x2, matrix products, part(): lax.dot_general(scaled, h_c, (((0,), (0,)), ((), ())), preferred_element_...  25.6 us
    dot_general x2, matrix products, score(): lax.dot_general(dy_c, w_full, (((1,), (0,)), ((), ())), preferred_element...  22.6 us
    unnamed x30, local copies, waits for them, and re-layouts  16.4 us
    all_to_all x1, blocking collectives, body(): lax.all_to_all(by_source, ez, split_axis=0, concat_axis=0, tiled=True)  11.4 us
    all_to_all x1, starting transfers between devices, body(): recv_h = lax.all_to_all(send_h, ez, split_axis=0, concat_axis=0, tiled=True)  9.44 us
    all_to_all x1, starting transfers between devices, body(): lax.all_to_all(send_meta, ez, split_axis=0, concat_axis=0, tiled=True)  9.02 us
  transfers between devices with their start and end apart: 11, of which 9 were waited for; matrix products, arithmetic and copies ran while one was open for 27% of the time, Pallas kernels for 0%

profile of v13, /device:TPU:1, one launch (start us, length us, event | category | flops | bytes accessed | tf_op | source)
XLA Modules:
  0.0 267.4 jit_solution(7172541264673652860)
XLA Ops:
  7.2 0.7 all-gather.2.cloned.1.call-update
  7.9 3.6 %collective-permute-start = (bf16[256,768]{1,0:T(8,128)(2,1)}, bf16[256,768]{1,0:T(8,128)(2,1)S(1)}, u32[]{:S(2)}, u32[]{:S(2)}) collective-permute-start(bf16[256,768]{1,0:T(8,128)(2,1)} %bitcast.81), channel_id=1, source_target_pairs={{0,48},{16,0},{32,16},{48,32},{1,49},{17,1},{33,17},{49,33},{2,50}... | collective-permute-start | bytes 1179656 | tf_op jit(solution)/shard_map/ppermute | solution.py:50
  11.6 0.3 collective-permute-start.1
  11.9 0.7 collective-permute-start.2
  12.6 0.7 convert_reduce_fusion.1
  13.3 0.1 copy.28
  13.4 0.2 reduce_window_sum.11
  13.7 0.9 convert_reduce_fusion
  14.7 0.1 add.80
  14.8 1.0 constant_dynamic-update-slice_fusion.1
  15.8 12.1 %collective-permute-done = bf16[256,768]{1,0:T(8,128)(2,1)S(1)} collective-permute-done((bf16[256,768]{1,0:T(8,128)(2,1)}, bf16[256,768]{1,0:T(8,128)(2,1)S(1)}, u32[]{:S(2)}, u32[]{:S(2)}) %collective-permute-start) | collective-permute-done | bytes 393248 | tf_op jit(solution)/shard_map/ppermute | solution.py:50
  28.0 4.8 %collective-permute-done.2 = bf16[256,768]{1,0:T(8,128)(2,1)S(1)} collective-permute-done((bf16[256,768]{1,0:T(8,128)(2,1)}, bf16[256,768]{1,0:T(8,128)(2,1)S(1)}, u32[]{:S(2)}, u32[]{:S(2)}) %collective-permute-start.2) | collective-permute-done | bytes 393248 | tf_op jit(solution)/shard_map/ppermute | solution.py:50
  33.0 1.9 bitcast_dynamic-update-slice_fusion.6
  34.9 2.5 collective-permute-start.3
  37.4 4.6 %gather_fusion = bf16[1152,768]{1,0:T(8,128)(2,1)S(1)} fusion(bf16[1024,768]{1,0:T(8,128)(2,1)S(1)} %bitcast.71, s32[2048]{0:T(1024)S(1)} %pad_clamp_fusion), kind=kCustom, calls=%fused_computation | custom fusion | bytes 3543552 | tf_op jit(solution)/shard_map/gather | solution.py:33
  42.0 0.6 collective-permute-start.4
  42.6 1.5 broadcast_select_fusion
  44.0 9.4 %all-to-all-start = ((bf16[16,72,768]{2,1,0:T(8,128)(2,1)}), bf16[16,72,768]{2,1,0:T(8,128)(2,1)S(1)}, u32[]{:S(2)}, u32[]{:S(2)}) async-start(bf16[16,72,768]{2,1,0:T(8,128)(2,1)} %broadcast_select_fusion), calls=%async_computation | async-start | bytes 3538944 | tf_op jit(solution)/shard_map/all_to_all | solution.py:45
  53.5 0.6 collective-permute-start.5
  54.2 17.6 %collective-permute-done.3 = bf16[4,256,768]{2,1,0:T(8,128)(2,1)} collective-permute-done((bf16[4,256,768]{2,1,0:T(8,128)(2,1)}, bf16[4,256,768]{2,1,0:T(8,128)(2,1)}, u32[]{:S(2)}, u32[]{:S(2)}) %collective-permute-start.3) | collective-permute-done | bytes 1572896 | tf_op jit(solution)/shard_map/ppermute | solution.py:50
  71.8 2.7 bitcast_dynamic-update-slice_fusion.4
  74.4 4.6 %collective-permute-done.4 = bf16[4,256,768]{2,1,0:T(8,128)(2,1)S(1)} collective-permute-done((bf16[4,256,768]{2,1,0:T(8,128)(2,1)}, bf16[4,256,768]{2,1,0:T(8,128)(2,1)S(1)}, u32[]{:S(2)}, u32[]{:S(2)}) %collective-permute-start.4) | collective-permute-done | bytes 1572896 | tf_op jit(solution)/shard_map/ppermute | solution.py:50
  79.1 1.2 bitcast_dynamic-update-slice_fusion.2
  80.3 33.6 %collective-permute-done.5 = bf16[4,256,768]{2,1,0:T(8,128)(2,1)} collective-permute-done((bf16[4,256,768]{2,1,0:T(8,128)(2,1)}, bf16[4,256,768]{2,1,0:T(8,128)(2,1)}, u32[]{:S(2)}, u32[]{:S(2)}) %collective-permute-start.5) | collective-permute-done | bytes 1572896 | tf_op jit(solution)/shard_map/ppermute | solution.py:50
  113.9 2.7 %bitcast_dynamic-update-slice_fusion = bf16[8,4,256,768]{3,2,1,0:T(8,128)(2,1)} fusion(bf16[8,4,256,768]{3,2,1,0:T(8,128)(2,1)} %bitcast_dynamic-update-slice_fusion.2, bf16[4,256,768]{2,1,0:T(8,128)(2,1)} %collective-permute-done.5), kind=kLoop, calls=%fused_computation.13 | loop fusion | bytes 3145728
  116.6 2.7 bitcast_dynamic-update-slice_fusion.7
  119.3 2.7 %bitcast_dynamic-update-slice_fusion.5 = bf16[8,4,256,768]{3,2,1,0:T(8,128)(2,1)} fusion(bf16[8,4,256,768]{3,2,1,0:T(8,128)(2,1)} %bitcast_dynamic-update-slice_fusion.7, bf16[4,256,768]{2,1,0:T(8,128)(2,1)} %collective-permute-done.3), kind=kLoop, calls=%fused_computation.18 | loop fusion | bytes 3145728
  122.0 1.3 bitcast_dynamic-update-slice_fusion.3
  123.3 2.7 bitcast_dynamic-update-slice_fusion.1
  126.0 0.6 copy.33
  126.6 9.0 %all-to-all-start.1 = ((f32[16,2,128]{2,1,0:T(2,128)}), f32[16,2,128]{2,1,0:T(2,128)S(1)}, u32[]{:S(2)}, u32[]{:S(2)}) async-start(f32[16,2,128]{2,1,0:T(2,128)} %copy.33), calls=%async_computation.1 | async-start | bytes 32768 | tf_op jit(solution)/shard_map/all_to_all | solution.py:47
  135.6 6.0 %constant_dynamic-slice_fusion.2 = bf16[4,4,256,768]{3,2,1,0:T(8,128)(2,1)} fusion(bf16[8,4,256,768]{3,2,1,0:T(8,128)(2,1)} %bitcast_dynamic-update-slice_fusion.1, s32[]{:T(128)S(6)} %select_n.102), kind=kLoop, calls=%fused_computation.71 | loop fusion | bytes 12582916 | tf_op jit(solution)/shard_map/jit(_roll_dynamic)/dynamic_slice | solution.py:51
  141.6 1.3 all-to-all-done.1
  143.0 3.1 %all-gather.2.cloned.1.call-done = bf16[1024,4096]{1,0:T(8,128)(2,1)} async-done(((bf16[128,4096]{1,0:T(8,128)(2,1)}), bf16[1024,4096]{1,0:T(8,128)(2,1)}) %all-gather.2.cloned.1.call-update) | async-done | bytes 8388624 | tf_op jit(solution)/shard_map/all_gather | solution.py:44
  146.1 0.7 collective-permute-start.6
  146.8 0.6 convolution_convert_fusion
  147.4 0.6 convolution_convert_fusion.1
  148.1 10.7 %fusion = f32[4096,768]{1,0:T(8,128)S(1)} fusion(bf16[1024,768]{1,0:T(8,128)(2,1)S(1)} %bitcast.79, bf16[1024,4096]{1,0:T(8,128)(2,1)} %all-gather.2.cloned.1.call-done, f32[1024]{0:T(1024)S(1)} %get-tuple-element.30), kind=kOutput, calls=%fused_computation.4 | convolution fusion | flops 6455033856 | bytes 22548480 | tf_op jit(solution)/shard_map/dot_general | solution.py:83
  158.8 1.1 collective-permute-done.6
  159.9 14.9 %add_convert_fusion = bf16[4096,768]{1,0:T(8,128)(2,1)} fusion(f32[4096,768]{1,0:T(8,128)S(1)} %fusion, bf16[1024,768]{1,0:T(8,128)(2,1)S(1)} %bitcast.77, bf16[1024,4096]{1,0:T(8,128)(2,1)} %collective-permute-done.6, f32[1024]{0:T(1024)S(1)} %get-tuple-element.28), kind=kOutput, calls=%fused_computation.3 | convolution fusion | flops 6461325312 | bytes 28839936 | tf_op jit(solution)/shard_map/dot_general | solution.py:83
  174.8 1.6 copy.36
  176.4 0.7 copy.35
  177.2 11.1 %multiply_reduce_fusion.1 = f32[1024]{0:T(1024)S(1)} fusion(bf16[1024,768]{0,1:T(8,128)(2,1)S(1)} %copy.35, bf16[1024,4096]{1,0:T(8,128)(2,1)} %all-gather.2.cloned.1.call-done, bf16[4096,768]{1,0:T(8,128)(2,1)} %bitcast.75), kind=kOutput, calls=%fused_computation.9 | convolution fusion | flops 6444809216 | bytes 16257024 | tf_op jit(solution)/shard_map/dot_general | solution.py:86
  188.4 11.5 %multiply_reduce_fusion = f32[1024]{0:T(1024)S(1)} fusion(bf16[1024,768]{0,1:T(8,128)(2,1)S(1)} %copy-done.4, bf16[1024,4096]{1,0:T(8,128)(2,1)} %collective-permute-done.6, bf16[4096,768]{1,0:T(8,128)(2,1)} %bitcast.76), kind=kOutput, calls=%fused_computation.8 | convolution fusion | flops 6444809216 | bytes 16257024 | tf_op jit(solution)/shard_map/dot_general | solution.py:86
  199.9 11.4 %all_to_all.22 = f32[16,1,128]{2,1,0:T(1,128)S(1)} all-to-all(f32[16,1,128]{2,1,0:T(1,128)S(1)} %bitcast.85), channel_id=1, replica_groups=mesh['x'=4,'y'=4,'z'=8,'core'=2] {'z','core'}, dimensions={0} | all-to-all | bytes 16384 | tf_op jit(solution)/shard_map/all_to_all | solution.py:97
  211.3 0.6 select_reduce_fusion.2
  211.9 46.7 %reduce-scatter.2.cloned.1.call-done = bf16[256,768]{1,0:T(8,128)(2,1)} async-done(((bf16[4096,768]{1,0:T(8,128)(2,1)}), bf16[256,768]{1,0:T(8,128)(2,1)}) %reduce-scatter.2.cloned.1.call-update) | async-done | bytes 393232 | tf_op jit(solution)/shard_map/reduce_scatter | solution.py:90
  258.6 1.9 bitcast_convert_fusion
  (46 shorter events, 0.7 us)
Async XLA Ops:
  7.2 30.2 %copy-start = (bf16[128,8,768]{2,1,0:T(8,128)(2,1)S(1)}, bf16[128,8,768]{2,1,0:T(8,128)(2,1)}, u32[]{:S(2)}) copy-start(bf16[128,8,768]{2,1,0:T(8,128)(2,1)} %param.5) | copy-start | bytes 4718596
  7.2 25.7 %copy-start.5 = (bf16[1,256,768]{2,1,0:T(8,128)(2,1)S(1)}, bf16[1,256,768]{2,1,0:T(8,128)(2,1)}, u32[]{:S(2)}) copy-start(bf16[1,256,768]{2,1,0:T(8,128)(2,1)} %param.9) | copy-start | bytes 1179652
  7.2 138.9 %all-gather.2.cloned.1.call-start = ((), (), s32[]{:S(2)}) async-start(), calls=%async_computation.4 | async-start | bytes 9437184 | tf_op jit(solution)/shard_map/all_gather | solution.py:44
  7.9 20.0 %collective-permute-start = (bf16[256,768]{1,0:T(8,128)(2,1)}, bf16[256,768]{1,0:T(8,128)(2,1)S(1)}, u32[]{:S(2)}, u32[]{:S(2)}) collective-permute-start(bf16[256,768]{1,0:T(8,128)(2,1)} %bitcast.81), channel_id=1, source_target_pairs={{0,48},{16,0},{32,16},{48,32},{1,49},{17,1},{33,17},{49,33},{2,50}... | collective-permute-start | bytes 1179656 | tf_op jit(solution)/shard_map/ppermute | solution.py:50
  11.6 16.4 %collective-permute-start.1 = (bf16[256,768]{1,0:T(8,128)(2,1)}, bf16[256,768]{1,0:T(8,128)(2,1)S(1)}, u32[]{:S(2)}, u32[]{:S(2)}) collective-permute-start(bf16[256,768]{1,0:T(8,128)(2,1)} %bitcast.82), channel_id=1, source_target_pairs={{0,32},{16,48},{32,0},{48,16},{1,33},{17,49},{33,1},{49,17},{2,34}... | collective-permute-start | bytes 1179656 | tf_op jit(solution)/shard_map/ppermute | solution.py:50
  11.9 20.9 %collective-permute-start.2 = (bf16[256,768]{1,0:T(8,128)(2,1)}, bf16[256,768]{1,0:T(8,128)(2,1)S(1)}, u32[]{:S(2)}, u32[]{:S(2)}) collective-permute-start(bf16[256,768]{1,0:T(8,128)(2,1)} %bitcast.83), channel_id=1, source_target_pairs={{0,16},{16,32},{32,48},{48,0},{1,17},{17,33},{33,49},{49,1},{2,18}... | collective-permute-start | bytes 1179656 | tf_op jit(solution)/shard_map/ppermute | solution.py:50
  34.9 36.9 %collective-permute-start.3 = (bf16[4,256,768]{2,1,0:T(8,128)(2,1)}, bf16[4,256,768]{2,1,0:T(8,128)(2,1)}, u32[]{:S(2)}, u32[]{:S(2)}) collective-permute-start(bf16[4,256,768]{2,1,0:T(8,128)(2,1)} %get-tuple-element.22), channel_id=1, source_target_pairs={{0,192},{64,0},{128,64},{192,128},{1,193},{65,1},{129,65},{193,129... | collective-permute-start | bytes 4718600 | tf_op jit(solution)/shard_map/ppermute | solution.py:50
  42.0 37.1 %collective-permute-start.4 = (bf16[4,256,768]{2,1,0:T(8,128)(2,1)}, bf16[4,256,768]{2,1,0:T(8,128)(2,1)S(1)}, u32[]{:S(2)}, u32[]{:S(2)}) collective-permute-start(bf16[4,256,768]{2,1,0:T(8,128)(2,1)} %get-tuple-element.22), channel_id=1, source_target_pairs={{0,128},{64,192},{128,0},{192,64},{1,129},{65,193},{129,1},{193,65... | collective-permute-start | bytes 4718600 | tf_op jit(solution)/shard_map/ppermute | solution.py:50
  42.6 11.6 %copy-start.7 = (bf16[128,8]{0,1:T(8,128)(2,1)S(1)}, bf16[128,8]{0,1:T(8,128)(2,1)}, u32[]{:S(2)}) copy-start(bf16[128,8]{0,1:T(8,128)(2,1)} %param.7) | copy-start | bytes 6148
  42.6 11.6 %copy-start.6 = (s32[128,8]{0,1:T(8,128)S(1)}, s32[128,8]{0,1:T(8,128)}, u32[]{:S(2)}) copy-start(s32[128,8]{0,1:T(8,128)} %param.8) | copy-start | bytes 12292
  44.0 81.9 %all-to-all-start = ((bf16[16,72,768]{2,1,0:T(8,128)(2,1)}), bf16[16,72,768]{2,1,0:T(8,128)(2,1)S(1)}, u32[]{:S(2)}, u32[]{:S(2)}) async-start(bf16[16,72,768]{2,1,0:T(8,128)(2,1)} %broadcast_select_fusion), calls=%async_computation | async-start | bytes 3538944 | tf_op jit(solution)/shard_map/all_to_all | solution.py:45
  53.5 60.5 %collective-permute-start.5 = (bf16[4,256,768]{2,1,0:T(8,128)(2,1)}, bf16[4,256,768]{2,1,0:T(8,128)(2,1)}, u32[]{:S(2)}, u32[]{:S(2)}) collective-permute-start(bf16[4,256,768]{2,1,0:T(8,128)(2,1)} %get-tuple-element.22), channel_id=1, source_target_pairs={{0,64},{64,128},{128,192},{192,0},{1,65},{65,129},{129,193},{193,1... | collective-permute-start | bytes 4718600 | tf_op jit(solution)/shard_map/ppermute | solution.py:50
  126.6 16.4 %all-to-all-start.1 = ((f32[16,2,128]{2,1,0:T(2,128)}), f32[16,2,128]{2,1,0:T(2,128)S(1)}, u32[]{:S(2)}, u32[]{:S(2)}) async-start(f32[16,2,128]{2,1,0:T(2,128)} %copy.33), calls=%async_computation.1 | async-start | bytes 32768 | tf_op jit(solution)/shard_map/all_to_all | solution.py:47
  135.6 123.0 %reduce-scatter.2.cloned.1.call-start = ((), (), s32[]{:S(2)}) async-start(), calls=%async_computation.5 | async-start | bytes 6684672 | tf_op jit(solution)/shard_map/reduce_scatter | solution.py:90
  146.1 13.8 %collective-permute-start.6 = (bf16[1024,4096]{1,0:T(8,128)(2,1)}, bf16[1024,4096]{1,0:T(8,128)(2,1)}, u32[]{:S(2)}, u32[]{:S(2)}) collective-permute-start(bf16[1024,4096]{1,0:T(8,128)(2,1)} %all-gather.2.cloned.1.call-done), channel_id=1, source_target_pairs={{0,1},{1,0},{2,3},{3,2},{4,5},{5,4},{6,7},{7,6},{8,9},{9,8},{10,11... | collective-permute-start | bytes 25165832 | tf_op jit(solution)/shard_map/ppermute | solution.py:56
  148.0 10.8 %copy-start.2 = (bf16[8,128,768]{2,1,0:T(8,128)(2,1)}, bf16[8,128,768]{2,1,0:T(8,128)(2,1)S(1)}, u32[]{:S(2)}) copy-start(bf16[8,128,768]{2,1,0:T(8,128)(2,1)S(1)} %convolution_convert_fusion.1) | copy-start | bytes 4718596
  174.8 1.7 copy-start.3
  177.2 11.1 %copy-start.4 = (bf16[1024,768]{0,1:T(8,128)(2,1)S(1)}, bf16[1024,768]{0,1:T(8,128)(2,1)}, u32[]{:S(2)}) copy-start(bf16[1024,768]{0,1:T(8,128)(2,1)} %copy.36) | copy-start | bytes 4718596
  188.3 72.2 %copy-start.1 = (bf16[128,8,768]{2,1,0:T(8,128)(2,1)S(1)}, bf16[128,8,768]{2,1,0:T(8,128)(2,1)}, u32[]{:S(2)}) copy-start(bf16[128,8,768]{2,1,0:T(8,128)(2,1)} %param.5) | copy-start | bytes 4718596
Sparse Core Ops, SparseCore 0:
  9.8 136.2 all-gather.1
  174.9 83.6 reduce-scatter.1
